TPU v7x, 256 devices: a whole 4x4x8 slice. The times are simulated.
256 devices in a mesh: gx: 16 (over y_lo, z), gy: 16 (over y_hi, x, core).
Axes of the slice: x: 4, y: 4 (y_hi: 2, y_lo: 2; y = y_hi * 2 + y_lo), z: 8, core: 2. Of those that a mesh axis runs over, the one named last changes fastest.
Arguments:
- initial_warmth_field: float32 [16, 2048, 2048], P(None, 'gx', 'gy'), may hold values from -8 to 8
- horizontal_motion_pair: float32 [2, 16, 2048, 2048], P(None, None, 'gx', 'gy'), may hold values from -4 to 4
- z_directed_motion: float32 [16, 2048, 2048], P(None, 'gx', 'gy'), may hold values from -3 to 3
- earlier_rate_change: float32 [16, 2048, 2048], P(None, 'gx', 'gy'), may hold values from -6 to 6
- layer_depth_spacing: float32 [16], replicated, may hold values from 0.5 to 2
- backward_spread_ratio: float32 [16], replicated, may hold values from 4 to 100000
- wall_warmth_bounds: float32 [2, 2048, 2048], P(None, 'gx', 'gy'), may hold values from -4 to 4
Outputs:
- resulting_warmth_field: float32 [16, 2048, 2048], P(None, 'gx', 'gy')
- current_rate_change: float32 [16, 2048, 2048], P(None, 'gx', 'gy')
All inputs are finite; a program needn't handle non-finite values.
Results may differ from a plain program's by a relative error of at most 0.000071.
Values sent between devices are 32-bit elements; how exact they have to be, the bound alone decides.
No kernel may reach another device: no remote copies, remote signals or barrier semaphores. Data moves between devices by JAX's collectives and lax.ppermute only.
A program may use at most 64 MiB of HBM per device.

v0:
```python
import jax
import jax.numpy as jnp
from jax import lax
from jax.sharding import PartitionSpec as P

COURANT = 0.5
DIFF_Y = 0.2
DIFF_Z = 0.25
NEW_TERM_COEF = 0.75
OLD_TERM_COEF = -5.0 / 12.0


def with_halo(cells, sides, width):
    for axis, dim in sides:
        count = lax.axis_size(axis)
        head = lax.slice_in_dim(cells, 0, width, axis=dim)
        tail = lax.slice_in_dim(cells, cells.shape[dim] - width, cells.shape[dim], axis=dim)
        cells = jnp.concatenate(
            [
                lax.ppermute(tail, axis, [(i, (i + 1) % count) for i in range(count)]),
                cells,
                lax.ppermute(head, axis, [((i + 1) % count, i) for i in range(count)]),
            ],
            axis=dim,
        )
    return cells


def depthwise_rate_change(
    initial_warmth_field, z_directed_motion, layer_depth_spacing, wall_warmth_bounds
):
    inner_face_transport = (
        (z_directed_motion[:-1] + z_directed_motion[1:])
        * (initial_warmth_field[:-1] + initial_warmth_field[1:])
        * 0.25
    )
    empty_layer_sheet = jnp.zeros_like(initial_warmth_field[:1])
    flux_up = jnp.concatenate([empty_layer_sheet, inner_face_transport, empty_layer_sheet], 0)
    spacing = layer_depth_spacing[:, None, None]
    carry_through_depth = (flux_up[1:] - flux_up[:-1]) / spacing
    warmth_with_ghosts = jnp.concatenate(
        [wall_warmth_bounds[:1], initial_warmth_field, wall_warmth_bounds[1:]], 0
    )
    midway_average = jnp.concatenate(
        [
            layer_depth_spacing[:1],
            0.5 * (layer_depth_spacing[:-1] + layer_depth_spacing[1:]),
            layer_depth_spacing[-1:],
        ],
        0,
    )
    gradient_at_faces = (warmth_with_ghosts[1:] - warmth_with_ghosts[:-1]) / midway_average[
        :, None, None
    ]
    thermal_spreading_step = (gradient_at_faces[1:] - gradient_at_faces[:-1]) / spacing
    return (carry_through_depth, thermal_spreading_step)


def reduce_cyclic(values, number):
    margin = jnp.ones_like(number)
    coupling = -number
    saved_levels = []
    current = values
    while current.shape[1] > 1:
        diagonal = margin - 2.0 * coupling
        even_part = current[:, 0::2]
        odd_part = current[:, 1::2]
        saved_levels.append((odd_part, diagonal, coupling))
        current = even_part - coupling / diagonal * (odd_part + jnp.roll(odd_part, 1, axis=1))
        margin = margin * (margin - 4.0 * coupling) / diagonal
        coupling = -(coupling * coupling) / diagonal
    result = current / margin
    for odd_saved, diagonal_saved, coupling_saved in reversed(saved_levels):
        odd_value = (
            odd_saved - coupling_saved * (result + jnp.roll(result, -1, axis=1))
        ) / diagonal_saved
        result = jnp.stack([result, odd_value], axis=2).reshape(
            result.shape[0], 2 * result.shape[1], result.shape[2]
        )
    return result


def on_device(
    initial_warmth_field,
    horizontal_motion_pair,
    z_directed_motion,
    earlier_rate_change,
    layer_depth_spacing,
    backward_spread_ratio,
    wall_warmth_bounds,
):
    warmth_with_margin = with_halo(initial_warmth_field, (("gx", 1), ("gy", 2)), 1)
    flow_pad = with_halo(horizontal_motion_pair, (("gx", 2), ("gy", 3)), 1)
    east_pad = flow_pad[0]
    north_pad = flow_pad[1]
    x_directed_transport = (
        (east_pad[:, :-1, 1:-1] + east_pad[:, 1:, 1:-1])
        * (warmth_with_margin[:, :-1, 1:-1] + warmth_with_margin[:, 1:, 1:-1])
        * 0.25
    )
    y_directed_transport = (
        (north_pad[:, 1:-1, :-1] + north_pad[:, 1:-1, 1:])
        * (warmth_with_margin[:, 1:-1, :-1] + warmth_with_margin[:, 1:-1, 1:])
        * 0.25
    )
    advect_xy = (
        x_directed_transport[:, 1:]
        - x_directed_transport[:, :-1]
        + (y_directed_transport[:, :, 1:] - y_directed_transport[:, :, :-1])
    )
    carry_through_depth, thermal_spreading_step = depthwise_rate_change(
        initial_warmth_field, z_directed_motion, layer_depth_spacing, wall_warmth_bounds
    )
    stacked_layer_count = (
        warmth_with_margin[:, 1:-1, 2:]
        - 2.0 * initial_warmth_field
        + warmth_with_margin[:, 1:-1, :-2]
    )
    current_rate_change = (
        -COURANT * (advect_xy + carry_through_depth)
        + DIFF_Y * stacked_layer_count
        + DIFF_Z * thermal_spreading_step
    )
    linear_system_source = (
        initial_warmth_field
        + NEW_TERM_COEF * current_rate_change
        + OLD_TERM_COEF * earlier_rate_change
    )
    levels_dev = linear_system_source.shape[0] // lax.axis_size("gx")
    first_level = lax.axis_index("gx") * levels_dev
    number = lax.dynamic_slice_in_dim(backward_spread_ratio, first_level, levels_dev)[:, None, None]
    solved_line_values = reduce_cyclic(
        lax.all_to_all(linear_system_source, "gx", split_axis=0, concat_axis=1, tiled=True), number
    )
    resulting_warmth_field = lax.all_to_all(
        solved_line_values, "gx", split_axis=1, concat_axis=0, tiled=True
    )
    return (resulting_warmth_field, current_rate_change)


def solution(mesh):
    in_specs = (
        P(None, "gx", "gy"),
        P(None, None, "gx", "gy"),
        P(None, "gx", "gy"),
        P(None, "gx", "gy"),
        P(),
        P(),
        P(None, "gx", "gy"),
    )
    out_specs = (P(None, "gx", "gy"), P(None, "gx", "gy"))
    return jax.shard_map(
        on_device, mesh=mesh, in_specs=in_specs, out_specs=out_specs, check_vma=False
    )
```

profile of v0, /device:TPU:7, one launch (start us, length us, event | category | flops | bytes accessed | tf_op | source)
XLA Modules:
  0.0 126.9 jit_solution(10844930283711397860)
XLA Ops:
  0.6 1.0 fusion.80
  1.6 6.7 %collective-permute-start.5 = (f32[16,1,128]{2,0,1:T(8,128)S(1)}, f32[16,1,128]{2,0,1:T(8,128)S(1)}, u32[]{:S(2)}, u32[]{:S(2)}) collective-permute-start(f32[16,1,128]{2,0,1:T(8,128)S(1)} %bitcast.155), channel_id=1, source_target_pairs={{16,0},{32,16},{48,32},{64,48},{80,64},{96,80},{112,96},{128,112},... | collective-permute-start | bytes 24584 | tf_op jit(solution)/shard_map/ppermute | solution.py:22
  8.3 1.0 fusion.78
  9.3 3.6 %collective-permute-start.1 = (f32[2,16,1,128]{3,1,2,0:T(8,128)S(1)}, f32[2,16,1,128]{3,1,2,0:T(8,128)S(1)}, u32[]{:S(2)}, u32[]{:S(2)}) collective-permute-start(f32[2,16,1,128]{3,1,2,0:T(8,128)S(1)} %bitcast.153), channel_id=1, source_target_pairs={{16,0},{32,16},{48,32},{64,48},{80,64},{96,80},{112,96},{128,112},... | collective-permute-start | bytes 49160 | tf_op jit(solution)/shard_map/ppermute | solution.py:22
  13.0 0.8 add_multiply_fusion
  13.8 1.4 %fusion.84 = (f32[1]{0:T(128)}, f32[1]{0:T(128)}) fusion(f32[16]{0:T(128)} %param.11), kind=kLoop, calls=%fused_computation.141 | loop fusion | bytes 16 | tf_op jit(solution)/shard_map/slice | solution.py:46
  15.1 1.7 %copy.92 = f32[16,128,128]{1,0,2:T(8,128)S(1)} copy(f32[16,128,128]{2,1,0:T(8,128)} %param.7) | data formatting | bytes 2097152 | tf_op args[0]
  17.1 1.2 fusion.79
  18.3 0.5 copy.122
  18.8 1.7 %copy.121 = f32[15,128,128]{1,0,2:T(8,128)S(1)} copy(f32[15,128,128]{2,1,0:T(8,128)} %get-tuple-element.21) | data formatting | bytes 1966080
  20.5 1.4 %pad_maximum_fusion.19 = f32[17]{0:T(128)S(1)} fusion(f32[1]{0:T(128)} %get-tuple-element.33, f32[15]{0:T(128)S(1)} %add_multiply_fusion, f32[1]{0:T(128)} %get-tuple-element.32), kind=kLoop, calls=%fused_computation.129 | loop fusion | flops 34 | bytes 136 | tf_op jit(solution)/shard_map/concatenate | solution.py:44
  21.9 1.2 fusion.11
  23.1 1.4 %fusion.2 = f32[17,128,128]{1,0,2:T(8,128)} fusion(f32[1,128,128]{1,0,2:T(1,128)S(1)} %copy.89, f32[16,128,128]{1,0,2:T(8,128)S(1)} %copy.92, f32[1,128,128]{1,0,2:T(1,128)S(1)} %copy.90, f32[17]{0:T(128)S(1)} %pad_maximum_fusion.19), kind=kLoop, calls=%fused_computation.10 | loop fusion | flops 1114112 | bytes 2293828 | tf_op jit(solution)/shard_map/div | solution.py:52
  24.6 0.7 copy-done.8
  25.3 2.0 %copy.72 = f32[2,16,128,128]{2,1,3,0:T(8,128)} copy(f32[2,16,128,128]{3,2,1,0:T(8,128)S(1)} %copy-done.8) | data formatting | bytes 4194304 | tf_op args[1]
  27.3 2.6 %copy.93 = f32[16,128,128]{1,0,2:T(8,128)} copy(f32[16,128,128]{2,1,0:T(8,128)} %param.10) | data formatting | bytes 2097152 | tf_op args[3]
  29.9 0.5 copy.75
  30.4 0.5 copy.79
  31.0 1.6 %collective-permute-start.7 = (f32[16,130,1]{1,0,2:T(8,128)S(1)}, f32[16,130,1]{1,0,2:T(8,128)S(1)}, u32[]{:S(2)}, u32[]{:S(2)}) collective-permute-start(f32[16,130,1]{1,0,2:T(8,128)S(1)} %get-tuple-element.16), channel_id=1, source_target_pairs={{1,0},{2,1},{3,2},{4,3},{5,4},{6,5},{7,6},{8,7},{9,8},{10,9},{11,1... | collective-permute-start | bytes 24968 | tf_op jit(solution)/shard_map/ppermute | solution.py:22
  32.6 3.8 %collective-permute-start.6 = (f32[16,130,1]{1,0,2:T(8,128)S(1)}, f32[16,130,1]{1,0,2:T(8,128)S(1)}, u32[]{:S(2)}, u32[]{:S(2)}) collective-permute-start(f32[16,130,1]{1,0,2:T(8,128)S(1)} %get-tuple-element.17), channel_id=1, source_target_pairs={{0,1},{1,2},{2,3},{3,4},{4,5},{5,6},{6,7},{7,8},{8,9},{9,10},{10,1... | collective-permute-start | bytes 24968 | tf_op jit(solution)/shard_map/ppermute | solution.py:20
  36.5 2.2 %copy.71 = f32[2,16,1,128]{2,1,3,0:T(8,128)} copy(f32[2,16,1,128]{3,1,2,0:T(8,128)S(1)} %collective-permute-done) | data formatting | bytes 32768 | tf_op jit(solution)/shard_map/ppermute | solution.py:20
  38.6 2.1 %copy.73 = f32[2,16,1,128]{2,1,3,0:T(8,128)} copy(f32[2,16,1,128]{3,1,2,0:T(8,128)S(1)} %collective-permute-done.1) | data formatting | bytes 32768 | tf_op jit(solution)/shard_map/ppermute | solution.py:22
  40.7 0.9 pad_maximum_fusion.9
  41.8 0.5 collective-permute-start.3
  42.2 1.7 %maximum_maximum_fusion = (f32[16,130,129]{1,0,2:T(8,128)S(1)}, f32[16,130,129]{1,0,2:T(8,128)S(1)}) fusion(f32[16,1,128]{1,0,2:T(8,128)S(1)} %copy.79, f32[16,128,128]{1,0,2:T(8,128)S(1)} %copy.92, f32[16,1,128]{1,0,2:T(8,128)S(1)} %copy.75, f32[16,130,1]{1,0,2:T(8,128)S(1)} %collective-permute-done.6, f32[16,130,1]{1,0,2:T(8,128)S(1)} %collective-permute-done.7), kind=kLoop, calls=%fused_computation.3 | loop fusion | flops 1609920 | bytes 3228160 | tf_op jit(solution)/shard_map/concatenate | solution.py:18
  43.9 5.0 %collective-permute-done.3 = f32[2,16,130,1]{2,1,3,0:T(8,128)S(1)} collective-permute-done((f32[2,16,130,1]{2,1,3,0:T(8,128)S(1)}, f32[2,16,130,1]{2,1,3,0:T(8,128)S(1)}, u32[]{:S(2)}, u32[]{:S(2)}) %collective-permute-start.3) | collective-permute-done | bytes 16672 | tf_op jit(solution)/shard_map/ppermute | solution.py:22
  49.0 1.7 %pad_maximum_fusion = f32[2,16,130,130]{2,1,3,0:T(8,128)S(1)} fusion(f32[2,16,130,1]{2,1,3,0:T(8,128)S(1)} %collective-permute-done.3, f32[2,16,1,128]{2,1,3,0:T(8,128)S(1)} %copy-done.2, f32[2,16,128,128]{2,1,3,0:T(8,128)S(1)} %copy-done, f32[2,16,1,128]{2,1,3,0:T(8,128)S(1)} %copy-done.1, f32[2,16,130,1]{2,1,3,0:T(8,128)S(1)} %collective-permute-done.2), kind=kLoop, calls=%fused_computation | loop fusion | flops 2163200 | bytes 4326400 | tf_op jit(solution)/shard_map/concatenate | solution.py:18
  50.7 0.5 slice_bitcast_fusion.1
  51.1 1.3 %fusion.1 = f32[16,129,128]{1,0,2:T(8,128)S(1)} fusion(f32[16,130,130]{1,0,2:T(8,128)S(1)} %get-tuple-element.12, f32[16,128,128]{1,0,2:T(8,128)S(1)} %copy.92, f32[16,1,128]{1,0,2:T(8,128)S(1)} %copy.75, f32[16,1,128]{1,0,2:T(8,128)S(1)} %copy.79), kind=kLoop, calls=%fused_computation.7 | loop fusion | flops 1585152 | bytes 4235264 | tf_op jit(solution)/shard_map/mul | solution.py:97
  52.4 1.2 fusion.4
  53.8 0.3 copy-done.4
  54.1 0.3 copy-done.6
  54.4 2.8 %multiply_add_fusion = (f32[16,128,128]{1,0,2:T(8,128)S(1)}, f32[16,128,128]{1,0,2:T(8,128)}) fusion(f32[16,128,128]{1,0,2:T(8,128)S(1)} %copy-done.6, f32[16,128,128]{1,0,2:T(8,128)S(1)} %copy.92, f32[17,128,128]{1,0,2:T(8,128)S(1)} %copy-done.3, f32[16,1,128]{1,0,2:T(8,128)S(1)} %copy.79, f32[16,1,128]{1,0,2:T(8,128)S(1)} %copy.75, ...), kind=kLoop, calls=%fused_computation.32 | loop fusion | flops 6815744 | bytes 11501888 | tf_op jit(solution)/shard_map/add | solution.py:125
  57.2 1.3 %copy.94 = f32[16,128,128]{1,2,0:T(8,128)} copy(f32[16,128,128]{1,0,2:T(8,128)S(1)} %get-tuple-element.8) | data formatting | bytes 2097152 | tf_op jit(solution)/shard_map/add | solution.py:125
  58.5 5.0 %all-to-all-start = ((f32[16,128,128]{1,2,0:T(8,128)}), f32[16,128,128]{1,2,0:T(8,128)S(1)}, u32[]{:S(2)}, u32[]{:S(2)}) async-start(f32[16,128,128]{1,2,0:T(8,128)} %copy.94), calls=%async_computation | async-start | bytes 2097152 | tf_op jit(solution)/shard_map/all_to_all | solution.py:133
  63.5 0.6 dynamic_slice.3
  67.4 20.2 %all-to-all-done = f32[16,128,128]{1,2,0:T(8,128)S(1)} async-done(((f32[16,128,128]{1,2,0:T(8,128)}), f32[16,128,128]{1,2,0:T(8,128)S(1)}, u32[]{:S(2)}, u32[]{:S(2)}) %all-to-all-start) | async-done | bytes 1048608 | tf_op jit(solution)/shard_map/all_to_all | solution.py:133
  87.6 0.3 copy.95
  88.0 0.7 slice.381
  88.7 0.7 slice.380
  89.5 0.4 slice.385
  89.9 0.4 slice.384
  92.2 0.4 copy.112
  92.9 1.8 %copy.114 = f32[1,1024,2,128]{3,2,1,0:T(2,128)} copy(f32[1,1024,2,128]{3,1,2,0:T(8,128)S(1)} %pad_maximum_fusion.2) | data formatting | bytes 2097152 | tf_op jit(solution)/shard_map/stack | solution.py:77
  94.7 4.2 %all-to-all-start.1 = ((f32[1,2048,128]{2,0,1:T(1,128)}), f32[1,2048,128]{2,0,1:T(1,128)S(1)}, u32[]{:S(2)}, u32[]{:S(2)}) async-start(f32[1,2048,128]{2,0,1:T(1,128)} %bitcast.72), calls=%async_computation.1 | async-start | bytes 2097152 | tf_op jit(solution)/shard_map/all_to_all | solution.py:135
  98.8 1.4 %copy.116 = f32[16,128,128]{2,1,0:T(8,128)} copy(f32[16,128,128]{1,0,2:T(8,128)S(1)} %copy-done.5) | data formatting | bytes 2097152
  100.2 25.7 %all-to-all-done.1 = f32[1,2048,128]{2,0,1:T(1,128)S(1)} async-done(((f32[1,2048,128]{2,0,1:T(1,128)}), f32[1,2048,128]{2,0,1:T(1,128)S(1)}, u32[]{:S(2)}, u32[]{:S(2)}) %all-to-all-start.1) | async-done | bytes 1048608 | tf_op jit(solution)/shard_map/all_to_all | solution.py:135
  125.9 1.0 copy.124
  (120 shorter events, 2.4 us)
Async XLA Ops:
  0.6 16.2 %copy-start.9 = (f32[2,128,128]{2,1,0:T(8,128)S(1)}, f32[2,128,128]{2,1,0:T(8,128)}, u32[]{:S(2)}) copy-start(f32[2,128,128]{2,1,0:T(8,128)} %param.13) | copy-start | bytes 393220
  0.6 16.5 %copy-start.7 = (f32[16,128,128]{2,1,0:T(8,128)S(1)}, f32[16,128,128]{2,1,0:T(8,128)}, u32[]{:S(2)}) copy-start(f32[16,128,128]{2,1,0:T(8,128)} %param.9) | copy-start | bytes 3145732
  1.6 28.8 %collective-permute-start.5 = (f32[16,1,128]{2,0,1:T(8,128)S(1)}, f32[16,1,128]{2,0,1:T(8,128)S(1)}, u32[]{:S(2)}, u32[]{:S(2)}) collective-permute-start(f32[16,1,128]{2,0,1:T(8,128)S(1)} %bitcast.155), channel_id=1, source_target_pairs={{16,0},{32,16},{48,32},{64,48},{80,64},{96,80},{112,96},{128,112},... | collective-permute-start | bytes 24584 | tf_op jit(solution)/shard_map/ppermute | solution.py:22
  8.3 21.6 %collective-permute-start.4 = (f32[16,1,128]{2,0,1:T(8,128)S(1)}, f32[16,1,128]{2,0,1:T(8,128)S(1)}, u32[]{:S(2)}, u32[]{:S(2)}) collective-permute-start(f32[16,1,128]{2,0,1:T(8,128)S(1)} %bitcast.156), channel_id=1, source_target_pairs={{0,16},{16,32},{32,48},{48,64},{64,80},{80,96},{96,112},{112,128},... | collective-permute-start | bytes 24584 | tf_op jit(solution)/shard_map/ppermute | solution.py:20
  9.3 29.3 %collective-permute-start.1 = (f32[2,16,1,128]{3,1,2,0:T(8,128)S(1)}, f32[2,16,1,128]{3,1,2,0:T(8,128)S(1)}, u32[]{:S(2)}, u32[]{:S(2)}) collective-permute-start(f32[2,16,1,128]{3,1,2,0:T(8,128)S(1)} %bitcast.153), channel_id=1, source_target_pairs={{16,0},{32,16},{48,32},{64,48},{80,64},{96,80},{112,96},{128,112},... | collective-permute-start | bytes 49160 | tf_op jit(solution)/shard_map/ppermute | solution.py:22
  12.9 23.5 %collective-permute-start = (f32[2,16,1,128]{3,1,2,0:T(8,128)S(1)}, f32[2,16,1,128]{3,1,2,0:T(8,128)S(1)}, u32[]{:S(2)}, u32[]{:S(2)}) collective-permute-start(f32[2,16,1,128]{3,1,2,0:T(8,128)S(1)} %bitcast.154), channel_id=1, source_target_pairs={{0,16},{16,32},{32,48},{48,64},{64,80},{80,96},{96,112},{112,128},... | collective-permute-start | bytes 49160 | tf_op jit(solution)/shard_map/ppermute | solution.py:20
  23.1 2.2 %copy-start.8 = (f32[2,16,128,128]{3,2,1,0:T(8,128)S(1)}, f32[2,16,128,128]{3,2,1,0:T(8,128)}, u32[]{:S(2)}) copy-start(f32[2,16,128,128]{3,2,1,0:T(8,128)} %param.8) | copy-start | bytes 6291460
  31.0 11.2 %collective-permute-start.7 = (f32[16,130,1]{1,0,2:T(8,128)S(1)}, f32[16,130,1]{1,0,2:T(8,128)S(1)}, u32[]{:S(2)}, u32[]{:S(2)}) collective-permute-start(f32[16,130,1]{1,0,2:T(8,128)S(1)} %get-tuple-element.16), channel_id=1, source_target_pairs={{1,0},{2,1},{3,2},{4,3},{5,4},{6,5},{7,6},{8,7},{9,8},{10,9},{11,1... | collective-permute-start | bytes 24968 | tf_op jit(solution)/shard_map/ppermute | solution.py:22
  32.6 9.6 %collective-permute-start.6 = (f32[16,130,1]{1,0,2:T(8,128)S(1)}, f32[16,130,1]{1,0,2:T(8,128)S(1)}, u32[]{:S(2)}, u32[]{:S(2)}) collective-permute-start(f32[16,130,1]{1,0,2:T(8,128)S(1)} %get-tuple-element.17), channel_id=1, source_target_pairs={{0,1},{1,2},{2,3},{3,4},{4,5},{5,6},{6,7},{7,8},{8,9},{9,10},{10,1... | collective-permute-start | bytes 24968 | tf_op jit(solution)/shard_map/ppermute | solution.py:20
  41.6 2.3 %collective-permute-start.2 = (f32[2,16,130,1]{2,1,3,0:T(8,128)S(1)}, f32[2,16,130,1]{2,1,3,0:T(8,128)S(1)}, u32[]{:S(2)}, u32[]{:S(2)}) collective-permute-start(f32[2,16,130,1]{2,1,3,0:T(8,128)S(1)} %get-tuple-element.10), channel_id=1, source_target_pairs={{0,1},{1,2},{2,3},{3,4},{4,5},{5,6},{6,7},{7,8},{8,9},{9,10},{10,1... | collective-permute-start | bytes 49928 | tf_op jit(solution)/shard_map/ppermute | solution.py:20
  41.7 7.2 %copy-start = (f32[2,16,128,128]{2,1,3,0:T(8,128)S(1)}, f32[2,16,128,128]{2,1,3,0:T(8,128)}, u32[]{:S(2)}) copy-start(f32[2,16,128,128]{2,1,3,0:T(8,128)} %copy.72) | copy-start | bytes 6291460
  41.7 7.2 %copy-start.1 = (f32[2,16,1,128]{2,1,3,0:T(8,128)S(1)}, f32[2,16,1,128]{2,1,3,0:T(8,128)}, u32[]{:S(2)}) copy-start(f32[2,16,1,128]{2,1,3,0:T(8,128)} %copy.71) | copy-start | bytes 49156
  41.7 7.2 %copy-start.2 = (f32[2,16,1,128]{2,1,3,0:T(8,128)S(1)}, f32[2,16,1,128]{2,1,3,0:T(8,128)}, u32[]{:S(2)}) copy-start(f32[2,16,1,128]{2,1,3,0:T(8,128)} %copy.73) | copy-start | bytes 49156
  41.8 7.2 %collective-permute-start.3 = (f32[2,16,130,1]{2,1,3,0:T(8,128)S(1)}, f32[2,16,130,1]{2,1,3,0:T(8,128)S(1)}, u32[]{:S(2)}, u32[]{:S(2)}) collective-permute-start(f32[2,16,130,1]{2,1,3,0:T(8,128)S(1)} %get-tuple-element.11), channel_id=1, source_target_pairs={{1,0},{2,1},{3,2},{4,3},{5,4},{6,5},{7,6},{8,7},{9,8},{10,9},{11,1... | collective-permute-start | bytes 49928 | tf_op jit(solution)/shard_map/ppermute | solution.py:22
  52.4 1.4 %copy-start.3 = (f32[17,128,128]{1,0,2:T(8,128)S(1)}, f32[17,128,128]{1,0,2:T(8,128)}, u32[]{:S(2)}) copy-start(f32[17,128,128]{1,0,2:T(8,128)} %fusion.2) | copy-start | bytes 3342340
  52.4 1.7 %copy-start.4 = (f32[15,128,128]{1,0,2:T(8,128)S(1)}, f32[15,128,128]{1,0,2:T(8,128)}, u32[]{:S(2)}) copy-start(f32[15,128,128]{1,0,2:T(8,128)} %fusion.11) | copy-start | bytes 2949124
  52.4 2.0 %copy-start.6 = (f32[16,128,128]{1,0,2:T(8,128)S(1)}, f32[16,128,128]{1,0,2:T(8,128)}, u32[]{:S(2)}) copy-start(f32[16,128,128]{1,0,2:T(8,128)} %copy.93) | copy-start | bytes 3145732
  52.4 2.0 %copy-start.10 = (f32[16]{0:T(128)S(1)}, f32[16]{0:T(128)}, u32[]{:S(2)}) copy-start(f32[16]{0:T(128)} %param.11) | copy-start | bytes 196
  57.2 6.3 %copy-start.11 = (f32[16]{0:T(128)S(1)}, f32[16]{0:T(128)}, u32[]{:S(2)}) copy-start(f32[16]{0:T(128)} %param.12) | copy-start | bytes 196
  58.5 29.1 %all-to-all-start = ((f32[16,128,128]{1,2,0:T(8,128)}), f32[16,128,128]{1,2,0:T(8,128)S(1)}, u32[]{:S(2)}, u32[]{:S(2)}) async-start(f32[16,128,128]{1,2,0:T(8,128)} %copy.94), calls=%async_computation | async-start | bytes 2097152 | tf_op jit(solution)/shard_map/all_to_all | solution.py:133
  92.9 6.0 %copy-start.5 = (f32[16,128,128]{1,0,2:T(8,128)S(1)}, f32[16,128,128]{1,0,2:T(8,128)}, u32[]{:S(2)}) copy-start(f32[16,128,128]{1,0,2:T(8,128)} %get-tuple-element.9) | copy-start | bytes 3145732
  94.7 31.2 %all-to-all-start.1 = ((f32[1,2048,128]{2,0,1:T(1,128)}), f32[1,2048,128]{2,0,1:T(1,128)S(1)}, u32[]{:S(2)}, u32[]{:S(2)}) async-start(f32[1,2048,128]{2,0,1:T(1,128)} %bitcast.72), calls=%async_computation.1 | async-start | bytes 2097152 | tf_op jit(solution)/shard_map/all_to_all | solution.py:135
where the time goes:
time: 127 us
  waiting for transfers between devices  50.9 us (40%)
  local copies, waits for them, and re-layouts  30.6 us (24%)
  starting transfers between devices  25.4 us (20%)
  other arithmetic  15.2 us (12%)
  between operations  4.74 us (4%)
    all_to_all x1, waiting for transfers between devices, on_device(): lax.all_to_all(solved_line_values, 'gx', split_axis=1, concat_axis=0, til...  25.7 us
    all_to_all x1, waiting for transfers between devices, on_device(): lax.all_to_all(linear_system_source, 'gx', split_axis=0, concat_axis=1, t...  20.2 us
    unnamed x31, local copies, waits for them, and re-layouts  12.4 us
    ppermute x4, starting transfers between devices, with_halo(): lax.ppermute(head, axis, [((i + 1) % count, i) for i in range(count)])  12.4 us
    ppermute x4, waiting for transfers between devices, with_halo(): lax.ppermute(head, axis, [((i + 1) % count, i) for i in range(count)])  5.04 us
    all_to_all x1, starting transfers between devices, on_device(): lax.all_to_all(linear_system_source, 'gx', split_axis=0, concat_axis=1, t...  4.95 us
    all_to_all x1, starting transfers between devices, on_device(): lax.all_to_all(solved_line_values, 'gx', split_axis=1, concat_axis=0, til...  4.16 us
    ppermute x4, starting transfers between devices, with_halo(): lax.ppermute(tail, axis, [(i, (i + 1) % count) for i in range(count)])  3.93 us
  transfers between devices with their start and end apart: 10, of which 3 were waited for; matrix products, arithmetic and copies ran while one was open for 21% of the time, Pallas kernels for 0%

commit v1 on v0

v1 whole, which is shorter than its diff:
```python
import jax
import jax.numpy as jnp
from jax import lax
from jax.sharding import PartitionSpec as P

COURANT = 0.5
DIFF_Y = 0.2
DIFF_Z = 0.25
NEW_TERM_COEF = 0.75
OLD_TERM_COEF = -5.0 / 12.0


def ring_pairs(count, step):
    return [(i, (i + step) % count) for i in range(count)]


def exchange_edges(first, last, axis):
    count = lax.axis_size(axis)
    from_prev = lax.ppermute(last, axis, ring_pairs(count, 1))
    from_next = lax.ppermute(first, axis, ring_pairs(count, -1))
    return from_prev, from_next


def shifted(a, halo, axis, step):
    n = a.shape[axis]
    halo = jnp.expand_dims(halo, axis)
    if step > 0:
        return jnp.concatenate([lax.slice_in_dim(a, 1, n, axis=axis), halo], axis)
    return jnp.concatenate([halo, lax.slice_in_dim(a, 0, n - 1, axis=axis)], axis)


def depthwise_rate_change(
    initial_warmth_field, z_directed_motion, layer_depth_spacing, wall_warmth_bounds
):
    inner_face_transport = (
        (z_directed_motion[:-1] + z_directed_motion[1:])
        * (initial_warmth_field[:-1] + initial_warmth_field[1:])
        * 0.25
    )
    empty_layer_sheet = jnp.zeros_like(initial_warmth_field[:1])
    flux_up = jnp.concatenate([empty_layer_sheet, inner_face_transport, empty_layer_sheet], 0)
    spacing = layer_depth_spacing[:, None, None]
    carry_through_depth = (flux_up[1:] - flux_up[:-1]) / spacing
    warmth_with_ghosts = jnp.concatenate(
        [wall_warmth_bounds[:1], initial_warmth_field, wall_warmth_bounds[1:]], 0
    )
    midway_average = jnp.concatenate(
        [
            layer_depth_spacing[:1],
            0.5 * (layer_depth_spacing[:-1] + layer_depth_spacing[1:]),
            layer_depth_spacing[-1:],
        ],
        0,
    )
    gradient_at_faces = (warmth_with_ghosts[1:] - warmth_with_ghosts[:-1]) / midway_average[
        :, None, None
    ]
    thermal_spreading_step = (gradient_at_faces[1:] - gradient_at_faces[:-1]) / spacing
    return (carry_through_depth, thermal_spreading_step)


def periodic_solve(source, ratio):
    levels, rows, cols = source.shape
    parts = lax.axis_size("gx")
    me = lax.axis_index("gx")
    root = jnp.sqrt(1.0 + 4.0 * ratio)
    mu = (1.0 + root) / ((1.0 + 2.0 * ratio) + root)
    log_lam = jnp.log1p(-mu)[:, None]

    idx = jnp.arange(rows, dtype=jnp.float32)
    to_end = jnp.exp(log_lam * (rows - 1 - idx)[None, :])
    from_start = jnp.exp(log_lam * idx[None, :])
    ends = jnp.stack(
        [
            jnp.sum(to_end[:, :, None] * source, axis=1),
            jnp.sum(from_start[:, :, None] * source, axis=1),
        ]
    )
    gathered = lax.all_gather(ends, "gx", axis=0)

    dist = jnp.abs(idx[:, None] - idx[None, :])
    kernel = jnp.exp(log_lam[:, :, None] * dist[None])
    local = jnp.einsum(
        "kij,kjc->kic", kernel, source, precision=lax.Precision.HIGHEST
    )

    others = jnp.arange(parts)
    whole = -jnp.expm1(log_lam * (parts * rows))
    lag_f = ((me - others - 1) % parts).astype(jnp.float32) * rows
    lag_b = ((others - me - 1) % parts).astype(jnp.float32) * rows
    weight_f = jnp.exp(log_lam * lag_f[None, :]) / whole
    weight_b = jnp.exp(log_lam * lag_b[None, :]) / whole
    carry_f = jnp.sum(weight_f.T[:, :, None] * gathered[:, 0], axis=0)
    carry_b = jnp.sum(weight_b.T[:, :, None] * gathered[:, 1], axis=0)
    into_f = jnp.exp(log_lam * (idx + 1.0)[None, :])
    into_b = jnp.exp(log_lam * (rows - idx)[None, :])
    total = (
        local
        + into_f[:, :, None] * carry_f[:, None, :]
        + into_b[:, :, None] * carry_b[:, None, :]
    )
    return total / root[:, None, None]


def on_device(
    initial_warmth_field,
    horizontal_motion_pair,
    z_directed_motion,
    earlier_rate_change,
    layer_depth_spacing,
    backward_spread_ratio,
    wall_warmth_bounds,
):
    t = initial_warmth_field
    u = horizontal_motion_pair[0]
    v = horizontal_motion_pair[1]
    x_prev, x_next = exchange_edges(
        jnp.stack([t[:, 0, :], u[:, 0, :]]), jnp.stack([t[:, -1, :], u[:, -1, :]]), "gx"
    )
    y_prev, y_next = exchange_edges(
        jnp.stack([t[:, :, 0], v[:, :, 0]]), jnp.stack([t[:, :, -1], v[:, :, -1]]), "gy"
    )
    t_xn = shifted(t, x_next[0], 1, 1)
    t_xp = shifted(t, x_prev[0], 1, -1)
    u_xn = shifted(u, x_next[1], 1, 1)
    u_xp = shifted(u, x_prev[1], 1, -1)
    t_yn = shifted(t, y_next[0], 2, 1)
    t_yp = shifted(t, y_prev[0], 2, -1)
    v_yn = shifted(v, y_next[1], 2, 1)
    v_yp = shifted(v, y_prev[1], 2, -1)

    flux_x_hi = (u + u_xn) * (t + t_xn) * 0.25
    flux_x_lo = (u_xp + u) * (t_xp + t) * 0.25
    flux_y_hi = (v + v_yn) * (t + t_yn) * 0.25
    flux_y_lo = (v_yp + v) * (t_yp + t) * 0.25
    advect_xy = (flux_x_hi - flux_x_lo) + (flux_y_hi - flux_y_lo)
    carry_through_depth, thermal_spreading_step = depthwise_rate_change(
        t, z_directed_motion, layer_depth_spacing, wall_warmth_bounds
    )
    stacked_layer_count = t_yn - 2.0 * t + t_yp
    current_rate_change = (
        -COURANT * (advect_xy + carry_through_depth)
        + DIFF_Y * stacked_layer_count
        + DIFF_Z * thermal_spreading_step
    )
    linear_system_source = (
        t + NEW_TERM_COEF * current_rate_change + OLD_TERM_COEF * earlier_rate_change
    )
    resulting_warmth_field = periodic_solve(linear_system_source, backward_spread_ratio)
    return (resulting_warmth_field, current_rate_change)


def solution(mesh):
    in_specs = (
        P(None, "gx", "gy"),
        P(None, None, "gx", "gy"),
        P(None, "gx", "gy"),
        P(None, "gx", "gy"),
        P(),
        P(),
        P(None, "gx", "gy"),
    )
    out_specs = (P(None, "gx", "gy"), P(None, "gx", "gy"))
    return jax.shard_map(
        on_device, mesh=mesh, in_specs=in_specs, out_specs=out_specs, check_vma=False
    )
```

time: 127 us -> 94.8 us (0.75)
  the two profiles are of different devices: /device:TPU:7 before, /device:TPU:8 now
where the time goes in v1:
time: 94.8 us; the launch traced here: 94.4 us
  blocking collectives  35.3 us (37%)
  local copies, waits for them, and re-layouts  29.5 us (31%)
  other arithmetic  15.8 us (17%)
  starting transfers between devices  10.1 us (11%)
  matrix products  2.76 us (3%)
    all_gather x1, blocking collectives, periodic_solve(): gathered = lax.all_gather(ends, 'gx', axis=0)  35.3 us
    ppermute x2, starting transfers between devices, exchange_edges(): from_next = lax.ppermute(first, axis, ring_pairs(count, -1))  9.81 us
    reduce_sum x1, other arithmetic, periodic_solve(): jnp.sum(to_end[:, :, None] * source, axis=1)  9.2 us
    slice x4, local copies, waits for them, and re-layouts, shifted(): return jnp.concatenate([lax.slice_in_dim(a, 1, n, axis=axis), halo], axis)  6.25 us
    unnamed x26, local copies, waits for them, and re-layouts  6.06 us
    another operation x8, local copies, waits for them, and re-layouts, shifted(): halo = jnp.expand_dims(halo, axis)  5.71 us
    mul x1, other arithmetic, depthwise_rate_change(): (z_directed_motion[:-1] + z_directed_motion[1:]) * (initial_warmth_field[...  3.38 us
    slice x2, local copies, waits for them, and re-layouts, on_device(): v[:, :, 0]  3.28 us
  transfers between devices with their start and end apart: 4, of which 0 were waited for; matrix products, arithmetic and copies ran while one was open for 32% of the time, Pallas kernels for 0%

profile of v1, /device:TPU:8, one launch (start us, length us, event | category | flops | bytes accessed | tf_op | source)
XLA Modules:
  0.0 94.4 jit_solution(784480876953769007)
XLA Ops:
  0.6 1.7 %fusion.40 = (f32[1,16,128,128]{3,2,1,0:T(8,128)S(1)}, f32[1,16,128,128]{3,2,1,0:T(8,128)S(1)}) fusion(f32[2,16,128,128]{3,2,1,0:T(8,128)} %param.8), kind=kLoop, calls=%fused_computation.97 | loop fusion | bytes 4194304 | tf_op jit(solution)/shard_map/slice | solution.py:115
  2.3 0.0 copy-start.1
  2.3 0.0 copy-start.3
  2.3 0.0 copy-start
  2.4 1.2 %copy_bitcast_fusion = (f32[16,128,128]{2,0,1:T(8,128)S(1)}, f32[16,128,128]{2,0,1:T(8,128)S(1)}) fusion(f32[1,16,128,128]{3,2,1,0:T(8,128)S(1)} %get-tuple-element.21, f32[1,16,128,128]{3,2,1,0:T(8,128)S(1)} %get-tuple-element.20), kind=kLoop, calls=%fused_computation.35 | loop fusion | bytes 4194304 | tf_op jit(solution)/shard_map/squeeze | solution.py:116
  3.6 0.0 copy-done.1
  3.6 0.0 copy-done.3
  3.6 0.7 copy-done
  4.3 0.6 copy.188
  5.0 5.8 %collective-permute-start = (f32[2,16,128]{2,1,0:T(8,128)S(1)}, f32[2,16,128]{2,1,0:T(8,128)S(1)}, u32[]{:S(2)}, u32[]{:S(2)}) collective-permute-start(f32[2,16,128]{2,1,0:T(8,128)S(1)} %pad_maximum_fusion.2), channel_id=1, source_target_pairs={{0,240},{16,0},{32,16},{48,32},{64,48},{80,64},{96,80},{112,96},{1... | collective-permute-start | bytes 49160 | tf_op jit(solution)/shard_map/ppermute | solution.py:20
  10.8 0.0 collective-permute-start.1
  10.8 1.7 %fusion.45 = (f32[16,128,1]{2,1,0:T(8,128)}, f32[16,128,1]{2,1,0:T(8,128)}) fusion(f32[16,128,128]{2,1,0:T(8,128)S(1)} %copy-done), kind=kLoop, calls=%fused_computation.102 | loop fusion | bytes 32768 | tf_op jit(solution)/shard_map/slice | solution.py:121
  12.5 0.0 copy-done.5
  12.5 1.6 %fusion.46 = (f32[16,128,1]{2,0,1:T(8,128)}, f32[16,128,1]{2,0,1:T(8,128)}) fusion(f32[16,128,128]{2,0,1:T(8,128)S(1)} %get-tuple-element.61), kind=kLoop, calls=%fused_computation.103 | loop fusion | bytes 32768 | tf_op jit(solution)/shard_map/slice | solution.py:121
  14.1 1.6 %copy.168 = f32[16,128,1]{1,0,2:T(8,128)S(1)} copy(f32[16,128,1]{2,0,1:T(8,128)} %get-tuple-element.36) | data formatting | bytes 16384 | tf_op jit(solution)/shard_map/slice | solution.py:121
  15.8 1.6 %copy.196 = f32[16,128,1]{1,0,2:T(8,128)S(1)} copy(f32[16,128,1]{2,1,0:T(8,128)} %get-tuple-element.34) | data formatting | bytes 16384
  17.3 4.0 %collective-permute-start.2 = (f32[2,16,128]{2,1,0:T(8,128)S(1)}, f32[2,16,128]{2,1,0:T(8,128)S(1)}, u32[]{:S(2)}, u32[]{:S(2)}) collective-permute-start(f32[2,16,128]{2,1,0:T(8,128)S(1)} %pad_maximum_fusion.4), channel_id=1, source_target_pairs={{0,15},{1,0},{2,1},{3,2},{4,3},{5,4},{6,5},{7,6},{8,7},{9,8},{10,9... | collective-permute-start | bytes 49160 | tf_op jit(solution)/shard_map/ppermute | solution.py:20
  21.3 1.6 %copy.174 = f32[16,128,1]{1,0,2:T(8,128)S(1)} copy(f32[16,128,1]{2,0,1:T(8,128)} %get-tuple-element.37) | data formatting | bytes 16384 | tf_op jit(solution)/shard_map/slice | solution.py:121
  23.0 1.6 %copy.197 = f32[16,128,1]{1,0,2:T(8,128)S(1)} copy(f32[16,128,1]{2,1,0:T(8,128)} %get-tuple-element.35) | data formatting | bytes 16384
  24.5 0.2 collective-permute-start.3
  24.8 0.6 fusion.49
  25.4 0.1 add_multiply_fusion
  25.5 1.6 %fusion.43 = (f32[16,128,127]{2,0,1:T(8,128)}, f32[16,128,127]{2,0,1:T(8,128)}) fusion(f32[16,128,128]{2,0,1:T(8,128)S(1)} %get-tuple-element.61), kind=kLoop, calls=%fused_computation.100 | loop fusion | bytes 4161536 | tf_op jit(solution)/shard_map/slice | solution.py:28
  27.1 1.4 %fusion.41 = (f32[16,127,128]{2,0,1:T(8,128)}, f32[16,127,128]{2,0,1:T(8,128)}) fusion(f32[16,128,128]{2,0,1:T(8,128)S(1)} %copy-done.6), kind=kLoop, calls=%fused_computation.98 | loop fusion | bytes 4161536 | tf_op jit(solution)/shard_map/slice | solution.py:28
  28.5 1.6 %fusion.44 = (f32[16,128,127]{2,0,1:T(8,128)}, f32[16,128,127]{2,0,1:T(8,128)}) fusion(f32[16,128,128]{2,0,1:T(8,128)S(1)} %copy.188), kind=kLoop, calls=%fused_computation.101 | loop fusion | bytes 4161536 | tf_op jit(solution)/shard_map/slice | solution.py:28
  30.2 1.5 %fusion.42 = (f32[16,127,128]{2,0,1:T(8,128)}, f32[16,127,128]{2,0,1:T(8,128)}) fusion(f32[16,128,128]{2,0,1:T(8,128)S(1)} %copy.188), kind=kLoop, calls=%fused_computation.99 | loop fusion | bytes 4161536 | tf_op jit(solution)/shard_map/slice | solution.py:28
  31.8 0.3 copy-done.7
  32.1 1.2 %fusion.47 = (f32[15,128,128]{2,1,0:T(8,128)S(1)}, f32[15,128,128]{2,1,0:T(8,128)}) fusion(f32[16,128,128]{2,1,0:T(8,128)S(1)} %copy-done.7), kind=kLoop, calls=%fused_computation.104 | loop fusion | bytes 3932160 | tf_op jit(solution)/shard_map/slice | solution.py:36
  33.3 3.4 %fusion.7 = f32[15,128,128]{2,0,1:T(8,128)} fusion(f32[16,128,128]{2,0,1:T(8,128)S(1)} %copy.188, f32[15,128,128]{2,1,0:T(8,128)} %get-tuple-element.39, f32[15,128,128]{2,1,0:T(8,128)S(1)} %get-tuple-element.38), kind=kLoop, calls=%fused_computation.11 | loop fusion | flops 983040 | bytes 4915200 | tf_op jit(solution)/shard_map/mul | solution.py:36
  36.7 1.3 %pad_maximum_fusion.7 = f32[17]{0:T(128)S(1)} fusion(f32[1]{0:T(128)} %get-tuple-element.58, f32[15]{0:T(128)S(1)} %add_multiply_fusion, f32[1]{0:T(128)} %get-tuple-element.57), kind=kLoop, calls=%fused_computation.88 | loop fusion | flops 34 | bytes 136 | tf_op jit(solution)/shard_map/concatenate | solution.py:47
  38.0 1.5 %fusion = f32[17,128,128]{2,0,1:T(8,128)} fusion(f32[1,128,128]{2,0,1:T(1,128)S(1)} %bitcast.57, f32[16,128,128]{2,0,1:T(8,128)S(1)} %copy.188, f32[1,128,128]{2,0,1:T(1,128)S(1)} %bitcast.56, f32[17]{0:T(128)S(1)} %pad_maximum_fusion.7), kind=kLoop, calls=%fused_computation.1 | loop fusion | flops 1114112 | bytes 2293828 | tf_op jit(solution)/shard_map/div | solution.py:55
  39.5 0.1 multiply_exponential_fusion.3
  39.5 0.1 exponential_divide_fusion
  39.7 0.1 copy.191
  39.8 0.1 copy.192
  39.9 0.0 collective-permute-done
  39.9 0.0 collective-permute-done.2
  39.9 0.0 collective-permute-done.3
  39.9 1.4 %copy.169 = f32[16,128,1]{2,0,1:T(8,128)} copy(f32[16,128,1]{1,0,2:T(8,128)S(1)} %get-tuple-element.46) | data formatting | bytes 16384 | tf_op jit(solution)/shard_map/broadcast_in_dim;squeeze | solution.py:26
  41.3 1.4 %copy.171 = f32[16,128,1]{2,0,1:T(8,128)} copy(f32[16,128,1]{1,0,2:T(8,128)S(1)} %get-tuple-element.47) | data formatting | bytes 16384 | tf_op jit(solution)/shard_map/broadcast_in_dim;squeeze | solution.py:26
  42.7 1.5 %copy.175 = f32[16,128,1]{2,0,1:T(8,128)} copy(f32[16,128,1]{1,0,2:T(8,128)S(1)} %get-tuple-element.48) | data formatting | bytes 16384 | tf_op jit(solution)/shard_map/broadcast_in_dim;squeeze | solution.py:26
  44.2 1.4 %copy.177 = f32[16,128,1]{2,0,1:T(8,128)} copy(f32[16,128,1]{1,0,2:T(8,128)S(1)} %get-tuple-element.49) | data formatting | bytes 16384 | tf_op jit(solution)/shard_map/broadcast_in_dim;squeeze | solution.py:26
  45.6 0.0 collective-permute-done.1
  45.7 9.2 %multiply_reduce_fusion.1 = (f32[16,128]{1,0:T(8,128)S(1)}, f32[16,128]{1,0:T(8,128)S(1)}, f32[16,128,128]{2,0,1:T(8,128)S(1)}, f32[16,128,128]{2,0,1:T(8,128)S(1)}) fusion(f32[16,128]{0,1:T(8,128)S(1)} %copy.191, f32[16,128]{0,1:T(8,128)S(1)} %copy.192, f32[16,128,128]{2,1,0:T(8,128)} %param.10, f32[16,128,128]{2,1,0:T(8,128)S(1)} %copy-done, ...), kind=kLoop, calls=%fused_computation.41 | loop fusion | flops 12578816 | bytes 17793088 | tf_op jit(solution)/shard_map/reduce_sum | solution.py:75
  54.9 35.3 %all-gather = f32[32,16,128]{2,1,0:T(8,128)S(1)} all-gather(f32[2,16,128]{2,1,0:T(8,128)S(1)} %pad_maximum_fusion.6), channel_id=2, replica_groups=mesh['gx'=16,'gy'=16] {'gx'}, dimensions={0}, use_global_device_ids=true | all-gather | bytes 278528 | tf_op jit(solution)/shard_map/all_gather | solution.py:79
  90.2 1.3 %copy.193 = f32[16,128,128]{2,1,0:T(8,128)} copy(f32[16,128,128]{2,0,1:T(8,128)S(1)} %get-tuple-element.19) | data formatting | bytes 2097152
  91.5 0.1 fusion.31
  91.7 2.8 %fusion.2 = f32[16,128,128]{2,1,0:T(8,128)} fusion(f32[16,128,128]{2,0,1:T(8,128)S(1)} %get-tuple-element.18, f32[16]{0:T(128)S(1)} %get-tuple-element.56, f32[16,128]{1,0:T(8,128)S(1)} %get-tuple-element.15, f32[16,128]{1,0:T(8,128)S(1)} %get-tuple-element.54, f32[16,128]{1,0:T(8,128)S(1)} %get-tuple-element.14, f32[16,128]{1,0:T(8,128)S(1)} %get-tuple-element.52, ...), kind=kOutput, calls=%fused_computation.4 | convolution fusion | flops 404226048 | bytes 2195584 | tf_op jit(solution)/shard_map/kij,kjc->kic/dot_general | solution.py:83
  (31 shorter events, 0.2 us)
Async XLA Ops:
  2.3 1.3 %copy-start.1 = (f32[1,16,128,128]{3,2,1,0:T(8,128)}, f32[1,16,128,128]{3,2,1,0:T(8,128)S(1)}, u32[]{:S(2)}) copy-start(f32[1,16,128,128]{3,2,1,0:T(8,128)S(1)} %get-tuple-element.20) | copy-start | bytes 3145732
  2.3 1.3 %copy-start.3 = (f32[1,16,128,128]{3,2,1,0:T(8,128)}, f32[1,16,128,128]{3,2,1,0:T(8,128)S(1)}, u32[]{:S(2)}) copy-start(f32[1,16,128,128]{3,2,1,0:T(8,128)S(1)} %get-tuple-element.21) | copy-start | bytes 3145732
  2.3 2.0 %copy-start = (f32[16,128,128]{2,1,0:T(8,128)S(1)}, f32[16,128,128]{2,1,0:T(8,128)}, u32[]{:S(2)}) copy-start(f32[16,128,128]{2,1,0:T(8,128)} %param.7) | copy-start | bytes 3145732
  3.6 8.8 %copy-start.5 = (f32[16,128,128]{2,0,1:T(8,128)}, f32[16,128,128]{2,0,1:T(8,128)S(1)}, u32[]{:S(2)}) copy-start(f32[16,128,128]{2,0,1:T(8,128)S(1)} %get-tuple-element.62) | copy-start | bytes 3145732
  5.0 34.9 %collective-permute-start = (f32[2,16,128]{2,1,0:T(8,128)S(1)}, f32[2,16,128]{2,1,0:T(8,128)S(1)}, u32[]{:S(2)}, u32[]{:S(2)}) collective-permute-start(f32[2,16,128]{2,1,0:T(8,128)S(1)} %pad_maximum_fusion.2), channel_id=1, source_target_pairs={{0,240},{16,0},{32,16},{48,32},{64,48},{80,64},{96,80},{112,96},{1... | collective-permute-start | bytes 49160 | tf_op jit(solution)/shard_map/ppermute | solution.py:20
  10.8 34.8 %collective-permute-start.1 = (f32[2,16,128]{2,1,0:T(8,128)S(1)}, f32[2,16,128]{2,1,0:T(8,128)S(1)}, u32[]{:S(2)}, u32[]{:S(2)}) collective-permute-start(f32[2,16,128]{2,1,0:T(8,128)S(1)} %pad_maximum_fusion.3), channel_id=1, source_target_pairs={{0,16},{16,32},{32,48},{48,64},{64,80},{80,96},{96,112},{112,128},... | collective-permute-start | bytes 49160 | tf_op jit(solution)/shard_map/ppermute | solution.py:19
  15.8 9.0 %copy-start.9 = (f32[16]{0:T(128)S(1)}, f32[16]{0:T(128)}, u32[]{:S(2)}) copy-start(f32[16]{0:T(128)} %param.11) | copy-start | bytes 196
  17.3 22.6 %collective-permute-start.2 = (f32[2,16,128]{2,1,0:T(8,128)S(1)}, f32[2,16,128]{2,1,0:T(8,128)S(1)}, u32[]{:S(2)}, u32[]{:S(2)}) collective-permute-start(f32[2,16,128]{2,1,0:T(8,128)S(1)} %pad_maximum_fusion.4), channel_id=1, source_target_pairs={{0,15},{1,0},{2,1},{3,2},{4,3},{5,4},{6,5},{7,6},{8,7},{9,8},{10,9... | collective-permute-start | bytes 49160 | tf_op jit(solution)/shard_map/ppermute | solution.py:20
  24.5 15.4 %collective-permute-start.3 = (f32[2,16,128]{2,1,0:T(8,128)S(1)}, f32[2,16,128]{2,1,0:T(8,128)S(1)}, u32[]{:S(2)}, u32[]{:S(2)}) collective-permute-start(f32[2,16,128]{2,1,0:T(8,128)S(1)} %pad_maximum_fusion.5), channel_id=1, source_target_pairs={{0,1},{1,2},{2,3},{3,4},{4,5},{5,6},{6,7},{7,8},{8,9},{9,10},{10,1... | collective-permute-start | bytes 49160 | tf_op jit(solution)/shard_map/ppermute | solution.py:19
  25.5 1.6 %copy-start.6 = (f32[16,128,128]{2,0,1:T(8,128)S(1)}, f32[16,128,128]{2,0,1:T(8,128)}, u32[]{:S(2)}) copy-start(f32[16,128,128]{2,0,1:T(8,128)} %copy-done.5) | copy-start | bytes 3145732
  30.2 1.6 %copy-start.10 = (f32[16]{0:T(128)S(1)}, f32[16]{0:T(128)}, u32[]{:S(2)}) copy-start(f32[16]{0:T(128)} %param.12) | copy-start | bytes 196
  30.2 1.6 %copy-start.8 = (f32[2,128,128]{2,1,0:T(8,128)S(1)}, f32[2,128,128]{2,1,0:T(8,128)}, u32[]{:S(2)}) copy-start(f32[2,128,128]{2,1,0:T(8,128)} %param.13) | copy-start | bytes 393220
  30.2 1.9 %copy-start.7 = (f32[16,128,128]{2,1,0:T(8,128)S(1)}, f32[16,128,128]{2,1,0:T(8,128)}, u32[]{:S(2)}) copy-start(f32[16,128,128]{2,1,0:T(8,128)} %param.9) | copy-start | bytes 3145732
  41.3 4.3 %copy-start.2 = (f32[1,16,128,128]{3,2,1,0:T(8,128)S(1)}, f32[1,16,128,128]{3,2,1,0:T(8,128)}, u32[]{:S(2)}) copy-start(f32[1,16,128,128]{3,2,1,0:T(8,128)} %copy-done.1) | copy-start | bytes 3145732
  41.3 4.3 %copy-start.4 = (f32[1,16,128,128]{3,2,1,0:T(8,128)S(1)}, f32[1,16,128,128]{3,2,1,0:T(8,128)}, u32[]{:S(2)}) copy-start(f32[1,16,128,128]{3,2,1,0:T(8,128)} %copy-done.3) | copy-start | bytes 3145732

commit v2 on v1

--- a/solution.py
+++ b/solution.py
@@ -68,20 +68,23 @@
     log_lam = jnp.log1p(-mu)[:, None]
 
     idx = jnp.arange(rows, dtype=jnp.float32)
-    to_end = jnp.exp(log_lam * (rows - 1 - idx)[None, :])
-    from_start = jnp.exp(log_lam * idx[None, :])
-    ends = jnp.stack(
+    dist = jnp.abs(idx[:, None] - idx[None, :])
+    kernel = jnp.concatenate(
         [
-            jnp.sum(to_end[:, :, None] * source, axis=1),
-            jnp.sum(from_start[:, :, None] * source, axis=1),
-        ]
+            jnp.exp(log_lam[:, :, None] * dist[None]),
+            jnp.exp(log_lam * (rows - 1 - idx)[None, :])[:, None, :],
+            jnp.exp(log_lam * idx[None, :])[:, None, :],
+            jnp.zeros((levels, 6, rows), jnp.float32),
+        ],
+        axis=1,
     )
-    gathered = lax.all_gather(ends, "gx", axis=0)
-
-    dist = jnp.abs(idx[:, None] - idx[None, :])
-    kernel = jnp.exp(log_lam[:, :, None] * dist[None])
-    local = jnp.einsum(
+    product = jnp.einsum(
         "kij,kjc->kic", kernel, source, precision=lax.Precision.HIGHEST
+    )
+    local = product[:, :rows]
+    ends = jnp.transpose(product[:, rows : rows + 2], (1, 0, 2))
+    gathered = lax.all_to_all(
+        jnp.broadcast_to(ends[None], (parts,) + ends.shape), "gx", 0, 0, tiled=True
     )
 
     others = jnp.arange(parts)

time: 94.8 us -> 75.1 us (0.79)
  the two profiles are of different devices: /device:TPU:8 before, /device:TPU:32 now
where the time goes in v2:
time: 75.1 us; the launch traced here: 74.6 us
  local copies, waits for them, and re-layouts  29.6 us (39%)
  other arithmetic  18.2 us (24%)
  starting transfers between devices  16.1 us (21%)
  waiting for transfers between devices  7.59 us (10%)
  matrix products  2.15 us (3%)
  between operations  0.88 us (1%)
    add x1, other arithmetic, on_device(): t + NEW_TERM_COEF * current_rate_change  9.93 us
    all_to_all x1, starting transfers between devices, periodic_solve(): lax.all_to_all(jnp.broadcast_to(ends[None], (parts,) + ends.shape), 'gx',...  9.2 us
    all_to_all x1, waiting for transfers between devices, periodic_solve(): lax.all_to_all(jnp.broadcast_to(ends[None], (parts,) + ends.shape), 'gx',...  7.58 us
    unnamed x30, local copies, waits for them, and re-layouts  6.52 us
    ppermute x2, starting transfers between devices, exchange_edges(): from_next = lax.ppermute(first, axis, ring_pairs(count, -1))  6.51 us
    slice x4, local copies, waits for them, and re-layouts, shifted(): return jnp.concatenate([lax.slice_in_dim(a, 1, n, axis=axis), halo], axis)  6.25 us
    another operation x8, local copies, waits for them, and re-layouts, shifted(): halo = jnp.expand_dims(halo, axis)  5.74 us
    slice x2, local copies, waits for them, and re-layouts, on_device(): v[:, :, 0]  3.28 us
  transfers between devices with their start and end apart: 5, of which 1 were waited for; matrix products, arithmetic and copies ran while one was open for 41% of the time, Pallas kernels for 0%

profile of v2, /device:TPU:32, one launch (start us, length us, event | category | flops | bytes accessed | tf_op | source)
XLA Modules:
  0.0 74.6 jit_solution(16121872904219149688)
XLA Ops:
  0.6 1.7 %fusion.44 = (f32[1,16,128,128]{3,2,1,0:T(8,128)S(1)}, f32[1,16,128,128]{3,2,1,0:T(8,128)S(1)}) fusion(f32[2,16,128,128]{3,2,1,0:T(8,128)} %param.8), kind=kLoop, calls=%fused_computation.101 | loop fusion | bytes 4194304 | tf_op jit(solution)/shard_map/slice | solution.py:118
  2.3 0.0 copy-start
  2.3 1.2 %copy_bitcast_fusion = (f32[16,128,128]{2,0,1:T(8,128)S(1)}, f32[16,128,128]{2,0,1:T(8,128)S(1)}) fusion(f32[1,16,128,128]{3,2,1,0:T(8,128)S(1)} %get-tuple-element.21, f32[1,16,128,128]{3,2,1,0:T(8,128)S(1)} %get-tuple-element.20), kind=kLoop, calls=%fused_computation.42 | loop fusion | bytes 4194304 | tf_op jit(solution)/shard_map/squeeze | solution.py:119
  3.6 0.1 copy-done.3
  3.7 0.7 copy-done
  4.3 0.6 copy.223
  5.0 1.9 %collective-permute-start = (f32[2,16,128]{2,1,0:T(8,128)S(1)}, f32[2,16,128]{2,1,0:T(8,128)S(1)}, u32[]{:S(2)}, u32[]{:S(2)}) collective-permute-start(f32[2,16,128]{2,1,0:T(8,128)S(1)} %pad_maximum_fusion.2), channel_id=1, source_target_pairs={{0,240},{16,0},{32,16},{48,32},{64,48},{80,64},{96,80},{112,96},{1... | collective-permute-start | bytes 49160 | tf_op jit(solution)/shard_map/ppermute | solution.py:20
  6.9 0.2 collective-permute-start.1
  7.1 1.7 %fusion.49 = (f32[16,128,1]{2,1,0:T(8,128)}, f32[16,128,1]{2,1,0:T(8,128)}) fusion(f32[16,128,128]{2,1,0:T(8,128)S(1)} %copy-done), kind=kLoop, calls=%fused_computation.106 | loop fusion | bytes 32768 | tf_op jit(solution)/shard_map/slice | solution.py:124
  8.7 1.6 %fusion.50 = (f32[16,128,1]{2,0,1:T(8,128)}, f32[16,128,1]{2,0,1:T(8,128)}) fusion(f32[16,128,128]{2,0,1:T(8,128)S(1)} %get-tuple-element.59), kind=kLoop, calls=%fused_computation.107 | loop fusion | bytes 32768 | tf_op jit(solution)/shard_map/slice | solution.py:124
  10.4 1.6 %copy.203 = f32[16,128,1]{1,0,2:T(8,128)S(1)} copy(f32[16,128,1]{2,0,1:T(8,128)} %get-tuple-element.36) | data formatting | bytes 16384 | tf_op jit(solution)/shard_map/slice | solution.py:124
  12.0 1.6 %copy.230 = f32[16,128,1]{1,0,2:T(8,128)S(1)} copy(f32[16,128,1]{2,1,0:T(8,128)} %get-tuple-element.34) | data formatting | bytes 16384
  13.6 4.6 %collective-permute-start.2 = (f32[2,16,128]{2,1,0:T(8,128)S(1)}, f32[2,16,128]{2,1,0:T(8,128)S(1)}, u32[]{:S(2)}, u32[]{:S(2)}) collective-permute-start(f32[2,16,128]{2,1,0:T(8,128)S(1)} %pad_maximum_fusion.4), channel_id=1, source_target_pairs={{0,15},{1,0},{2,1},{3,2},{4,3},{5,4},{6,5},{7,6},{8,7},{9,8},{10,9... | collective-permute-start | bytes 49160 | tf_op jit(solution)/shard_map/ppermute | solution.py:20
  18.2 1.6 %copy.209 = f32[16,128,1]{1,0,2:T(8,128)S(1)} copy(f32[16,128,1]{2,0,1:T(8,128)} %get-tuple-element.37) | data formatting | bytes 16384 | tf_op jit(solution)/shard_map/slice | solution.py:124
  19.8 1.6 %copy.231 = f32[16,128,1]{1,0,2:T(8,128)S(1)} copy(f32[16,128,1]{2,1,0:T(8,128)} %get-tuple-element.35) | data formatting | bytes 16384
  21.4 0.2 collective-permute-start.3
  21.6 0.6 fusion.53
  22.2 0.1 add_multiply_fusion
  22.3 1.6 %fusion.47 = (f32[16,128,127]{2,0,1:T(8,128)}, f32[16,128,127]{2,0,1:T(8,128)}) fusion(f32[16,128,128]{2,0,1:T(8,128)S(1)} %get-tuple-element.59), kind=kLoop, calls=%fused_computation.104 | loop fusion | bytes 4161536 | tf_op jit(solution)/shard_map/slice | solution.py:28
  23.9 1.5 %fusion.45 = (f32[16,127,128]{2,0,1:T(8,128)}, f32[16,127,128]{2,0,1:T(8,128)}) fusion(f32[16,128,128]{2,0,1:T(8,128)S(1)} %copy-done.6), kind=kLoop, calls=%fused_computation.102 | loop fusion | bytes 4161536 | tf_op jit(solution)/shard_map/slice | solution.py:28
  25.4 1.7 %fusion.48 = (f32[16,128,127]{2,0,1:T(8,128)}, f32[16,128,127]{2,0,1:T(8,128)}) fusion(f32[16,128,128]{2,0,1:T(8,128)S(1)} %copy.223), kind=kLoop, calls=%fused_computation.105 | loop fusion | bytes 4161536 | tf_op jit(solution)/shard_map/slice | solution.py:28
  27.1 1.5 %fusion.46 = (f32[16,127,128]{2,0,1:T(8,128)}, f32[16,127,128]{2,0,1:T(8,128)}) fusion(f32[16,128,128]{2,0,1:T(8,128)S(1)} %copy.223), kind=kLoop, calls=%fused_computation.103 | loop fusion | bytes 4161536 | tf_op jit(solution)/shard_map/slice | solution.py:28
  28.6 0.3 copy-done.9
  28.9 0.2 fusion.51
  29.2 0.4 copy-done.12
  29.6 0.1 multiply_exponential_fusion.4
  29.7 1.2 %multiply_exponential_fusion = f32[16,128,128]{2,1,0:T(8,128)} fusion(f32[128,128]{1,0:T(8,128)S(1)} %subtract_abs_fusion, f32[16]{0:T(128)S(1)} %get-tuple-element.17), kind=kLoop, calls=%fused_computation.47 | loop fusion | flops 262144 | bytes 1114176 | tf_op jit(solution)/shard_map/exp | solution.py:74
  30.9 2.2 %fusion.14 = f32[15,128,128]{2,0,1:T(8,128)} fusion(f32[16,128,128]{2,0,1:T(8,128)S(1)} %copy.223, f32[15,128,128]{2,1,0:T(8,128)S(1)} %get-tuple-element.39, f32[15,128,128]{2,1,0:T(8,128)S(1)} %get-tuple-element.38), kind=kLoop, calls=%fused_computation.18 | loop fusion | flops 983040 | bytes 4915200 | tf_op jit(solution)/shard_map/mul | solution.py:36
  33.1 1.3 %pad_maximum_fusion.6 = f32[17]{0:T(128)S(1)} fusion(f32[1]{0:T(128)} %get-tuple-element.56, f32[15]{0:T(128)S(1)} %add_multiply_fusion, f32[1]{0:T(128)} %get-tuple-element.55), kind=kLoop, calls=%fused_computation.91 | loop fusion | flops 34 | bytes 136 | tf_op jit(solution)/shard_map/concatenate | solution.py:47
  34.4 1.5 %fusion = f32[17,128,128]{2,0,1:T(8,128)} fusion(f32[1,128,128]{2,0,1:T(1,128)S(1)} %bitcast.57, f32[16,128,128]{2,0,1:T(8,128)S(1)} %copy.223, f32[1,128,128]{2,0,1:T(1,128)S(1)} %bitcast.56, f32[17]{0:T(128)S(1)} %pad_maximum_fusion.6), kind=kLoop, calls=%fused_computation.1 | loop fusion | flops 1114112 | bytes 2293828 | tf_op jit(solution)/shard_map/div | solution.py:55
  35.9 0.1 pad.36.clone
  36.0 0.0 collective-permute-done
  36.0 0.0 collective-permute-done.2
  36.1 1.4 %copy.204 = f32[16,128,1]{2,0,1:T(8,128)} copy(f32[16,128,1]{1,0,2:T(8,128)S(1)} %get-tuple-element.46) | data formatting | bytes 16384 | tf_op jit(solution)/shard_map/broadcast_in_dim;squeeze | solution.py:26
  37.5 1.4 %copy.206 = f32[16,128,1]{2,0,1:T(8,128)} copy(f32[16,128,1]{1,0,2:T(8,128)S(1)} %get-tuple-element.47) | data formatting | bytes 16384 | tf_op jit(solution)/shard_map/broadcast_in_dim;squeeze | solution.py:26
  38.9 1.4 %copy.210 = f32[16,128,1]{2,0,1:T(8,128)} copy(f32[16,128,1]{1,0,2:T(8,128)S(1)} %get-tuple-element.48) | data formatting | bytes 16384 | tf_op jit(solution)/shard_map/broadcast_in_dim;squeeze | solution.py:26
  40.3 1.5 %copy.212 = f32[16,128,1]{2,0,1:T(8,128)} copy(f32[16,128,1]{1,0,2:T(8,128)S(1)} %get-tuple-element.49) | data formatting | bytes 16384 | tf_op jit(solution)/shard_map/broadcast_in_dim;squeeze | solution.py:26
  41.8 0.0 copy-start.8
  41.8 9.9 %fusion.30 = (f32[16,128,128]{2,0,1:T(8,128)S(1)}, f32[16,128,128]{2,0,1:T(8,128)}) fusion(f32[16,128,128]{2,1,0:T(8,128)} %param.10, f32[16,128,128]{2,1,0:T(8,128)S(1)} %copy-done, f32[17,128,128]{2,0,1:T(8,128)} %fusion, f32[16]{0:T(128)S(1)} %copy-done.11, f32[15,128,128]{2,0,1:T(8,128)} %fusion.14, f32[16,128,127]{2,0,1:T(8,128)} %get-tuple-element.33, ...), kind=kLoop, calls=%fused_computation.46 | loop fusion | flops 11534336 | bytes 17760320 | tf_op jit(solution)/shard_map/add | solution.py:150
  51.8 2.1 %fusion.1 = f32[16,136,128]{2,1,0:T(8,128)S(1)} fusion(f32[16,1,128]{2,1,0:T(1,128)S(1)} %bitcast.59, f32[16,1,128]{2,1,0:T(1,128)S(1)} %bitcast.58, f32[16,128,128]{2,1,0:T(8,128)S(1)} %copy-done.8, f32[16,128,128]{2,0,1:T(8,128)S(1)} %get-tuple-element.18, f32[136]{0:T(256)S(1)} %pad.36.clone), kind=kOutput, calls=%fused_computation.2 | convolution fusion | flops 428654592 | bytes 3228192 | tf_op jit(solution)/shard_map/kij,kjc->kic/dot_general | solution.py:81
  54.0 0.7 broadcast_in_dim.5
  54.7 9.2 %all-to-all-start = ((f32[16,2,16,128]{3,2,1,0:T(8,128)}), f32[16,2,16,128]{3,2,1,0:T(8,128)S(1)}, u32[]{:S(2)}, u32[]{:S(2)}) async-start(f32[16,2,16,128]{3,2,1,0:T(8,128)} %broadcast_in_dim.5), calls=%async_computation | async-start | bytes 524288 | tf_op jit(solution)/shard_map/all_to_all | solution.py:86
  63.9 0.1 multiply_exponential_fusion.2
  64.0 0.1 exponential_divide_fusion
  64.1 1.3 %copy.227 = f32[16,128,128]{2,1,0:T(8,128)} copy(f32[16,128,128]{2,0,1:T(8,128)S(1)} %copy-done.7) | data formatting | bytes 2097152
  65.4 7.6 %all-to-all-done = f32[16,2,16,128]{3,2,1,0:T(8,128)S(1)} async-done(((f32[16,2,16,128]{3,2,1,0:T(8,128)}), f32[16,2,16,128]{3,2,1,0:T(8,128)S(1)}, u32[]{:S(2)}, u32[]{:S(2)}) %all-to-all-start) | async-done | bytes 262176 | tf_op jit(solution)/shard_map/all_to_all | solution.py:86
  73.0 0.1 fusion.35
  73.1 1.5 %fusion.9 = f32[16,128,128]{2,1,0:T(8,128)} fusion(f32[16,136,128]{2,1,0:T(8,128)S(1)} %fusion.1, f32[16]{0:T(128)S(1)} %get-tuple-element.54, f32[16,128]{1,0:T(8,128)S(1)} %get-tuple-element.15, f32[16,128]{1,0:T(8,128)S(1)} %get-tuple-element.53, f32[16,128]{1,0:T(8,128)S(1)} %get-tuple-element.14, f32[16,128]{1,0:T(8,128)S(1)} %get-tuple-element.52), kind=kLoop, calls=%fused_computation.11 | loop fusion | flops 1310720 | bytes 2129984 | tf_op jit(solution)/shard_map/div | solution.py:105
  (41 shorter events, 0.2 us)
Async XLA Ops:
  2.3 1.3 %copy-start.1 = (f32[1,16,128,128]{3,2,1,0:T(8,128)}, f32[1,16,128,128]{3,2,1,0:T(8,128)S(1)}, u32[]{:S(2)}) copy-start(f32[1,16,128,128]{3,2,1,0:T(8,128)S(1)} %get-tuple-element.20) | copy-start | bytes 3145732
  2.3 1.3 %copy-start.3 = (f32[1,16,128,128]{3,2,1,0:T(8,128)}, f32[1,16,128,128]{3,2,1,0:T(8,128)S(1)}, u32[]{:S(2)}) copy-start(f32[1,16,128,128]{3,2,1,0:T(8,128)S(1)} %get-tuple-element.21) | copy-start | bytes 3145732
  2.3 2.0 %copy-start = (f32[16,128,128]{2,1,0:T(8,128)S(1)}, f32[16,128,128]{2,1,0:T(8,128)}, u32[]{:S(2)}) copy-start(f32[16,128,128]{2,1,0:T(8,128)} %param.7) | copy-start | bytes 3145732
  3.7 5.1 %copy-start.5 = (f32[16,128,128]{2,0,1:T(8,128)}, f32[16,128,128]{2,0,1:T(8,128)S(1)}, u32[]{:S(2)}) copy-start(f32[16,128,128]{2,0,1:T(8,128)S(1)} %get-tuple-element.60) | copy-start | bytes 3145732
  5.0 31.1 %collective-permute-start = (f32[2,16,128]{2,1,0:T(8,128)S(1)}, f32[2,16,128]{2,1,0:T(8,128)S(1)}, u32[]{:S(2)}, u32[]{:S(2)}) collective-permute-start(f32[2,16,128]{2,1,0:T(8,128)S(1)} %pad_maximum_fusion.2), channel_id=1, source_target_pairs={{0,240},{16,0},{32,16},{48,32},{64,48},{80,64},{96,80},{112,96},{1... | collective-permute-start | bytes 49160 | tf_op jit(solution)/shard_map/ppermute | solution.py:20
  6.9 34.9 %collective-permute-start.1 = (f32[2,16,128]{2,1,0:T(8,128)S(1)}, f32[2,16,128]{2,1,0:T(8,128)S(1)}, u32[]{:S(2)}, u32[]{:S(2)}) collective-permute-start(f32[2,16,128]{2,1,0:T(8,128)S(1)} %pad_maximum_fusion.3), channel_id=1, source_target_pairs={{0,16},{16,32},{32,48},{48,64},{64,80},{80,96},{96,112},{112,128},... | collective-permute-start | bytes 49160 | tf_op jit(solution)/shard_map/ppermute | solution.py:19
  12.0 9.6 %copy-start.11 = (f32[16]{0:T(128)S(1)}, f32[16]{0:T(128)}, u32[]{:S(2)}) copy-start(f32[16]{0:T(128)} %param.11) | copy-start | bytes 196
  13.6 22.5 %collective-permute-start.2 = (f32[2,16,128]{2,1,0:T(8,128)S(1)}, f32[2,16,128]{2,1,0:T(8,128)S(1)}, u32[]{:S(2)}, u32[]{:S(2)}) collective-permute-start(f32[2,16,128]{2,1,0:T(8,128)S(1)} %pad_maximum_fusion.4), channel_id=1, source_target_pairs={{0,15},{1,0},{2,1},{3,2},{4,3},{5,4},{6,5},{7,6},{8,7},{9,8},{10,9... | collective-permute-start | bytes 49160 | tf_op jit(solution)/shard_map/ppermute | solution.py:20
  21.4 14.7 %collective-permute-start.3 = (f32[2,16,128]{2,1,0:T(8,128)S(1)}, f32[2,16,128]{2,1,0:T(8,128)S(1)}, u32[]{:S(2)}, u32[]{:S(2)}) collective-permute-start(f32[2,16,128]{2,1,0:T(8,128)S(1)} %pad_maximum_fusion.5), channel_id=1, source_target_pairs={{0,1},{1,2},{2,3},{3,4},{4,5},{5,6},{6,7},{7,8},{8,9},{9,10},{10,1... | collective-permute-start | bytes 49160 | tf_op jit(solution)/shard_map/ppermute | solution.py:19
  22.3 1.6 %copy-start.6 = (f32[16,128,128]{2,0,1:T(8,128)S(1)}, f32[16,128,128]{2,0,1:T(8,128)}, u32[]{:S(2)}) copy-start(f32[16,128,128]{2,0,1:T(8,128)} %copy-done.5) | copy-start | bytes 3145732
  27.1 1.5 %copy-start.10 = (f32[2,128,128]{2,1,0:T(8,128)S(1)}, f32[2,128,128]{2,1,0:T(8,128)}, u32[]{:S(2)}) copy-start(f32[2,128,128]{2,1,0:T(8,128)} %param.13) | copy-start | bytes 393220
  27.1 1.8 %copy-start.9 = (f32[16,128,128]{2,1,0:T(8,128)S(1)}, f32[16,128,128]{2,1,0:T(8,128)}, u32[]{:S(2)}) copy-start(f32[16,128,128]{2,1,0:T(8,128)} %param.9) | copy-start | bytes 3145732
  28.9 0.7 copy-start.12
  37.5 4.3 %copy-start.2 = (f32[1,16,128,128]{3,2,1,0:T(8,128)S(1)}, f32[1,16,128,128]{3,2,1,0:T(8,128)}, u32[]{:S(2)}) copy-start(f32[1,16,128,128]{3,2,1,0:T(8,128)} %copy-done.1) | copy-start | bytes 3145732
  37.5 4.3 %copy-start.4 = (f32[1,16,128,128]{3,2,1,0:T(8,128)S(1)}, f32[1,16,128,128]{3,2,1,0:T(8,128)}, u32[]{:S(2)}) copy-start(f32[1,16,128,128]{3,2,1,0:T(8,128)} %copy-done.3) | copy-start | bytes 3145732
  41.8 9.9 %copy-start.8 = (f32[16,128,128]{2,1,0:T(8,128)S(1)}, f32[16,128,128]{2,1,0:T(8,128)}, u32[]{:S(2)}) copy-start(f32[16,128,128]{2,1,0:T(8,128)} %multiply_exponential_fusion) | copy-start | bytes 3145732
  51.8 12.3 %copy-start.7 = (f32[16,128,128]{2,0,1:T(8,128)S(1)}, f32[16,128,128]{2,0,1:T(8,128)}, u32[]{:S(2)}) copy-start(f32[16,128,128]{2,0,1:T(8,128)} %get-tuple-element.19) | copy-start | bytes 3145732
  54.7 18.2 %all-to-all-start = ((f32[16,2,16,128]{3,2,1,0:T(8,128)}), f32[16,2,16,128]{3,2,1,0:T(8,128)S(1)}, u32[]{:S(2)}, u32[]{:S(2)}) async-start(f32[16,2,16,128]{3,2,1,0:T(8,128)} %broadcast_in_dim.5), calls=%async_computation | async-start | bytes 524288 | tf_op jit(solution)/shard_map/all_to_all | solution.py:86

commit v3 on v2

v3 whole, which is shorter than its diff:
```python
import jax
import jax.numpy as jnp
from jax import lax
from jax.experimental import pallas as pl
from jax.experimental.pallas import tpu as pltpu
from jax.sharding import PartitionSpec as P

COURANT = 0.5
DIFF_Y = 0.2
DIFF_Z = 0.25
NEW_TERM_COEF = 0.75
OLD_TERM_COEF = -5.0 / 12.0


def ring_pairs(count, step):
    return [(i, (i + step) % count) for i in range(count)]


def exchange_edges(first, last, axis):
    count = lax.axis_size(axis)
    from_prev = lax.ppermute(last, axis, ring_pairs(count, 1))
    from_next = lax.ppermute(first, axis, ring_pairs(count, -1))
    return from_prev, from_next


def periodic_solve(source, ratio):
    levels, rows, cols = source.shape
    parts = lax.axis_size("gx")
    me = lax.axis_index("gx")
    root = jnp.sqrt(1.0 + 4.0 * ratio)
    mu = (1.0 + root) / ((1.0 + 2.0 * ratio) + root)
    log_lam = jnp.log1p(-mu)[:, None]

    idx = jnp.arange(rows, dtype=jnp.float32)
    dist = jnp.abs(idx[:, None] - idx[None, :])
    kernel = jnp.concatenate(
        [
            jnp.exp(log_lam[:, :, None] * dist[None]),
            jnp.exp(log_lam * (rows - 1 - idx)[None, :])[:, None, :],
            jnp.exp(log_lam * idx[None, :])[:, None, :],
            jnp.zeros((levels, 6, rows), jnp.float32),
        ],
        axis=1,
    )
    product = jnp.einsum(
        "kij,kjc->kic", kernel, source, precision=lax.Precision.HIGHEST
    )
    local = product[:, :rows]
    ends = jnp.transpose(product[:, rows : rows + 2], (1, 0, 2))
    gathered = lax.all_to_all(
        jnp.broadcast_to(ends[None], (parts,) + ends.shape), "gx", 0, 0, tiled=True
    )

    others = jnp.arange(parts)
    whole = -jnp.expm1(log_lam * (parts * rows))
    lag_f = ((me - others - 1) % parts).astype(jnp.float32) * rows
    lag_b = ((others - me - 1) % parts).astype(jnp.float32) * rows
    weight_f = jnp.exp(log_lam * lag_f[None, :]) / whole
    weight_b = jnp.exp(log_lam * lag_b[None, :]) / whole
    carry_f = jnp.sum(weight_f.T[:, :, None] * gathered[:, 0], axis=0)
    carry_b = jnp.sum(weight_b.T[:, :, None] * gathered[:, 1], axis=0)
    into_f = jnp.exp(log_lam * (idx + 1.0)[None, :])
    into_b = jnp.exp(log_lam * (rows - idx)[None, :])
    total = (
        local
        + into_f[:, :, None] * carry_f[:, None, :]
        + into_b[:, :, None] * carry_b[:, None, :]
    )
    return total / root[:, None, None]


def stencil_kernel(
    spacing_ref, between_ref, t_ref, u_ref, v_ref, w_ref, early_ref, wall_ref, xh_ref, yh_ref,
    rate_ref, source_ref,
):
    k = pl.program_id(0)
    top = pl.num_programs(0) - 1
    below = jnp.maximum(k - 1, 0)
    above = jnp.minimum(k + 1, top)
    t = t_ref[k]
    u = u_ref[0, 0]
    v = v_ref[0, 0]
    w = w_ref[k]
    rows, cols = t.shape
    row = lax.broadcasted_iota(jnp.int32, (rows, cols), 0)
    col = lax.broadcasted_iota(jnp.int32, (rows, cols), 1)
    xh = xh_ref[0]
    yh = yh_ref[0].T

    def along_x(a, prev, nxt):
        a_next = jnp.where(row == rows - 1, nxt, pltpu.roll(a, rows - 1, 0))
        a_prev = jnp.where(row == 0, prev, pltpu.roll(a, 1, 0))
        return a_prev, a_next

    def along_y(a, prev, nxt):
        a_next = jnp.where(col == cols - 1, nxt, pltpu.roll(a, cols - 1, 1))
        a_prev = jnp.where(col == 0, prev, pltpu.roll(a, 1, 1))
        return a_prev, a_next

    t_xp, t_xn = along_x(t, xh[0:1], xh[2:3])
    u_xp, u_xn = along_x(u, xh[1:2], xh[3:4])
    t_yp, t_yn = along_y(t, yh[:, 0:1], yh[:, 2:3])
    v_yp, v_yn = along_y(v, yh[:, 1:2], yh[:, 3:4])
    flux_x_hi = (u + u_xn) * (t + t_xn) * 0.25
    flux_x_lo = (u_xp + u) * (t_xp + t) * 0.25
    flux_y_hi = (v + v_yn) * (t + t_yn) * 0.25
    flux_y_lo = (v_yp + v) * (t_yp + t) * 0.25
    advect_xy = (flux_x_hi - flux_x_lo) + (flux_y_hi - flux_y_lo)

    t_up = t_ref[above]
    t_dn = t_ref[below]
    flux_up = jnp.where(k == top, 0.0, (w + w_ref[above]) * (t + t_up) * 0.25)
    flux_dn = jnp.where(k == 0, 0.0, (w_ref[below] + w) * (t_dn + t) * 0.25)
    dz = spacing_ref[k]
    carry_through_depth = (flux_up - flux_dn) / dz
    ghost_up = jnp.where(k == top, wall_ref[1], t_up)
    ghost_dn = jnp.where(k == 0, wall_ref[0], t_dn)
    slope_up = (ghost_up - t) / between_ref[k + 1]
    slope_dn = (t - ghost_dn) / between_ref[k]
    thermal_spreading_step = (slope_up - slope_dn) / dz
    stacked_layer_count = t_yn - 2.0 * t + t_yp
    rate = (
        -COURANT * (advect_xy + carry_through_depth)
        + DIFF_Y * stacked_layer_count
        + DIFF_Z * thermal_spreading_step
    )
    rate_ref[0] = rate
    source_ref[0] = t + NEW_TERM_COEF * rate + OLD_TERM_COEF * early_ref[0]


def on_device(
    initial_warmth_field,
    horizontal_motion_pair,
    z_directed_motion,
    earlier_rate_change,
    layer_depth_spacing,
    backward_spread_ratio,
    wall_warmth_bounds,
):
    t = initial_warmth_field
    levels, rows, cols = t.shape
    u = horizontal_motion_pair[0]
    v = horizontal_motion_pair[1]
    x_prev, x_next = exchange_edges(
        jnp.stack([t[:, 0, :], u[:, 0, :]], 1), jnp.stack([t[:, -1, :], u[:, -1, :]], 1), "gx"
    )
    y_prev, y_next = exchange_edges(
        jnp.stack([t[:, :, 0], v[:, :, 0]], 1), jnp.stack([t[:, :, -1], v[:, :, -1]], 1), "gy"
    )
    pad = jnp.zeros((levels, 4, rows), jnp.float32)
    x_halo = jnp.concatenate([x_prev, x_next, pad], 1)
    y_halo = jnp.concatenate([y_prev, y_next, pad], 1)
    between = jnp.concatenate(
        [
            layer_depth_spacing[:1],
            0.5 * (layer_depth_spacing[:-1] + layer_depth_spacing[1:]),
            layer_depth_spacing[-1:],
        ],
        0,
    )
    whole = lambda shape: pl.BlockSpec(shape, lambda k: (0,) * len(shape))
    level = lambda shape: pl.BlockSpec(shape, lambda k: (k,) + (0,) * (len(shape) - 1))
    smem = pl.BlockSpec(memory_space=pltpu.SMEM)
    current_rate_change, linear_system_source = pl.pallas_call(
        stencil_kernel,
        grid=(levels,),
        in_specs=[
            smem,
            smem,
            whole((levels, rows, cols)),
            pl.BlockSpec((1, 1, rows, cols), lambda k: (0, k, 0, 0)),
            pl.BlockSpec((1, 1, rows, cols), lambda k: (1, k, 0, 0)),
            whole((levels, rows, cols)),
            level((1, rows, cols)),
            whole((2, rows, cols)),
            level((1, 8, cols)),
            level((1, 8, rows)),
        ],
        out_specs=[level((1, rows, cols)), level((1, rows, cols))],
        out_shape=[jax.ShapeDtypeStruct(t.shape, jnp.float32)] * 2,
        cost_estimate=pl.CostEstimate(
            flops=80 * t.size, bytes_accessed=4 * 8 * t.size, transcendentals=0
        ),
    )(
        layer_depth_spacing, between, t, horizontal_motion_pair, horizontal_motion_pair,
        z_directed_motion, earlier_rate_change, wall_warmth_bounds, x_halo, y_halo,
    )
    resulting_warmth_field = periodic_solve(linear_system_source, backward_spread_ratio)
    return (resulting_warmth_field, current_rate_change)


def solution(mesh):
    in_specs = (
        P(None, "gx", "gy"),
        P(None, None, "gx", "gy"),
        P(None, "gx", "gy"),
        P(None, "gx", "gy"),
        P(),
        P(),
        P(None, "gx", "gy"),
    )
    out_specs = (P(None, "gx", "gy"), P(None, "gx", "gy"))
    return jax.shard_map(
        on_device, mesh=mesh, in_specs=in_specs, out_specs=out_specs, check_vma=False
    )
```

time: 75.1 us -> 57.6 us (0.77)
  local copies, waits for them, and re-layouts: 29.6 us -> 7.47 us
  other arithmetic: 18.2 us -> 4.96 us
  Pallas kernels: 0 us -> 12.9 us
  starting transfers between devices: 16.1 us -> 18.5 us
  waiting for transfers between devices: 7.59 us -> 8.89 us
  matrix products: 2.15 us -> 3.19 us
    pallas_call x0 -> x1, Pallas kernels: none -> 12.9 us  [on_device(): pl.pallas_call(stencil_kernel, grid=(levels,), in_specs=[smem, smem, whol...]
    slice x12 -> x4, local copies, waits for them, and re-layouts: 15.3 us -> 3.76 us  [the longest x1 1.81 us: on_device(): v = horizontal_motion_pair[1]]
    add x1 -> x0, other arithmetic: 9.93 us -> none  [on_device(): t + NEW_TERM_COEF * current_rate_change]
    another operation x10 -> x1, local copies, waits for them, and re-layouts: 5.75 us -> 0.73 us  [on_device(): jnp.stack([t[:, :, -1], v[:, :, -1]], 1)]
    unnamed x30 -> x11, local copies, waits for them, and re-layouts: 6.52 us -> 2.08 us
    mul x2 -> x1, other arithmetic: 2.29 us -> 0.07 us  [on_device(): 0.5 * (layer_depth_spacing[:-1] + layer_depth_spacing[1:])]
    ppermute x2, starting transfers between devices: 0.42 us -> 2.05 us  [exchange_edges(): from_prev = lax.ppermute(last, axis, ring_pairs(count, 1))]
    all_to_all x1, starting transfers between devices: 9.2 us -> 10.8 us  [periodic_solve(): lax.all_to_all(jnp.broadcast_to(ends[None], (parts,) + ends.shape), 'gx',...]
  transfers between devices with their start and end apart: 5 -> 5, of which waited for: 1 -> 1; matrix products, arithmetic and copies ran while one was open for 41% -> 13% of each run, Pallas kernels for 0% -> 0%
where the time goes in v3:
time: 57.6 us; the launch traced here: 56.6 us
  starting transfers between devices  18.5 us (32%)
  Pallas kernels  12.9 us (22%)
  waiting for transfers between devices  8.89 us (15%)
  local copies, waits for them, and re-layouts  7.47 us (13%)
  other arithmetic  4.96 us (9%)
  matrix products  3.19 us (6%)
  between operations  0.78 us (1%)
    pallas_call x1, Pallas kernels, on_device(): pl.pallas_call(stencil_kernel, grid=(levels,), in_specs=[smem, smem, whol...  12.9 us
    all_to_all x1, starting transfers between devices, periodic_solve(): lax.all_to_all(jnp.broadcast_to(ends[None], (parts,) + ends.shape), 'gx',...  10.8 us
    all_to_all x1, waiting for transfers between devices, periodic_solve(): lax.all_to_all(jnp.broadcast_to(ends[None], (parts,) + ends.shape), 'gx',...  8.88 us
    ppermute x2, starting transfers between devices, exchange_edges(): from_next = lax.ppermute(first, axis, ring_pairs(count, -1))  5.61 us
    dot_general x1, matrix products, periodic_solve(): jnp.einsum('kij,kjc->kic', kernel, source, precision=lax.Precision.HIGHEST)  3.19 us
    unnamed x11, local copies, waits for them, and re-layouts  2.08 us
    ppermute x2, starting transfers between devices, exchange_edges(): from_prev = lax.ppermute(last, axis, ring_pairs(count, 1))  2.05 us
    concatenate x1, other arithmetic, on_device(): jnp.concatenate([layer_depth_spacing[:1], 0.5 * (layer_depth_spacing[:-1]...  1.88 us
  transfers between devices with their start and end apart: 5, of which 1 were waited for; matrix products, arithmetic and copies ran while one was open for 13% of the time, Pallas kernels for 0%

profile of v3, /device:TPU:32, one launch (start us, length us, event | category | flops | bytes accessed | tf_op | source)
XLA Modules:
  0.0 56.6 jit_solution(11378071222144059291)
XLA Ops:
  0.6 0.0 copy-start
  0.6 1.8 %fusion.21 = (f32[1,16,128,128]{3,2,1,0:T(8,128)S(1)}, f32[16,128,128]{2,1,0:T(8,128)S(1)}) fusion(f32[2,16,128,128]{3,2,1,0:T(8,128)} %v_ref.1), kind=kLoop, calls=%fused_computation.56 | loop fusion | bytes 4194304 | tf_op jit(solution)/shard_map/slice | solution.py:143
  2.5 0.0 copy-done
  2.5 2.0 %collective-permute-start = (f32[16,2,128]{2,1,0:T(2,128)S(1)}, f32[16,2,128]{2,1,0:T(2,128)S(1)}, u32[]{:S(2)}, u32[]{:S(2)}) collective-permute-start(f32[16,2,128]{2,1,0:T(2,128)S(1)} %pad_maximum_fusion), channel_id=1, source_target_pairs={{0,16},{16,32},{32,48},{48,64},{64,80},{80,96},{96,112},{112,128},... | collective-permute-start | bytes 49160 | tf_op jit(solution)/shard_map/ppermute | solution.py:21
  4.6 0.2 collective-permute-start.1
  4.7 1.3 %fusion.22 = (f32[16,128,1]{2,1,0:T(8,128)}, f32[16,128,1]{2,1,0:T(8,128)S(1)}) fusion(f32[16,128,128]{2,1,0:T(8,128)S(1)} %copy-done), kind=kLoop, calls=%fused_computation.57 | loop fusion | bytes 32768 | tf_op jit(solution)/shard_map/slice | solution.py:148
  6.1 0.0 copy-start.1
  6.1 1.4 %copy.27 = f32[1,16,128,128]{2,1,3,0:T(8,128)} copy(f32[1,16,128,128]{3,2,1,0:T(8,128)S(1)} %get-tuple-element.10) | data formatting | bytes 2097152
  7.5 0.0 copy-start.2
  7.5 0.7 %slice_bitcast_fusion.4 = (f32[16,1,128]{2,0,1:T(8,128)S(1)}, f32[16,128,1]{1,0,2:T(8,128)S(1)}) fusion(f32[16,128,128]{1,0,2:T(8,128)} %bitcast.25), kind=kLoop, calls=%fused_computation.27 | loop fusion | bytes 32768 | tf_op jit(solution)/shard_map/stack;squeeze | solution.py:148
  8.2 0.0 copy-done.1
  8.2 0.0 copy-start.3
  8.2 0.3 copy.26
  8.5 0.1 collective-permute-start.2
  8.6 0.3 copy.28
  9.0 5.4 %collective-permute-start.3 = (f32[16,2,128]{2,1,0:T(2,128)S(1)}, f32[16,2,128]{2,1,0:T(2,128)S(1)}, u32[]{:S(2)}, u32[]{:S(2)}) collective-permute-start(f32[16,2,128]{2,1,0:T(2,128)S(1)} %pad_maximum_fusion.3), channel_id=1, source_target_pairs={{0,15},{1,0},{2,1},{3,2},{4,3},{5,4},{6,5},{7,6},{8,7},{9,8},{10,9... | collective-permute-start | bytes 49160 | tf_op jit(solution)/shard_map/ppermute | solution.py:22
  14.4 0.0 copy-done.2
  14.4 0.6 %fusion.25 = (f32[1]{0:T(128)}, f32[1]{0:T(128)}) fusion(f32[16]{0:T(128)S(1)} %copy-done.2), kind=kLoop, calls=%fused_computation.60 | loop fusion | bytes 16 | tf_op jit(solution)/shard_map/slice | solution.py:155
  15.0 0.1 add_multiply_fusion
  15.1 0.0 copy-done.3
  15.1 0.1 multiply_exponential_fusion.4
  15.2 0.2 multiply_exponential_fusion
  15.4 1.9 %pad_maximum_fusion.4.between_ref = f32[17]{0:T(128)} fusion(f32[1]{0:T(128)} %get-tuple-element.30, f32[15]{0:T(128)S(1)} %add_multiply_fusion, f32[1]{0:T(128)} %get-tuple-element.29), kind=kLoop, calls=%fused_computation.46 | loop fusion | flops 34 | bytes 136 | tf_op jit(solution)/shard_map/concatenate | solution.py:153
  17.3 0.1 pad.9.clone
  17.4 0.1 pad.20.clone
  17.5 0.0 collective-permute-done.2
  17.5 0.0 collective-permute-done
  17.5 0.0 collective-permute-done.1
  17.5 0.0 collective-permute-done.3
  17.5 0.8 %maximum_maximum_fusion.1 = (f32[16,8,128]{2,1,0:T(8,128)}, f32[16,8,128]{2,1,0:T(8,128)}) fusion(f32[16,2,128]{2,1,0:T(2,128)S(1)} %collective-permute-done.3, f32[16,2,128]{2,1,0:T(2,128)S(1)} %copy.24, f32[8]{0:T(128)S(1)} %pad.9.clone, f32[16,2,128]{2,1,0:T(2,128)S(1)} %collective-permute-done.1, f32[16,2,128]{2,1,0:T(2,128)S(1)} %collective-permute-done), kind=kLoop, calls=%fused_computation.20 | loop fusion | flops 65536 | bytes 196640 | tf_op jit(solution)/shard_map/concatenate | solution.py:152
  18.3 12.9 %shard_map.86 = (f32[16,128,128]{2,1,0:T(8,128)}, f32[16,128,128]{2,1,0:T(8,128)}) custom-call(f32[16]{0:T(128)} %spacing_ref.1, f32[17]{0:T(128)} %pad_maximum_fusion.4.between_ref, f32[16,128,128]{2,1,0:T(8,128)} %t_ref.1, f32[2,16,128,128]{3,2,1,0:T(8,128)} %v_ref.1, f32[2,16,128,128]{3,2,1,0:T(8,128)} %v_ref.1, f32[16,128,128]{2,1,0:T(8,128)} %w_ref.1, ...), custom_call_target="tpu_custom_call" | custom-call | flops 20971520 | bytes 8388608 | tf_op jit(solution)/shard_map/pallas_call | solution.py:164
  31.2 3.2 %fusion = f32[16,136,128]{2,1,0:T(8,128)S(1)} fusion(f32[16,128,128]{2,1,0:T(8,128)} %get-tuple-element.4, f32[16,1,128]{2,1,0:T(1,128)S(1)} %bitcast.27, f32[16,1,128]{2,1,0:T(1,128)S(1)} %bitcast.26, f32[16,128,128]{2,1,0:T(8,128)S(1)} %multiply_exponential_fusion, f32[136]{0:T(256)S(1)} %pad.20.clone), kind=kOutput, calls=%fused_computation | convolution fusion | flops 428654592 | bytes 3228192 | tf_op jit(solution)/shard_map/kij,kjc->kic/dot_general | solution.py:45
  34.4 0.7 %broadcast_in_dim.8 = f32[16,2,16,128]{3,2,1,0:T(8,128)} broadcast(f32[2,16,128]{2,1,0:T(8,128)S(1)} %copy.25), dimensions={1,2,3} | broadcast | bytes 278528 | tf_op jit(solution)/shard_map/broadcast_in_dim | solution.py:51
  35.1 10.8 %all-to-all-start = ((f32[16,2,16,128]{3,2,1,0:T(8,128)}), f32[16,2,16,128]{3,2,1,0:T(8,128)S(1)}, u32[]{:S(2)}, u32[]{:S(2)}) async-start(f32[16,2,16,128]{3,2,1,0:T(8,128)} %broadcast_in_dim.8), calls=%async_computation | async-start | bytes 524288 | tf_op jit(solution)/shard_map/all_to_all | solution.py:50
  45.9 0.1 multiply_exponential_fusion.2
  46.0 0.1 exponential_divide_fusion
  46.1 8.9 %all-to-all-done = f32[16,2,16,128]{3,2,1,0:T(8,128)S(1)} async-done(((f32[16,2,16,128]{3,2,1,0:T(8,128)}), f32[16,2,16,128]{3,2,1,0:T(8,128)S(1)}, u32[]{:S(2)}, u32[]{:S(2)}) %all-to-all-start) | async-done | bytes 262176 | tf_op jit(solution)/shard_map/all_to_all | solution.py:50
  55.0 0.1 fusion.13
  55.1 1.5 %fusion.8 = f32[16,128,128]{2,1,0:T(8,128)} fusion(f32[16,136,128]{2,1,0:T(8,128)S(1)} %fusion, f32[16]{0:T(128)S(1)} %get-tuple-element.24, f32[16,128]{1,0:T(8,128)S(1)} %get-tuple-element.7, f32[16,128]{1,0:T(8,128)S(1)} %get-tuple-element.23, f32[16,128]{1,0:T(8,128)S(1)} %get-tuple-element.6, f32[16,128]{1,0:T(8,128)S(1)} %get-tuple-element.22), kind=kLoop, calls=%fused_computation.9 | loop fusion | flops 1310720 | bytes 2129984 | tf_op jit(solution)/shard_map/div | solution.py:69
  (15 shorter events, 0.2 us)
Async XLA Ops:
  0.6 1.9 %copy-start = (f32[16,128,128]{2,1,0:T(8,128)S(1)}, f32[16,128,128]{2,1,0:T(8,128)}, u32[]{:S(2)}) copy-start(f32[16,128,128]{2,1,0:T(8,128)} %t_ref.1) | copy-start | bytes 3145732
  2.5 15.0 %collective-permute-start = (f32[16,2,128]{2,1,0:T(2,128)S(1)}, f32[16,2,128]{2,1,0:T(2,128)S(1)}, u32[]{:S(2)}, u32[]{:S(2)}) collective-permute-start(f32[16,2,128]{2,1,0:T(2,128)S(1)} %pad_maximum_fusion), channel_id=1, source_target_pairs={{0,16},{16,32},{32,48},{48,64},{64,80},{80,96},{96,112},{112,128},... | collective-permute-start | bytes 49160 | tf_op jit(solution)/shard_map/ppermute | solution.py:21
  4.6 13.0 %collective-permute-start.1 = (f32[16,2,128]{2,1,0:T(2,128)S(1)}, f32[16,2,128]{2,1,0:T(2,128)S(1)}, u32[]{:S(2)}, u32[]{:S(2)}) collective-permute-start(f32[16,2,128]{2,1,0:T(2,128)S(1)} %pad_maximum_fusion.1), channel_id=1, source_target_pairs={{0,240},{16,0},{32,16},{48,32},{64,48},{80,64},{96,80},{112,96},{1... | collective-permute-start | bytes 49160 | tf_op jit(solution)/shard_map/ppermute | solution.py:22
  6.1 2.1 %copy-start.1 = (f32[16,128,1]{2,1,0:T(8,128)S(1)}, f32[16,128,1]{2,1,0:T(8,128)}, u32[]{:S(2)}) copy-start(f32[16,128,1]{2,1,0:T(8,128)} %get-tuple-element.12) | copy-start | bytes 24580
  7.5 6.9 %copy-start.2 = (f32[16]{0:T(128)S(1)}, f32[16]{0:T(128)}, u32[]{:S(2)}) copy-start(f32[16]{0:T(128)} %spacing_ref.1) | copy-start | bytes 196
  8.2 6.9 %copy-start.3 = (f32[16]{0:T(128)S(1)}, f32[16]{0:T(128)}, u32[]{:S(2)}) copy-start(f32[16]{0:T(128)} %param.12) | copy-start | bytes 196
  8.5 9.0 %collective-permute-start.2 = (f32[16,2,128]{2,0,1:T(8,128)S(1)}, f32[16,2,128]{2,0,1:T(8,128)S(1)}, u32[]{:S(2)}, u32[]{:S(2)}) collective-permute-start(f32[16,2,128]{2,0,1:T(8,128)S(1)} %pad_maximum_fusion.2), channel_id=1, source_target_pairs={{0,1},{1,2},{2,3},{3,4},{4,5},{5,6},{6,7},{7,8},{8,9},{9,10},{10,1... | collective-permute-start | bytes 49160 | tf_op jit(solution)/shard_map/ppermute | solution.py:21
  9.0 8.6 %collective-permute-start.3 = (f32[16,2,128]{2,1,0:T(2,128)S(1)}, f32[16,2,128]{2,1,0:T(2,128)S(1)}, u32[]{:S(2)}, u32[]{:S(2)}) collective-permute-start(f32[16,2,128]{2,1,0:T(2,128)S(1)} %pad_maximum_fusion.3), channel_id=1, source_target_pairs={{0,15},{1,0},{2,1},{3,2},{4,3},{5,4},{6,5},{7,6},{8,7},{9,8},{10,9... | collective-permute-start | bytes 49160 | tf_op jit(solution)/shard_map/ppermute | solution.py:22
  35.1 19.9 %all-to-all-start = ((f32[16,2,16,128]{3,2,1,0:T(8,128)}), f32[16,2,16,128]{3,2,1,0:T(8,128)S(1)}, u32[]{:S(2)}, u32[]{:S(2)}) async-start(f32[16,2,16,128]{3,2,1,0:T(8,128)} %broadcast_in_dim.8), calls=%async_computation | async-start | bytes 524288 | tf_op jit(solution)/shard_map/all_to_all | solution.py:50

commit v4 on v3

v4 whole, which is shorter than its diff:
```python
import jax
import jax.numpy as jnp
from jax import lax
from jax.experimental import pallas as pl
from jax.experimental.pallas import tpu as pltpu
from jax.sharding import PartitionSpec as P

COURANT = 0.5
DIFF_Y = 0.2
DIFF_Z = 0.25
NEW_TERM_COEF = 0.75
OLD_TERM_COEF = -5.0 / 12.0


def ring_pairs(count, step):
    return [(i, (i + step) % count) for i in range(count)]


def exchange_edges(first, last, axis):
    count = lax.axis_size(axis)
    from_prev = lax.ppermute(last, axis, ring_pairs(count, 1))
    from_next = lax.ppermute(first, axis, ring_pairs(count, -1))
    return from_prev, from_next


def spread_root(ratio):
    root = jnp.sqrt(1.0 + 4.0 * ratio)
    mu = (1.0 + root) / ((1.0 + 2.0 * ratio) + root)
    return jnp.log1p(-mu), root


def periodic_solve(source, ends, log_lam, root):
    levels, rows, cols = source.shape
    parts = lax.axis_size("gx")
    me = lax.axis_index("gx")
    log_lam = log_lam[:, None]
    gathered = lax.all_to_all(
        jnp.broadcast_to(ends[None], (parts,) + ends.shape), "gx", 0, 0, tiled=True
    )
    idx = jnp.arange(rows, dtype=jnp.float32)
    dist = jnp.abs(idx[:, None] - idx[None, :])
    kernel = jnp.exp(log_lam[:, :, None] * dist[None])
    local = lax.optimization_barrier(
        jnp.einsum("kij,kjc->kic", kernel, source, precision=lax.Precision.HIGHEST)
    )

    others = jnp.arange(parts)
    whole = -jnp.expm1(log_lam * (parts * rows))
    lag_f = ((me - others - 1) % parts).astype(jnp.float32) * rows
    lag_b = ((others - me - 1) % parts).astype(jnp.float32) * rows
    weight_f = jnp.exp(log_lam * lag_f[None, :]) / whole
    weight_b = jnp.exp(log_lam * lag_b[None, :]) / whole
    carry_f = jnp.sum(weight_f.T[:, :, None] * gathered[:, 0], axis=0)
    carry_b = jnp.sum(weight_b.T[:, :, None] * gathered[:, 1], axis=0)
    into_f = jnp.exp(log_lam * (idx + 1.0)[None, :])
    into_b = jnp.exp(log_lam * (rows - idx)[None, :])
    total = (
        local
        + into_f[:, :, None] * carry_f[:, None, :]
        + into_b[:, :, None] * carry_b[:, None, :]
    )
    return total / root[:, None, None]


def edge_kernel(t_ref, u_ref, v_ref, x_first_ref, x_last_ref, y_first_ref, y_last_ref):
    levels, rows, cols = t_ref.shape
    for k in range(levels):
        t = t_ref[k]
        u = u_ref[0, k]
        x_first_ref[k, 0:1, :] = t[0:1]
        x_first_ref[k, 1:2, :] = u[0:1]
        x_last_ref[k, 0:1, :] = t[rows - 1 : rows]
        x_last_ref[k, 1:2, :] = u[rows - 1 : rows]
        t_cols = t.T
        v_cols = v_ref[0, k].T
        y_first_ref[k, 0:1, :] = t_cols[0:1]
        y_first_ref[k, 1:2, :] = v_cols[0:1]
        y_last_ref[k, 0:1, :] = t_cols[cols - 1 : cols]
        y_last_ref[k, 1:2, :] = v_cols[cols - 1 : cols]


def stencil_kernel(
    inv_dz_ref, inv_between_ref, log_lam_ref, t_ref, u_ref, v_ref, w_ref, early_ref, wall_ref,
    x_prev_ref, x_next_ref, y_prev_ref, y_next_ref, rate_ref, source_ref, ends_ref,
):
    per_step = rate_ref.shape[0]
    levels, rows, cols = t_ref.shape
    top = levels - 1
    row = lax.broadcasted_iota(jnp.int32, (rows, cols), 0)
    col = lax.broadcasted_iota(jnp.int32, (rows, cols), 1)
    row_f = row.astype(jnp.float32)
    slot = lax.broadcasted_iota(jnp.int32, (8, rows), 0)
    for j in range(per_step):
        k = pl.program_id(0) * per_step + j
        below = jnp.maximum(k - 1, 0)
        above = jnp.minimum(k + 1, top)
        t = t_ref[k]
        u = u_ref[0, j]
        v = v_ref[0, j]
        w = w_ref[k]
        xp = x_prev_ref[j]
        xn = x_next_ref[j]
        yp = y_prev_ref[j]
        yn = y_next_ref[j]
        y_rows = jnp.where(
            slot == 0, yp[0:1],
            jnp.where(slot == 1, yp[1:2], jnp.where(slot == 2, yn[0:1], jnp.where(slot == 3, yn[1:2], 0.0))),
        )
        yh = y_rows.T

        def along_x(a, prev, nxt):
            a_next = jnp.where(row == rows - 1, nxt, pltpu.roll(a, rows - 1, 0))
            a_prev = jnp.where(row == 0, prev, pltpu.roll(a, 1, 0))
            return a_prev, a_next

        def along_y(a, prev, nxt):
            a_next = jnp.where(col == cols - 1, nxt, pltpu.roll(a, cols - 1, 1))
            a_prev = jnp.where(col == 0, prev, pltpu.roll(a, 1, 1))
            return a_prev, a_next

        t_xp, t_xn = along_x(t, xp[0:1], xn[0:1])
        u_xp, u_xn = along_x(u, xp[1:2], xn[1:2])
        t_yp, t_yn = along_y(t, yh[:, 0:1], yh[:, 2:3])
        v_yp, v_yn = along_y(v, yh[:, 1:2], yh[:, 3:4])
        flux_x_hi = (u + u_xn) * (t + t_xn) * 0.25
        flux_x_lo = (u_xp + u) * (t_xp + t) * 0.25
        flux_y_hi = (v + v_yn) * (t + t_yn) * 0.25
        flux_y_lo = (v_yp + v) * (t_yp + t) * 0.25
        advect_xy = (flux_x_hi - flux_x_lo) + (flux_y_hi - flux_y_lo)

        t_up = t_ref[above]
        t_dn = t_ref[below]
        flux_up = jnp.where(k == top, 0.0, (w + w_ref[above]) * (t + t_up) * 0.25)
        flux_dn = jnp.where(k == 0, 0.0, (w_ref[below] + w) * (t_dn + t) * 0.25)
        inv_dz = inv_dz_ref[k]
        carry_through_depth = (flux_up - flux_dn) * inv_dz
        ghost_up = jnp.where(k == top, wall_ref[1], t_up)
        ghost_dn = jnp.where(k == 0, wall_ref[0], t_dn)
        slope_up = (ghost_up - t) * inv_between_ref[k + 1]
        slope_dn = (t - ghost_dn) * inv_between_ref[k]
        thermal_spreading_step = (slope_up - slope_dn) * inv_dz
        stacked_layer_count = t_yn - 2.0 * t + t_yp
        rate = (
            -COURANT * (advect_xy + carry_through_depth)
            + DIFF_Y * stacked_layer_count
            + DIFF_Z * thermal_spreading_step
        )
        source = t + NEW_TERM_COEF * rate + OLD_TERM_COEF * early_ref[j]
        rate_ref[j] = rate
        source_ref[j] = source
        log_lam = log_lam_ref[k]
        to_end = jnp.sum(jnp.exp(log_lam * ((rows - 1.0) - row_f)) * source, axis=0, keepdims=True)
        from_start = jnp.sum(jnp.exp(log_lam * row_f) * source, axis=0, keepdims=True)
        ends_ref[j] = jnp.where(slot == 0, to_end, jnp.where(slot == 1, from_start, 0.0))


def on_device(
    initial_warmth_field,
    horizontal_motion_pair,
    z_directed_motion,
    earlier_rate_change,
    layer_depth_spacing,
    backward_spread_ratio,
    wall_warmth_bounds,
):
    t = initial_warmth_field
    levels, rows, cols = t.shape
    f32 = jnp.float32
    pair = lambda i: pl.BlockSpec((1, levels, rows, cols), lambda g: (i, 0, 0, 0))
    x_first, x_last, y_first, y_last = pl.pallas_call(
        edge_kernel,
        grid=(1,),
        in_specs=[pl.BlockSpec((levels, rows, cols), lambda g: (0, 0, 0)), pair(0), pair(1)],
        out_shape=[
            jax.ShapeDtypeStruct((levels, 2, cols), f32),
            jax.ShapeDtypeStruct((levels, 2, cols), f32),
            jax.ShapeDtypeStruct((levels, 2, rows), f32),
            jax.ShapeDtypeStruct((levels, 2, rows), f32),
        ],
    )(t, horizontal_motion_pair, horizontal_motion_pair)
    x_prev, x_next = exchange_edges(x_first, x_last, "gx")
    y_prev, y_next = exchange_edges(y_first, y_last, "gy")

    between = jnp.concatenate(
        [
            layer_depth_spacing[:1],
            0.5 * (layer_depth_spacing[:-1] + layer_depth_spacing[1:]),
            layer_depth_spacing[-1:],
        ],
        0,
    )
    log_lam, root = spread_root(backward_spread_ratio)
    per_step = 4 if levels % 4 == 0 else 1
    whole = lambda shape: pl.BlockSpec(shape, lambda g: (0,) * len(shape))
    level = lambda shape: pl.BlockSpec(shape, lambda g: (g,) + (0,) * (len(shape) - 1))
    smem = pl.BlockSpec(memory_space=pltpu.SMEM)
    current_rate_change, linear_system_source, ends = pl.pallas_call(
        stencil_kernel,
        grid=(levels // per_step,),
        in_specs=[
            smem,
            smem,
            smem,
            whole((levels, rows, cols)),
            pl.BlockSpec((1, per_step, rows, cols), lambda g: (0, g, 0, 0)),
            pl.BlockSpec((1, per_step, rows, cols), lambda g: (1, g, 0, 0)),
            whole((levels, rows, cols)),
            level((per_step, rows, cols)),
            whole((2, rows, cols)),
            level((per_step, 2, cols)),
            level((per_step, 2, cols)),
            level((per_step, 2, rows)),
            level((per_step, 2, rows)),
        ],
        out_specs=[
            level((per_step, rows, cols)),
            level((per_step, rows, cols)),
            level((per_step, 8, cols)),
        ],
        out_shape=[
            jax.ShapeDtypeStruct(t.shape, f32),
            jax.ShapeDtypeStruct(t.shape, f32),
            jax.ShapeDtypeStruct((levels, 8, cols), f32),
        ],
        cost_estimate=pl.CostEstimate(
            flops=100 * t.size, bytes_accessed=4 * 8 * t.size, transcendentals=2 * t.size
        ),
    )(
        1.0 / layer_depth_spacing, 1.0 / between, log_lam, t, horizontal_motion_pair,
        horizontal_motion_pair, z_directed_motion, earlier_rate_change, wall_warmth_bounds,
        x_prev, x_next, y_prev, y_next,
    )
    resulting_warmth_field = periodic_solve(
        linear_system_source, jnp.transpose(ends[:, 0:2], (1, 0, 2)), log_lam, root
    )
    return (resulting_warmth_field, current_rate_change)


def solution(mesh):
    in_specs = (
        P(None, "gx", "gy"),
        P(None, None, "gx", "gy"),
        P(None, "gx", "gy"),
        P(None, "gx", "gy"),
        P(),
        P(),
        P(None, "gx", "gy"),
    )
    out_specs = (P(None, "gx", "gy"), P(None, "gx", "gy"))
    return jax.shard_map(
        on_device, mesh=mesh, in_specs=in_specs, out_specs=out_specs, check_vma=False
    )
```

time: 57.6 us -> 46.3 us (0.80); the launches traced: 56.6 us -> 45.9 us
  local copies, waits for them, and re-layouts: 7.47 us -> 2.83 us
  waiting for transfers between devices: 8.89 us -> 5.88 us
  Pallas kernels: 12.9 us -> 10.7 us
  matrix products: 3.19 us -> 2.5 us
    slice x3 -> x0, local copies, waits for them, and re-layouts: 3.18 us -> none  [the longest x1 1.81 us: on_device(): v = horizontal_motion_pair[1]]
    all_to_all x1, waiting for transfers between devices: 8.88 us -> 5.87 us  [periodic_solve(): lax.all_to_all(jnp.broadcast_to(ends[None], (parts,) + ends.shape), 'gx',...]
    concatenate x2 -> x0, other arithmetic: 2.63 us -> none  [the longest x1 1.88 us: on_device(): jnp.concatenate([layer_depth_spacing[:1], 0.5 * (layer_depth_spacing[:-1]...]
    pallas_call x1 -> x2, Pallas kernels: 12.9 us -> 10.7 us  [the longest x1 7.6 us: on_device(): pl.pallas_call(stencil_kernel, grid=(levels // per_step,), in_specs=[smem...]
    div x0 -> x1, other arithmetic: none -> 2.05 us  [on_device(): 1.0 / between]
    unnamed x11 -> x14, local copies, waits for them, and re-layouts: 2.08 us -> 0.6 us
    transpose x2, local copies, waits for them, and re-layouts: 0.01 us -> 0.85 us  [on_device(): jnp.transpose(ends[:, 0:2], (1, 0, 2))]
    another operation x1 -> x0, local copies, waits for them, and re-layouts: 0.73 us -> none  [on_device(): jnp.stack([t[:, :, -1], v[:, :, -1]], 1)]
  transfers between devices with their start and end apart: 5 -> 5, of which waited for: 1 -> 1; matrix products, arithmetic and copies ran while one was open for 13% -> 14% of each run, Pallas kernels for 0% -> 0%
where the time goes in v4:
time: 46.3 us; the launch traced here: 45.9 us
  starting transfers between devices  18.2 us (39%)
  Pallas kernels  10.7 us (23%)
  waiting for transfers between devices  5.88 us (13%)
  other arithmetic  5.11 us (11%)
  local copies, waits for them, and re-layouts  2.83 us (6%)
  matrix products  2.5 us (5%)
  between operations  0.74 us (2%)
    all_to_all x1, starting transfers between devices, periodic_solve(): lax.all_to_all(jnp.broadcast_to(ends[None], (parts,) + ends.shape), 'gx',...  10.8 us
    pallas_call x1, Pallas kernels, on_device(): pl.pallas_call(stencil_kernel, grid=(levels // per_step,), in_specs=[smem...  7.6 us
    all_to_all x1, waiting for transfers between devices, periodic_solve(): lax.all_to_all(jnp.broadcast_to(ends[None], (parts,) + ends.shape), 'gx',...  5.87 us
    ppermute x2, starting transfers between devices, exchange_edges(): from_next = lax.ppermute(first, axis, ring_pairs(count, -1))  5.47 us
    pallas_call x1, Pallas kernels, on_device(): pl.pallas_call(edge_kernel, grid=(1,), in_specs=[pl.BlockSpec((levels, ro...  3.08 us
    dot_general x1, matrix products, periodic_solve(): jnp.einsum('kij,kjc->kic', kernel, source, precision=lax.Precision.HIGHEST)  2.5 us
    div x1, other arithmetic, on_device(): 1.0 / between  2.05 us
    ppermute x2, starting transfers between devices, exchange_edges(): from_prev = lax.ppermute(last, axis, ring_pairs(count, 1))  1.92 us
  transfers between devices with their start and end apart: 5, of which 1 were waited for; matrix products, arithmetic and copies ran while one was open for 14% of the time, Pallas kernels for 0%

profile of v4, /device:TPU:32, one launch (start us, length us, event | category | flops | bytes accessed | tf_op | source)
XLA Modules:
  0.0 45.9 jit_solution(9104438638122866407)
XLA Ops:
  0.6 0.0 copy-start.5
  0.6 0.0 copy-start.6
  0.6 3.1 %shard_map.86 = (f32[16,2,128]{2,1,0:T(2,128)}, f32[16,2,128]{2,1,0:T(2,128)}, f32[16,2,128]{2,1,0:T(2,128)}, f32[16,2,128]{2,1,0:T(2,128)}) custom-call(f32[16,128,128]{2,1,0:T(8,128)} %t_ref.3, f32[2,16,128,128]{3,2,1,0:T(8,128)} %v_ref.3, f32[2,16,128,128]{3,2,1,0:T(8,128)} %v_ref.3), custom_call_target="tpu_custom_call" | custom-call | tf_op jit(solution)/shard_map/pallas_call | solution.py:170
  3.7 1.9 %collective-permute-start = (f32[16,2,128]{2,1,0:T(2,128)}, f32[16,2,128]{2,1,0:T(2,128)S(1)}, u32[]{:S(2)}, u32[]{:S(2)}) collective-permute-start(f32[16,2,128]{2,1,0:T(2,128)} %get-tuple-element.9), channel_id=1, source_target_pairs={{0,16},{16,32},{32,48},{48,64},{64,80},{80,96},{96,112},{112,128},... | collective-permute-start | bytes 49160 | tf_op jit(solution)/shard_map/ppermute | solution.py:21
  5.6 0.1 collective-permute-start.1
  5.8 0.0 collective-permute-start.2
  5.8 5.4 %collective-permute-start.3 = (f32[16,2,128]{2,1,0:T(2,128)}, f32[16,2,128]{2,1,0:T(2,128)S(1)}, u32[]{:S(2)}, u32[]{:S(2)}) collective-permute-start(f32[16,2,128]{2,1,0:T(2,128)} %get-tuple-element.12), channel_id=1, source_target_pairs={{0,15},{1,0},{2,1},{3,2},{4,3},{5,4},{6,5},{7,6},{8,7},{9,8},{10,9... | collective-permute-start | bytes 49160 | tf_op jit(solution)/shard_map/ppermute | solution.py:22
  11.1 0.0 copy-done.5
  11.1 0.7 %fusion.15 = (f32[1]{0:T(128)}, f32[1]{0:T(128)}) fusion(f32[16]{0:T(128)S(1)} %copy-done.5), kind=kLoop, calls=%fused_computation.39 | loop fusion | bytes 16 | tf_op jit(solution)/shard_map/slice | solution.py:186
  11.8 0.1 add_multiply_fusion
  11.9 0.0 copy-done.6
  11.9 0.5 %exponential-minus-one_negate_fusion = (f32[16]{0:T(128)S(1)}, f32[16]{0:T(128)S(1)}, f32[16]{0:T(128)S(1)}, f32[16]{0:T(128)}) fusion(f32[16]{0:T(128)S(1)} %copy-done.6, f32[16]{0:T(128)S(1)} %copy-done.5), kind=kLoop, calls=%fused_computation.32 | loop fusion | flops 176 | bytes 384 | tf_op jit(solution)/shard_map/neg | solution.py:48
  12.4 0.0 copy-start.4
  12.4 0.1 exponential_divide_fusion
  12.5 2.1 %maximum_divide_fusion.inv_between_ref = f32[17]{0:T(128)} fusion(f32[1]{0:T(128)} %get-tuple-element.26, f32[15]{0:T(128)S(1)} %add_multiply_fusion, f32[1]{0:T(128)} %get-tuple-element.25), kind=kLoop, calls=%fused_computation.30 | loop fusion | flops 51 | bytes 136 | tf_op jit(solution)/shard_map/div | solution.py:229
  14.6 0.0 collective-permute-done.x_prev_ref
  14.6 0.0 copy-start
  14.6 0.0 collective-permute-done.1.x_next_ref
  14.6 0.0 copy-start.1
  14.6 0.0 collective-permute-done.2.y_prev_ref
  14.6 0.0 copy-start.2
  14.6 0.0 collective-permute-done.3.y_next_ref
  14.6 0.0 copy-start.3
  14.6 0.0 copy-done.4
  14.7 0.5 %copy-done = f32[16,2,128]{2,1,0:T(2,128)} copy-done((f32[16,2,128]{2,1,0:T(2,128)}, f32[16,2,128]{2,1,0:T(2,128)S(1)}, u32[]{:S(2)}) %copy-start) | copy-done | bytes 16408
  15.2 0.0 copy-done.1
  15.2 0.0 copy-done.2
  15.2 0.0 copy-done.3
  15.2 7.6 %shard_map.87 = (f32[16,128,128]{2,1,0:T(8,128)}, f32[16,128,128]{2,1,0:T(8,128)}, f32[16,8,128]{2,1,0:T(8,128)}) custom-call(f32[16]{0:T(128)} %get-tuple-element.27.inv_dz_ref, f32[17]{0:T(128)} %maximum_divide_fusion.inv_between_ref, f32[16]{0:T(128)} %copy-done.4, f32[16,128,128]{2,1,0:T(8,128)} %t_ref.3, f32[2,16,128,128]{3,2,1,0:T(8,128)} %v_ref.3, ...), custom_call_target="tpu_custom_call" | custom-call | flops 26214400 | bytes 8388608 | tf_op jit(solution)/shard_map/pallas_call | solution.py:197
  22.8 0.8 %slice_bitcast_fusion.2 = f32[2,16,128]{2,0,1:T(2,128)S(1)} fusion(f32[16,8,128]{2,1,0:T(8,128)} %get-tuple-element.14), kind=kLoop, calls=%fused_computation.13 | loop fusion | bytes 32768 | tf_op jit(solution)/shard_map/transpose | solution.py:234
  23.7 0.7 %broadcast_in_dim.2 = f32[16,2,16,128]{3,2,1,0:T(8,128)} broadcast(f32[2,16,128]{2,1,0:T(8,128)S(1)} %copy.10), dimensions={1,2,3} | broadcast | bytes 278528 | tf_op jit(solution)/shard_map/broadcast_in_dim | solution.py:38
  24.4 10.8 %all-to-all-start = ((f32[16,2,16,128]{3,2,1,0:T(8,128)}), f32[16,2,16,128]{3,2,1,0:T(8,128)S(1)}, u32[]{:S(2)}, u32[]{:S(2)}) async-start(f32[16,2,16,128]{3,2,1,0:T(8,128)} %broadcast_in_dim.2), calls=%async_computation | async-start | bytes 524288 | tf_op jit(solution)/shard_map/all_to_all | solution.py:37
  35.2 0.7 %multiply_exponential_fusion.1 = (f32[16,128]{1,0:T(8,128)S(1)}, f32[16,128]{1,0:T(8,128)S(1)}) fusion(f32[128]{0:T(128)S(1)} %get-tuple-element.31, f32[16]{0:T(128)} %copy-done.4, f32[128]{0:T(128)S(1)} %get-tuple-element.30), kind=kLoop, calls=%fused_computation.17 | loop fusion | flops 4096 | bytes 17472 | tf_op jit(solution)/shard_map/exp | solution.py:55
  35.9 2.5 %fusion = f32[16,128,128]{2,1,0:T(8,128)S(1)} fusion(f32[16,128,128]{2,1,0:T(8,128)} %get-tuple-element.13, f32[128,128]{1,0:T(8,128)S(1)} %subtract_abs_fusion, f32[16]{0:T(128)} %copy-done.4), kind=kOutput, calls=%fused_computation.1 | convolution fusion | flops 402915328 | bytes 2162752 | tf_op jit(solution)/shard_map/kij,kjc->kic/dot_general | solution.py:44
  38.4 5.9 %all-to-all-done = f32[16,2,16,128]{3,2,1,0:T(8,128)S(1)} async-done(((f32[16,2,16,128]{3,2,1,0:T(8,128)}), f32[16,2,16,128]{3,2,1,0:T(8,128)S(1)}, u32[]{:S(2)}, u32[]{:S(2)}) %all-to-all-start) | async-done | bytes 262176 | tf_op jit(solution)/shard_map/all_to_all | solution.py:37
  44.3 0.1 fusion.8
  44.4 1.5 %add_divide_fusion = f32[16,128,128]{2,1,0:T(8,128)} fusion(f32[16,128,128]{2,1,0:T(8,128)S(1)} %fusion, f32[16]{0:T(128)S(1)} %get-tuple-element.24, f32[16,128]{1,0:T(8,128)S(1)} %get-tuple-element.17, f32[16,128]{1,0:T(8,128)S(1)} %get-tuple-element.23, f32[16,128]{1,0:T(8,128)S(1)} %get-tuple-element.16, f32[16,128]{1,0:T(8,128)S(1)} %get-tuple-element.22), kind=kLoop, calls=%fused_computation | loop fusion | flops 1310720 | bytes 2129984 | tf_op jit(solution)/shard_map/div | solution.py:62
  (4 shorter events, 0.1 us)
Async XLA Ops:
  0.6 10.5 %copy-start.5 = (f32[16]{0:T(128)S(1)}, f32[16]{0:T(128)}, u32[]{:S(2)}) copy-start(f32[16]{0:T(128)} %param.11) | copy-start | bytes 196
  0.6 11.3 %copy-start.6 = (f32[16]{0:T(128)S(1)}, f32[16]{0:T(128)}, u32[]{:S(2)}) copy-start(f32[16]{0:T(128)} %param.12) | copy-start | bytes 196
  3.7 10.9 %collective-permute-start = (f32[16,2,128]{2,1,0:T(2,128)}, f32[16,2,128]{2,1,0:T(2,128)S(1)}, u32[]{:S(2)}, u32[]{:S(2)}) collective-permute-start(f32[16,2,128]{2,1,0:T(2,128)} %get-tuple-element.9), channel_id=1, source_target_pairs={{0,16},{16,32},{32,48},{48,64},{64,80},{80,96},{96,112},{112,128},... | collective-permute-start | bytes 49160 | tf_op jit(solution)/shard_map/ppermute | solution.py:21
  5.6 8.9 %collective-permute-start.1 = (f32[16,2,128]{2,1,0:T(2,128)}, f32[16,2,128]{2,1,0:T(2,128)S(1)}, u32[]{:S(2)}, u32[]{:S(2)}) collective-permute-start(f32[16,2,128]{2,1,0:T(2,128)} %get-tuple-element.10), channel_id=1, source_target_pairs={{0,240},{16,0},{32,16},{48,32},{64,48},{80,64},{96,80},{112,96},{1... | collective-permute-start | bytes 49160 | tf_op jit(solution)/shard_map/ppermute | solution.py:22
  5.8 8.9 %collective-permute-start.2 = (f32[16,2,128]{2,1,0:T(2,128)}, f32[16,2,128]{2,1,0:T(2,128)S(1)}, u32[]{:S(2)}, u32[]{:S(2)}) collective-permute-start(f32[16,2,128]{2,1,0:T(2,128)} %get-tuple-element.11), channel_id=1, source_target_pairs={{0,1},{1,2},{2,3},{3,4},{4,5},{5,6},{6,7},{7,8},{8,9},{9,10},{10,1... | collective-permute-start | bytes 49160 | tf_op jit(solution)/shard_map/ppermute | solution.py:21
  5.8 8.9 %collective-permute-start.3 = (f32[16,2,128]{2,1,0:T(2,128)}, f32[16,2,128]{2,1,0:T(2,128)S(1)}, u32[]{:S(2)}, u32[]{:S(2)}) collective-permute-start(f32[16,2,128]{2,1,0:T(2,128)} %get-tuple-element.12), channel_id=1, source_target_pairs={{0,15},{1,0},{2,1},{3,2},{4,3},{5,4},{6,5},{7,6},{8,7},{9,8},{10,9... | collective-permute-start | bytes 49160 | tf_op jit(solution)/shard_map/ppermute | solution.py:22
  12.4 2.2 %copy-start.4 = (f32[16]{0:T(128)}, f32[16]{0:T(128)S(1)}, u32[]{:S(2)}) copy-start(f32[16]{0:T(128)S(1)} %get-tuple-element.19.log_lam_ref) | copy-start | bytes 196
  14.6 0.6 %copy-start = (f32[16,2,128]{2,1,0:T(2,128)}, f32[16,2,128]{2,1,0:T(2,128)S(1)}, u32[]{:S(2)}) copy-start(f32[16,2,128]{2,1,0:T(2,128)S(1)} %collective-permute-done.x_prev_ref) | copy-start | bytes 49156
  14.6 0.6 %copy-start.1 = (f32[16,2,128]{2,1,0:T(2,128)}, f32[16,2,128]{2,1,0:T(2,128)S(1)}, u32[]{:S(2)}) copy-start(f32[16,2,128]{2,1,0:T(2,128)S(1)} %collective-permute-done.1.x_next_ref) | copy-start | bytes 49156
  14.6 0.6 %copy-start.2 = (f32[16,2,128]{2,1,0:T(2,128)}, f32[16,2,128]{2,1,0:T(2,128)S(1)}, u32[]{:S(2)}) copy-start(f32[16,2,128]{2,1,0:T(2,128)S(1)} %collective-permute-done.2.y_prev_ref) | copy-start | bytes 49156
  14.6 0.6 %copy-start.3 = (f32[16,2,128]{2,1,0:T(2,128)}, f32[16,2,128]{2,1,0:T(2,128)S(1)}, u32[]{:S(2)}) copy-start(f32[16,2,128]{2,1,0:T(2,128)S(1)} %collective-permute-done.3.y_next_ref) | copy-start | bytes 49156
  24.4 19.9 %all-to-all-start = ((f32[16,2,16,128]{3,2,1,0:T(8,128)}), f32[16,2,16,128]{3,2,1,0:T(8,128)S(1)}, u32[]{:S(2)}, u32[]{:S(2)}) async-start(f32[16,2,16,128]{3,2,1,0:T(8,128)} %broadcast_in_dim.2), calls=%async_computation | async-start | bytes 524288 | tf_op jit(solution)/shard_map/all_to_all | solution.py:37

commit v5 on v4

--- a/solution.py
+++ b/solution.py
@@ -34,9 +34,7 @@
     parts = lax.axis_size("gx")
     me = lax.axis_index("gx")
     log_lam = log_lam[:, None]
-    gathered = lax.all_to_all(
-        jnp.broadcast_to(ends[None], (parts,) + ends.shape), "gx", 0, 0, tiled=True
-    )
+    gathered = lax.all_to_all(ends, "gx", 0, 0, tiled=True)
     idx = jnp.arange(rows, dtype=jnp.float32)
     dist = jnp.abs(idx[:, None] - idx[None, :])
     kernel = jnp.exp(log_lam[:, :, None] * dist[None])
@@ -50,8 +48,8 @@
     lag_b = ((others - me - 1) % parts).astype(jnp.float32) * rows
     weight_f = jnp.exp(log_lam * lag_f[None, :]) / whole
     weight_b = jnp.exp(log_lam * lag_b[None, :]) / whole
-    carry_f = jnp.sum(weight_f.T[:, :, None] * gathered[:, 0], axis=0)
-    carry_b = jnp.sum(weight_b.T[:, :, None] * gathered[:, 1], axis=0)
+    carry_f = jnp.sum(weight_f.T[:, :, None] * gathered[:, :, 0], axis=0)
+    carry_b = jnp.sum(weight_b.T[:, :, None] * gathered[:, :, 1], axis=0)
     into_f = jnp.exp(log_lam * (idx + 1.0)[None, :])
     into_b = jnp.exp(log_lam * (rows - idx)[None, :])
     total = (
@@ -62,25 +60,25 @@
     return total / root[:, None, None]
 
 
-def edge_kernel(t_ref, u_ref, v_ref, x_first_ref, x_last_ref, y_first_ref, y_last_ref):
-    levels, rows, cols = t_ref.shape
-    for k in range(levels):
-        t = t_ref[k]
-        u = u_ref[0, k]
-        x_first_ref[k, 0:1, :] = t[0:1]
-        x_first_ref[k, 1:2, :] = u[0:1]
-        x_last_ref[k, 0:1, :] = t[rows - 1 : rows]
-        x_last_ref[k, 1:2, :] = u[rows - 1 : rows]
+def edge_kernel(t_ref, u_lo_ref, u_hi_ref, v_ref, x_first_ref, x_last_ref, y_first_ref, y_last_ref):
+    per_step, rows, cols = t_ref.shape
+    tile = u_lo_ref.shape[2]
+    for j in range(per_step):
+        t = t_ref[j]
+        x_first_ref[j, 0:1, :] = t[0:1]
+        x_first_ref[j, 1:2, :] = u_lo_ref[0, j, 0:1, :]
+        x_last_ref[j, 0:1, :] = t[rows - 1 : rows]
+        x_last_ref[j, 1:2, :] = u_hi_ref[0, j, tile - 1 : tile, :]
         t_cols = t.T
-        v_cols = v_ref[0, k].T
-        y_first_ref[k, 0:1, :] = t_cols[0:1]
-        y_first_ref[k, 1:2, :] = v_cols[0:1]
-        y_last_ref[k, 0:1, :] = t_cols[cols - 1 : cols]
-        y_last_ref[k, 1:2, :] = v_cols[cols - 1 : cols]
+        v_cols = v_ref[0, j].T
+        y_first_ref[j, 0:1, :] = t_cols[0:1]
+        y_first_ref[j, 1:2, :] = v_cols[0:1]
+        y_last_ref[j, 0:1, :] = t_cols[cols - 1 : cols]
+        y_last_ref[j, 1:2, :] = v_cols[cols - 1 : cols]
 
 
 def stencil_kernel(
-    inv_dz_ref, inv_between_ref, log_lam_ref, t_ref, u_ref, v_ref, w_ref, early_ref, wall_ref,
+    inverse_ref, log_lam_ref, t_ref, u_ref, v_ref, w_ref, early_ref, wall_ref,
     x_prev_ref, x_next_ref, y_prev_ref, y_next_ref, rate_ref, source_ref, ends_ref,
 ):
     per_step = rate_ref.shape[0]
@@ -132,12 +130,12 @@
         t_dn = t_ref[below]
         flux_up = jnp.where(k == top, 0.0, (w + w_ref[above]) * (t + t_up) * 0.25)
         flux_dn = jnp.where(k == 0, 0.0, (w_ref[below] + w) * (t_dn + t) * 0.25)
-        inv_dz = inv_dz_ref[k]
+        inv_dz = inverse_ref[k]
         carry_through_depth = (flux_up - flux_dn) * inv_dz
         ghost_up = jnp.where(k == top, wall_ref[1], t_up)
         ghost_dn = jnp.where(k == 0, wall_ref[0], t_dn)
-        slope_up = (ghost_up - t) * inv_between_ref[k + 1]
-        slope_dn = (t - ghost_dn) * inv_between_ref[k]
+        slope_up = (ghost_up - t) * inverse_ref[levels + k + 1]
+        slope_dn = (t - ghost_dn) * inverse_ref[levels + k]
         thermal_spreading_step = (slope_up - slope_dn) * inv_dz
         stacked_layer_count = t_yn - 2.0 * t + t_yp
         rate = (
@@ -151,7 +149,9 @@
         log_lam = log_lam_ref[k]
         to_end = jnp.sum(jnp.exp(log_lam * ((rows - 1.0) - row_f)) * source, axis=0, keepdims=True)
         from_start = jnp.sum(jnp.exp(log_lam * row_f) * source, axis=0, keepdims=True)
-        ends_ref[j] = jnp.where(slot == 0, to_end, jnp.where(slot == 1, from_start, 0.0))
+        copies = ends_ref.shape[0]
+        ends_ref[:, j, 0:1, :] = jnp.broadcast_to(to_end[None], (copies, 1, cols))
+        ends_ref[:, j, 1:2, :] = jnp.broadcast_to(from_start[None], (copies, 1, cols))
 
 
 def on_device(
@@ -166,18 +166,26 @@
     t = initial_warmth_field
     levels, rows, cols = t.shape
     f32 = jnp.float32
-    pair = lambda i: pl.BlockSpec((1, levels, rows, cols), lambda g: (i, 0, 0, 0))
+    per_step = 4 if levels % 4 == 0 else 1
+    tile = 8
+    level = lambda shape: pl.BlockSpec(shape, lambda g: (g,) + (0,) * (len(shape) - 1))
     x_first, x_last, y_first, y_last = pl.pallas_call(
         edge_kernel,
-        grid=(1,),
-        in_specs=[pl.BlockSpec((levels, rows, cols), lambda g: (0, 0, 0)), pair(0), pair(1)],
+        grid=(levels // per_step,),
+        in_specs=[
+            level((per_step, rows, cols)),
+            pl.BlockSpec((1, per_step, tile, cols), lambda g: (0, g, 0, 0)),
+            pl.BlockSpec((1, per_step, tile, cols), lambda g: (0, g, rows // tile - 1, 0)),
+            pl.BlockSpec((1, per_step, rows, cols), lambda g: (1, g, 0, 0)),
+        ],
+        out_specs=[level((per_step, 2, cols))] * 2 + [level((per_step, 2, rows))] * 2,
         out_shape=[
             jax.ShapeDtypeStruct((levels, 2, cols), f32),
             jax.ShapeDtypeStruct((levels, 2, cols), f32),
             jax.ShapeDtypeStruct((levels, 2, rows), f32),
             jax.ShapeDtypeStruct((levels, 2, rows), f32),
         ],
-    )(t, horizontal_motion_pair, horizontal_motion_pair)
+    )(t, horizontal_motion_pair, horizontal_motion_pair, horizontal_motion_pair)
     x_prev, x_next = exchange_edges(x_first, x_last, "gx")
     y_prev, y_next = exchange_edges(y_first, y_last, "gy")
 
@@ -190,9 +198,9 @@
         0,
     )
     log_lam, root = spread_root(backward_spread_ratio)
-    per_step = 4 if levels % 4 == 0 else 1
+    inverse = 1.0 / jnp.concatenate([layer_depth_spacing, between])
     whole = lambda shape: pl.BlockSpec(shape, lambda g: (0,) * len(shape))
-    level = lambda shape: pl.BlockSpec(shape, lambda g: (g,) + (0,) * (len(shape) - 1))
+    parts = lax.axis_size("gx")
     smem = pl.BlockSpec(memory_space=pltpu.SMEM)
     current_rate_change, linear_system_source, ends = pl.pallas_call(
         stencil_kernel,
@@ -200,7 +208,6 @@
         in_specs=[
             smem,
             smem,
-            smem,
             whole((levels, rows, cols)),
             pl.BlockSpec((1, per_step, rows, cols), lambda g: (0, g, 0, 0)),
             pl.BlockSpec((1, per_step, rows, cols), lambda g: (1, g, 0, 0)),
@@ -215,24 +222,22 @@
         out_specs=[
             level((per_step, rows, cols)),
             level((per_step, rows, cols)),
-            level((per_step, 8, cols)),
+            pl.BlockSpec((parts, per_step, 2, cols), lambda g: (0, g, 0, 0)),
         ],
         out_shape=[
             jax.ShapeDtypeStruct(t.shape, f32),
             jax.ShapeDtypeStruct(t.shape, f32),
-            jax.ShapeDtypeStruct((levels, 8, cols), f32),
+            jax.ShapeDtypeStruct((parts, levels, 2, cols), f32),
         ],
         cost_estimate=pl.CostEstimate(
             flops=100 * t.size, bytes_accessed=4 * 8 * t.size, transcendentals=2 * t.size
         ),
     )(
-        1.0 / layer_depth_spacing, 1.0 / between, log_lam, t, horizontal_motion_pair,
+        inverse, log_lam, t, horizontal_motion_pair,
         horizontal_motion_pair, z_directed_motion, earlier_rate_change, wall_warmth_bounds,
         x_prev, x_next, y_prev, y_next,
     )
-    resulting_warmth_field = periodic_solve(
-        linear_system_source, jnp.transpose(ends[:, 0:2], (1, 0, 2)), log_lam, root
-    )
+    resulting_warmth_field = periodic_solve(linear_system_source, ends, log_lam, root)
     return (resulting_warmth_field, current_rate_change)
 
 

time: 46.3 us -> 45.9 us (level)
  local copies, waits for them, and re-layouts: 2.83 us -> 2.04 us
  Pallas kernels: 10.7 us -> 11.4 us
    transpose x2 -> x0, local copies, waits for them, and re-layouts: 0.85 us -> none  [on_device(): jnp.transpose(ends[:, 0:2], (1, 0, 2))]
    broadcast_in_dim x1 -> x0, local copies, waits for them, and re-layouts: 0.72 us -> none  [periodic_solve(): jnp.broadcast_to(ends[None], (parts,) + ends.shape)]
    pallas_call x1, Pallas kernels: 3.08 us -> 3.77 us  [on_device(): pl.pallas_call(edge_kernel, grid=(levels // per_step,), in_specs=[level((...]
    unnamed x14, local copies, waits for them, and re-layouts: 0.6 us -> 1.18 us
    neg x1, other arithmetic: 0.53 us -> 0.02 us  [periodic_solve(): whole = -jnp.expm1(log_lam * (parts * rows))]
where the time goes in v5:
time: 45.9 us; the launch traced here: 45.5 us
  starting transfers between devices  18.2 us (40%)
  Pallas kernels  11.4 us (25%)
  waiting for transfers between devices  5.81 us (13%)
  other arithmetic  4.72 us (10%)
  matrix products  2.5 us (5%)
  local copies, waits for them, and re-layouts  2.04 us (4%)
  between operations  0.77 us (2%)
    all_to_all x1, starting transfers between devices, periodic_solve(): gathered = lax.all_to_all(ends, 'gx', 0, 0, tiled=True)  10.8 us
    pallas_call x1, Pallas kernels, on_device(): pl.pallas_call(stencil_kernel, grid=(levels // per_step,), in_specs=[smem...  7.67 us
    all_to_all x1, waiting for transfers between devices, periodic_solve(): gathered = lax.all_to_all(ends, 'gx', 0, 0, tiled=True)  5.8 us
    ppermute x2, starting transfers between devices, exchange_edges(): from_next = lax.ppermute(first, axis, ring_pairs(count, -1))  5.46 us
    pallas_call x1, Pallas kernels, on_device(): pl.pallas_call(edge_kernel, grid=(levels // per_step,), in_specs=[level((...  3.77 us
    dot_general x1, matrix products, periodic_solve(): jnp.einsum('kij,kjc->kic', kernel, source, precision=lax.Precision.HIGHEST)  2.5 us
    div x1, other arithmetic, on_device(): inverse = 1.0 / jnp.concatenate([layer_depth_spacing, between])  2.04 us
    ppermute x2, starting transfers between devices, exchange_edges(): from_prev = lax.ppermute(last, axis, ring_pairs(count, 1))  1.93 us
  transfers between devices with their start and end apart: 5, of which 1 were waited for; matrix products, arithmetic and copies ran while one was open for 14% of the time, Pallas kernels for 0%

profile of v5, /device:TPU:32, one launch (start us, length us, event | category | flops | bytes accessed | tf_op | source)
XLA Modules:
  0.0 45.5 jit_solution(3996792454142834241)
XLA Ops:
  0.6 0.0 copy-start.5
  0.6 0.0 copy-start.6
  0.6 3.8 %shard_map.86 = (f32[16,2,128]{2,1,0:T(2,128)}, f32[16,2,128]{2,1,0:T(2,128)}, f32[16,2,128]{2,1,0:T(2,128)}, f32[16,2,128]{2,1,0:T(2,128)}) custom-call(f32[16,128,128]{2,1,0:T(8,128)} %t_ref.3, f32[2,16,128,128]{3,2,1,0:T(8,128)} %v_ref.3, f32[2,16,128,128]{3,2,1,0:T(8,128)} %v_ref.3, f32[2,16,128,128]{3,2,1,0:T(8,128)} %v_ref.3), custom_call_target="tpu_custom_call" | custom-call | tf_op jit(solution)/shard_map/pallas_call | solution.py:172
  4.4 1.9 %collective-permute-start = (f32[16,2,128]{2,1,0:T(2,128)}, f32[16,2,128]{2,1,0:T(2,128)S(1)}, u32[]{:S(2)}, u32[]{:S(2)}) collective-permute-start(f32[16,2,128]{2,1,0:T(2,128)} %get-tuple-element.9), channel_id=1, source_target_pairs={{0,16},{16,32},{32,48},{48,64},{64,80},{80,96},{96,112},{112,128},... | collective-permute-start | bytes 49160 | tf_op jit(solution)/shard_map/ppermute | solution.py:21
  6.4 0.1 collective-permute-start.1
  6.5 0.0 collective-permute-start.2
  6.5 5.4 %collective-permute-start.3 = (f32[16,2,128]{2,1,0:T(2,128)}, f32[16,2,128]{2,1,0:T(2,128)S(1)}, u32[]{:S(2)}, u32[]{:S(2)}) collective-permute-start(f32[16,2,128]{2,1,0:T(2,128)} %get-tuple-element.12), channel_id=1, source_target_pairs={{0,15},{1,0},{2,1},{3,2},{4,3},{5,4},{6,5},{7,6},{8,7},{9,8},{10,9... | collective-permute-start | bytes 49160 | tf_op jit(solution)/shard_map/ppermute | solution.py:22
  11.8 0.0 copy-done.5
  11.8 0.7 %fusion.12 = (f32[1]{0:T(128)}, f32[1]{0:T(128)}) fusion(f32[16]{0:T(128)S(1)} %copy-done.5), kind=kLoop, calls=%fused_computation.34 | loop fusion | bytes 16 | tf_op jit(solution)/shard_map/slice | solution.py:194
  12.5 0.1 add_multiply_fusion
  12.6 0.0 copy-done.6
  12.6 0.0 copy-start.4
  12.7 0.1 exponential_divide_fusion.1
  12.8 2.0 %maximum_divide_fusion.inverse_ref = f32[33]{0:T(128)} fusion(f32[1]{0:T(128)} %get-tuple-element.26, f32[15]{0:T(128)S(1)} %add_multiply_fusion, f32[1]{0:T(128)} %get-tuple-element.25, f32[16]{0:T(128)S(1)} %copy-done.5), kind=kLoop, calls=%fused_computation.25 | loop fusion | flops 132 | bytes 264 | tf_op jit(solution)/shard_map/div | solution.py:201
  14.8 0.0 collective-permute-done.x_prev_ref
  14.8 0.0 copy-start
  14.8 0.0 collective-permute-done.1.x_next_ref
  14.8 0.0 copy-start.1
  14.8 0.0 collective-permute-done.2.y_prev_ref
  14.8 0.0 copy-start.2
  14.8 0.0 collective-permute-done.3.y_next_ref
  14.8 0.0 copy-done.4
  14.9 0.5 %copy-done = f32[16,2,128]{2,1,0:T(2,128)} copy-done((f32[16,2,128]{2,1,0:T(2,128)}, f32[16,2,128]{2,1,0:T(2,128)S(1)}, u32[]{:S(2)}) %copy-start) | copy-done | bytes 16408
  15.4 0.0 copy-done.1
  15.4 0.0 copy-done.2
  15.4 0.0 copy-start.3
  15.4 0.6 %copy-done.3 = f32[16,2,128]{2,1,0:T(2,128)} copy-done((f32[16,2,128]{2,1,0:T(2,128)}, f32[16,2,128]{2,1,0:T(2,128)S(1)}, u32[]{:S(2)}) %copy-start.3) | copy-done | bytes 16408
  16.0 7.7 %shard_map.87 = (f32[16,128,128]{2,1,0:T(8,128)}, f32[16,128,128]{2,1,0:T(8,128)}, f32[16,16,2,128]{3,2,1,0:T(2,128)}) custom-call(f32[33]{0:T(128)} %maximum_divide_fusion.inverse_ref, f32[16]{0:T(128)} %copy-done.4, f32[16,128,128]{2,1,0:T(8,128)} %t_ref.3, f32[2,16,128,128]{3,2,1,0:T(8,128)} %v_ref.3, f32[2,16,128,128]{3,2,1,0:T(8,128)} %v_ref.3, ...), custom_call_target="tpu_custom_call" | custom-call | flops 26214400 | bytes 8388608 | tf_op jit(solution)/shard_map/pallas_call | solution.py:205
  23.7 10.8 %all-to-all-start = ((f32[16,16,2,128]{3,2,1,0:T(2,128)}), f32[16,16,2,128]{3,2,1,0:T(2,128)S(1)}, u32[]{:S(2)}, u32[]{:S(2)}) async-start(f32[16,16,2,128]{3,2,1,0:T(2,128)} %get-tuple-element.14), calls=%async_computation | async-start | bytes 524288 | tf_op jit(solution)/shard_map/all_to_all | solution.py:37
  34.5 0.7 %multiply_exponential_fusion.1 = (f32[16,128]{1,0:T(8,128)S(1)}, f32[16,128]{1,0:T(8,128)S(1)}) fusion(f32[128]{0:T(128)S(1)} %get-tuple-element.30, f32[16]{0:T(128)} %copy-done.4, f32[128]{0:T(128)S(1)} %get-tuple-element.29), kind=kLoop, calls=%fused_computation.12 | loop fusion | flops 4096 | bytes 17472 | tf_op jit(solution)/shard_map/exp | solution.py:53
  35.3 2.5 %fusion = f32[16,128,128]{2,1,0:T(8,128)S(1)} fusion(f32[16,128,128]{2,1,0:T(8,128)} %get-tuple-element.13, f32[128,128]{1,0:T(8,128)S(1)} %subtract_abs_fusion, f32[16]{0:T(128)} %copy-done.4), kind=kOutput, calls=%fused_computation.1 | convolution fusion | flops 402915328 | bytes 2162752 | tf_op jit(solution)/shard_map/kij,kjc->kic/dot_general | solution.py:42
  37.8 5.8 %all-to-all-done = f32[16,16,2,128]{3,2,1,0:T(2,128)S(1)} async-done(((f32[16,16,2,128]{3,2,1,0:T(2,128)}), f32[16,16,2,128]{3,2,1,0:T(2,128)S(1)}, u32[]{:S(2)}, u32[]{:S(2)}) %all-to-all-start) | async-done | bytes 262176 | tf_op jit(solution)/shard_map/all_to_all | solution.py:37
  43.6 0.2 fusion.11
  43.8 0.1 multiply_reduce_fusion
  43.9 0.1 multiply_reduce_fusion.1
  44.0 1.5 %add_divide_fusion = f32[16,128,128]{2,1,0:T(8,128)} fusion(f32[16,128,128]{2,1,0:T(8,128)S(1)} %fusion, f32[16]{0:T(128)S(1)} %get-tuple-element.24, f32[16,128]{1,0:T(8,128)S(1)} %multiply_reduce_fusion, f32[16,128]{1,0:T(8,128)S(1)} %get-tuple-element.23, f32[16,128]{1,0:T(8,128)S(1)} %multiply_reduce_fusion.1, f32[16,128]{1,0:T(8,128)S(1)} %get-tuple-element.22), kind=kLoop, calls=%fused_computation | loop fusion | flops 1310720 | bytes 2129984 | tf_op jit(solution)/shard_map/div | solution.py:60
  (4 shorter events, 0.1 us)
Async XLA Ops:
  0.6 11.2 %copy-start.5 = (f32[16]{0:T(128)S(1)}, f32[16]{0:T(128)}, u32[]{:S(2)}) copy-start(f32[16]{0:T(128)} %param.11) | copy-start | bytes 196
  0.6 12.0 %copy-start.6 = (f32[16]{0:T(128)S(1)}, f32[16]{0:T(128)}, u32[]{:S(2)}) copy-start(f32[16]{0:T(128)} %param.12) | copy-start | bytes 196
  4.4 10.4 %collective-permute-start = (f32[16,2,128]{2,1,0:T(2,128)}, f32[16,2,128]{2,1,0:T(2,128)S(1)}, u32[]{:S(2)}, u32[]{:S(2)}) collective-permute-start(f32[16,2,128]{2,1,0:T(2,128)} %get-tuple-element.9), channel_id=1, source_target_pairs={{0,16},{16,32},{32,48},{48,64},{64,80},{80,96},{96,112},{112,128},... | collective-permute-start | bytes 49160 | tf_op jit(solution)/shard_map/ppermute | solution.py:21
  6.4 8.4 %collective-permute-start.1 = (f32[16,2,128]{2,1,0:T(2,128)}, f32[16,2,128]{2,1,0:T(2,128)S(1)}, u32[]{:S(2)}, u32[]{:S(2)}) collective-permute-start(f32[16,2,128]{2,1,0:T(2,128)} %get-tuple-element.10), channel_id=1, source_target_pairs={{0,240},{16,0},{32,16},{48,32},{64,48},{80,64},{96,80},{112,96},{1... | collective-permute-start | bytes 49160 | tf_op jit(solution)/shard_map/ppermute | solution.py:22
  6.5 8.4 %collective-permute-start.2 = (f32[16,2,128]{2,1,0:T(2,128)}, f32[16,2,128]{2,1,0:T(2,128)S(1)}, u32[]{:S(2)}, u32[]{:S(2)}) collective-permute-start(f32[16,2,128]{2,1,0:T(2,128)} %get-tuple-element.11), channel_id=1, source_target_pairs={{0,1},{1,2},{2,3},{3,4},{4,5},{5,6},{6,7},{7,8},{8,9},{9,10},{10,1... | collective-permute-start | bytes 49160 | tf_op jit(solution)/shard_map/ppermute | solution.py:21
  6.5 8.4 %collective-permute-start.3 = (f32[16,2,128]{2,1,0:T(2,128)}, f32[16,2,128]{2,1,0:T(2,128)S(1)}, u32[]{:S(2)}, u32[]{:S(2)}) collective-permute-start(f32[16,2,128]{2,1,0:T(2,128)} %get-tuple-element.12), channel_id=1, source_target_pairs={{0,15},{1,0},{2,1},{3,2},{4,3},{5,4},{6,5},{7,6},{8,7},{9,8},{10,9... | collective-permute-start | bytes 49160 | tf_op jit(solution)/shard_map/ppermute | solution.py:22
  12.6 2.2 %copy-start.4 = (f32[16]{0:T(128)}, f32[16]{0:T(128)S(1)}, u32[]{:S(2)}) copy-start(f32[16]{0:T(128)S(1)} %get-tuple-element.17.log_lam_ref) | copy-start | bytes 196
  14.8 0.6 %copy-start = (f32[16,2,128]{2,1,0:T(2,128)}, f32[16,2,128]{2,1,0:T(2,128)S(1)}, u32[]{:S(2)}) copy-start(f32[16,2,128]{2,1,0:T(2,128)S(1)} %collective-permute-done.x_prev_ref) | copy-start | bytes 49156
  14.8 0.6 %copy-start.1 = (f32[16,2,128]{2,1,0:T(2,128)}, f32[16,2,128]{2,1,0:T(2,128)S(1)}, u32[]{:S(2)}) copy-start(f32[16,2,128]{2,1,0:T(2,128)S(1)} %collective-permute-done.1.x_next_ref) | copy-start | bytes 49156
  14.8 0.6 %copy-start.2 = (f32[16,2,128]{2,1,0:T(2,128)}, f32[16,2,128]{2,1,0:T(2,128)S(1)}, u32[]{:S(2)}) copy-start(f32[16,2,128]{2,1,0:T(2,128)S(1)} %collective-permute-done.2.y_prev_ref) | copy-start | bytes 49156
  15.4 0.6 %copy-start.3 = (f32[16,2,128]{2,1,0:T(2,128)}, f32[16,2,128]{2,1,0:T(2,128)S(1)}, u32[]{:S(2)}) copy-start(f32[16,2,128]{2,1,0:T(2,128)S(1)} %collective-permute-done.3.y_next_ref) | copy-start | bytes 49156
  23.7 19.9 %all-to-all-start = ((f32[16,16,2,128]{3,2,1,0:T(2,128)}), f32[16,16,2,128]{3,2,1,0:T(2,128)S(1)}, u32[]{:S(2)}, u32[]{:S(2)}) async-start(f32[16,16,2,128]{3,2,1,0:T(2,128)} %get-tuple-element.14), calls=%async_computation | async-start | bytes 524288 | tf_op jit(solution)/shard_map/all_to_all | solution.py:37

commit v6 on v5

--- a/solution.py
+++ b/solution.py
@@ -78,7 +78,7 @@
 
 
 def stencil_kernel(
-    inverse_ref, log_lam_ref, t_ref, u_ref, v_ref, w_ref, early_ref, wall_ref,
+    spacing_ref, ratio_ref, t_ref, u_ref, v_ref, w_ref, early_ref, wall_ref,
     x_prev_ref, x_next_ref, y_prev_ref, y_next_ref, rate_ref, source_ref, ends_ref,
 ):
     per_step = rate_ref.shape[0]
@@ -130,12 +130,15 @@
         t_dn = t_ref[below]
         flux_up = jnp.where(k == top, 0.0, (w + w_ref[above]) * (t + t_up) * 0.25)
         flux_dn = jnp.where(k == 0, 0.0, (w_ref[below] + w) * (t_dn + t) * 0.25)
-        inv_dz = inverse_ref[k]
+        dz = spacing_ref[k]
+        between_up = jnp.where(k == top, dz, 0.5 * (dz + spacing_ref[above]))
+        between_dn = jnp.where(k == 0, dz, 0.5 * (spacing_ref[below] + dz))
+        inv_dz = 1.0 / jnp.full((1, cols), dz, jnp.float32)
         carry_through_depth = (flux_up - flux_dn) * inv_dz
         ghost_up = jnp.where(k == top, wall_ref[1], t_up)
         ghost_dn = jnp.where(k == 0, wall_ref[0], t_dn)
-        slope_up = (ghost_up - t) * inverse_ref[levels + k + 1]
-        slope_dn = (t - ghost_dn) * inverse_ref[levels + k]
+        slope_up = (ghost_up - t) * (1.0 / jnp.full((1, cols), between_up, jnp.float32))
+        slope_dn = (t - ghost_dn) * (1.0 / jnp.full((1, cols), between_dn, jnp.float32))
         thermal_spreading_step = (slope_up - slope_dn) * inv_dz
         stacked_layer_count = t_yn - 2.0 * t + t_yp
         rate = (
@@ -146,7 +149,7 @@
         source = t + NEW_TERM_COEF * rate + OLD_TERM_COEF * early_ref[j]
         rate_ref[j] = rate
         source_ref[j] = source
-        log_lam = log_lam_ref[k]
+        log_lam = spread_root(jnp.full((1, cols), ratio_ref[k], jnp.float32))[0]
         to_end = jnp.sum(jnp.exp(log_lam * ((rows - 1.0) - row_f)) * source, axis=0, keepdims=True)
         from_start = jnp.sum(jnp.exp(log_lam * row_f) * source, axis=0, keepdims=True)
         copies = ends_ref.shape[0]
@@ -166,19 +169,18 @@
     t = initial_warmth_field
     levels, rows, cols = t.shape
     f32 = jnp.float32
-    per_step = 4 if levels % 4 == 0 else 1
     tile = 8
-    level = lambda shape: pl.BlockSpec(shape, lambda g: (g,) + (0,) * (len(shape) - 1))
+    whole = lambda shape: pl.BlockSpec(shape, lambda g: (0,) * len(shape))
     x_first, x_last, y_first, y_last = pl.pallas_call(
         edge_kernel,
-        grid=(levels // per_step,),
+        grid=(1,),
         in_specs=[
-            level((per_step, rows, cols)),
-            pl.BlockSpec((1, per_step, tile, cols), lambda g: (0, g, 0, 0)),
-            pl.BlockSpec((1, per_step, tile, cols), lambda g: (0, g, rows // tile - 1, 0)),
-            pl.BlockSpec((1, per_step, rows, cols), lambda g: (1, g, 0, 0)),
-        ],
-        out_specs=[level((per_step, 2, cols))] * 2 + [level((per_step, 2, rows))] * 2,
+            whole((levels, rows, cols)),
+            pl.BlockSpec((1, levels, tile, cols), lambda g: (0, 0, 0, 0)),
+            pl.BlockSpec((1, levels, tile, cols), lambda g: (0, 0, rows // tile - 1, 0)),
+            pl.BlockSpec((1, levels, rows, cols), lambda g: (1, 0, 0, 0)),
+        ],
+        out_specs=[whole((levels, 2, cols))] * 2 + [whole((levels, 2, rows))] * 2,
         out_shape=[
             jax.ShapeDtypeStruct((levels, 2, cols), f32),
             jax.ShapeDtypeStruct((levels, 2, cols), f32),
@@ -189,17 +191,9 @@
     x_prev, x_next = exchange_edges(x_first, x_last, "gx")
     y_prev, y_next = exchange_edges(y_first, y_last, "gy")
 
-    between = jnp.concatenate(
-        [
-            layer_depth_spacing[:1],
-            0.5 * (layer_depth_spacing[:-1] + layer_depth_spacing[1:]),
-            layer_depth_spacing[-1:],
-        ],
-        0,
-    )
     log_lam, root = spread_root(backward_spread_ratio)
-    inverse = 1.0 / jnp.concatenate([layer_depth_spacing, between])
-    whole = lambda shape: pl.BlockSpec(shape, lambda g: (0,) * len(shape))
+    per_step = 4 if levels % 4 == 0 else 1
+    level = lambda shape: pl.BlockSpec(shape, lambda g: (g,) + (0,) * (len(shape) - 1))
     parts = lax.axis_size("gx")
     smem = pl.BlockSpec(memory_space=pltpu.SMEM)
     current_rate_change, linear_system_source, ends = pl.pallas_call(
@@ -233,7 +227,7 @@
             flops=100 * t.size, bytes_accessed=4 * 8 * t.size, transcendentals=2 * t.size
         ),
     )(
-        inverse, log_lam, t, horizontal_motion_pair,
+        layer_depth_spacing, backward_spread_ratio, t, horizontal_motion_pair,
         horizontal_motion_pair, z_directed_motion, earlier_rate_change, wall_warmth_bounds,
         x_prev, x_next, y_prev, y_next,
     )

time: 45.9 us -> 43.9 us (0.956)
  other arithmetic: 4.72 us -> 1.94 us
  waiting for transfers between devices: 5.81 us -> 7.9 us
  Pallas kernels: 11.4 us -> 10.5 us
  local copies, waits for them, and re-layouts: 2.04 us -> 1.39 us
    div x1 -> x0, other arithmetic: 2.04 us -> none  [on_device(): inverse = 1.0 / jnp.concatenate([layer_depth_spacing, between])]
    ppermute x2, waiting for transfers between devices: 0.01 us -> 1.4 us  [exchange_edges(): from_prev = lax.ppermute(last, axis, ring_pairs(count, 1))]
    pallas_call x1, Pallas kernels: 3.77 us -> 2.81 us  [on_device(): pl.pallas_call(edge_kernel, grid=(1,), in_specs=[whole((levels, rows, col...]
    all_to_all x1, waiting for transfers between devices: 5.8 us -> 6.47 us  [periodic_solve(): gathered = lax.all_to_all(ends, 'gx', 0, 0, tiled=True)]
    exp x1, other arithmetic: 0.74 us -> 0.08 us  [periodic_solve(): into_f = jnp.exp(log_lam * (idx + 1.0)[None, :])]
    slice x1 -> x0, local copies, waits for them, and re-layouts: 0.66 us -> none  [on_device(): layer_depth_spacing[:1]]
    unnamed x14 -> x10, local copies, waits for them, and re-layouts: 1.18 us -> 1.18 us
  transfers between devices with their start and end apart: 5 -> 5, of which waited for: 1 -> 2; matrix products, arithmetic and copies ran while one was open for 14% -> 6% of each run, Pallas kernels for 0% -> 0%
where the time goes in v6:
time: 43.9 us; the launch traced here: 43.1 us
  starting transfers between devices  18.2 us (41%)
  Pallas kernels  10.5 us (24%)
  waiting for transfers between devices  7.9 us (18%)
  matrix products  2.5 us (6%)
  other arithmetic  1.94 us (4%)
  local copies, waits for them, and re-layouts  1.39 us (3%)
  between operations  0.74 us (2%)
    all_to_all x1, starting transfers between devices, periodic_solve(): gathered = lax.all_to_all(ends, 'gx', 0, 0, tiled=True)  10.8 us
    pallas_call x1, Pallas kernels, on_device(): pl.pallas_call(stencil_kernel, grid=(levels // per_step,), in_specs=[smem...  7.67 us
    all_to_all x1, waiting for transfers between devices, periodic_solve(): gathered = lax.all_to_all(ends, 'gx', 0, 0, tiled=True)  6.47 us
    ppermute x2, starting transfers between devices, exchange_edges(): from_next = lax.ppermute(first, axis, ring_pairs(count, -1))  5.47 us
    pallas_call x1, Pallas kernels, on_device(): pl.pallas_call(edge_kernel, grid=(1,), in_specs=[whole((levels, rows, col...  2.81 us
    dot_general x1, matrix products, periodic_solve(): jnp.einsum('kij,kjc->kic', kernel, source, precision=lax.Precision.HIGHEST)  2.5 us
    ppermute x2, starting transfers between devices, exchange_edges(): from_prev = lax.ppermute(last, axis, ring_pairs(count, 1))  1.92 us
    div x1, other arithmetic, periodic_solve(): return total / root[:, None, None]  1.52 us
  transfers between devices with their start and end apart: 5, of which 2 were waited for; matrix products, arithmetic and copies ran while one was open for 6% of the time, Pallas kernels for 0%

profile of v6, /device:TPU:32, one launch (start us, length us, event | category | flops | bytes accessed | tf_op | source)
XLA Modules:
  0.0 43.1 jit_solution(16916401722287527661)
XLA Ops:
  0.6 0.0 copy-start.4
  0.6 2.8 %shard_map.86 = (f32[16,2,128]{2,1,0:T(2,128)}, f32[16,2,128]{2,1,0:T(2,128)}, f32[16,2,128]{2,1,0:T(2,128)}, f32[16,2,128]{2,1,0:T(2,128)}) custom-call(f32[16,128,128]{2,1,0:T(8,128)} %t_ref.3, f32[2,16,128,128]{3,2,1,0:T(8,128)} %v_ref.3, f32[2,16,128,128]{3,2,1,0:T(8,128)} %v_ref.3, f32[2,16,128,128]{3,2,1,0:T(8,128)} %v_ref.3), custom_call_target="tpu_custom_call" | custom-call | tf_op jit(solution)/shard_map/pallas_call | solution.py:174
  3.5 1.9 %collective-permute-start = (f32[16,2,128]{2,1,0:T(2,128)}, f32[16,2,128]{2,1,0:T(2,128)S(1)}, u32[]{:S(2)}, u32[]{:S(2)}) collective-permute-start(f32[16,2,128]{2,1,0:T(2,128)} %get-tuple-element.9), channel_id=1, source_target_pairs={{0,16},{16,32},{32,48},{48,64},{64,80},{80,96},{96,112},{112,128},... | collective-permute-start | bytes 49160 | tf_op jit(solution)/shard_map/ppermute | solution.py:21
  5.4 0.1 collective-permute-start.1
  5.5 0.0 collective-permute-start.2
  5.5 5.4 %collective-permute-start.3 = (f32[16,2,128]{2,1,0:T(2,128)}, f32[16,2,128]{2,1,0:T(2,128)S(1)}, u32[]{:S(2)}, u32[]{:S(2)}) collective-permute-start(f32[16,2,128]{2,1,0:T(2,128)} %get-tuple-element.12), channel_id=1, source_target_pairs={{0,15},{1,0},{2,1},{3,2},{4,3},{5,4},{6,5},{7,6},{8,7},{9,8},{10,9... | collective-permute-start | bytes 49160 | tf_op jit(solution)/shard_map/ppermute | solution.py:22
  10.9 0.0 copy-done.4
  10.9 0.1 exponential_divide_fusion.1
  11.0 0.0 collective-permute-done.x_prev_ref
  11.0 0.0 copy-start
  11.1 0.0 collective-permute-done.1.x_next_ref
  11.1 0.0 copy-start.1
  11.1 1.4 %collective-permute-done.2.y_prev_ref = f32[16,2,128]{2,1,0:T(2,128)S(1)} collective-permute-done((f32[16,2,128]{2,1,0:T(2,128)}, f32[16,2,128]{2,1,0:T(2,128)S(1)}, u32[]{:S(2)}, u32[]{:S(2)}) %collective-permute-start.2) | collective-permute-done | bytes 16416 | tf_op jit(solution)/shard_map/ppermute | solution.py:21
  12.5 0.0 copy-start.2
  12.5 0.0 collective-permute-done.3.y_next_ref
  12.5 0.0 copy-done
  12.5 0.0 copy-done.1
  12.5 0.6 %copy-done.2 = f32[16,2,128]{2,1,0:T(2,128)} copy-done((f32[16,2,128]{2,1,0:T(2,128)}, f32[16,2,128]{2,1,0:T(2,128)S(1)}, u32[]{:S(2)}) %copy-start.2) | copy-done | bytes 16408
  13.1 0.0 copy-start.3
  13.1 0.6 %copy-done.3 = f32[16,2,128]{2,1,0:T(2,128)} copy-done((f32[16,2,128]{2,1,0:T(2,128)}, f32[16,2,128]{2,1,0:T(2,128)S(1)}, u32[]{:S(2)}) %copy-start.3) | copy-done | bytes 16408
  13.7 7.7 %shard_map.87 = (f32[16,128,128]{2,1,0:T(8,128)}, f32[16,128,128]{2,1,0:T(8,128)}, f32[16,16,2,128]{3,2,1,0:T(2,128)}) custom-call(f32[16]{0:T(128)} %spacing_ref.1, f32[16]{0:T(128)} %ratio_ref.1, f32[16,128,128]{2,1,0:T(8,128)} %t_ref.3, f32[2,16,128,128]{3,2,1,0:T(8,128)} %v_ref.3, f32[2,16,128,128]{3,2,1,0:T(8,128)} %v_ref.3, f32[16,128,128]{2,1,0:T(8,128)} %w_ref.1, ...), custom_call_target="tpu_custom_call" | custom-call | flops 26214400 | bytes 8388608 | tf_op jit(solution)/shard_map/pallas_call | solution.py:199
  21.3 10.8 %all-to-all-start = ((f32[16,16,2,128]{3,2,1,0:T(2,128)}), f32[16,16,2,128]{3,2,1,0:T(2,128)S(1)}, u32[]{:S(2)}, u32[]{:S(2)}) async-start(f32[16,16,2,128]{3,2,1,0:T(2,128)} %get-tuple-element.14), calls=%async_computation | async-start | bytes 524288 | tf_op jit(solution)/shard_map/all_to_all | solution.py:37
  32.2 0.1 multiply_exponential_fusion.1
  32.2 2.5 %fusion = f32[16,128,128]{2,1,0:T(8,128)S(1)} fusion(f32[16,128,128]{2,1,0:T(8,128)} %get-tuple-element.13, f32[128,128]{1,0:T(8,128)S(1)} %subtract_abs_fusion, f32[16]{0:T(128)S(1)} %get-tuple-element.17), kind=kOutput, calls=%fused_computation.1 | convolution fusion | flops 402915328 | bytes 2162752 | tf_op jit(solution)/shard_map/kij,kjc->kic/dot_general | solution.py:42
  34.7 6.5 %all-to-all-done = f32[16,16,2,128]{3,2,1,0:T(2,128)S(1)} async-done(((f32[16,16,2,128]{3,2,1,0:T(2,128)}), f32[16,16,2,128]{3,2,1,0:T(2,128)S(1)}, u32[]{:S(2)}, u32[]{:S(2)}) %all-to-all-start) | async-done | bytes 262176 | tf_op jit(solution)/shard_map/all_to_all | solution.py:37
  41.2 0.2 fusion.11
  41.4 0.1 multiply_reduce_fusion
  41.5 0.1 multiply_reduce_fusion.1
  41.6 1.5 %add_divide_fusion = f32[16,128,128]{2,1,0:T(8,128)} fusion(f32[16,128,128]{2,1,0:T(8,128)S(1)} %fusion, f32[16]{0:T(128)S(1)} %get-tuple-element.24, f32[16,128]{1,0:T(8,128)S(1)} %multiply_reduce_fusion, f32[16,128]{1,0:T(8,128)S(1)} %get-tuple-element.23, f32[16,128]{1,0:T(8,128)S(1)} %multiply_reduce_fusion.1, f32[16,128]{1,0:T(8,128)S(1)} %get-tuple-element.22), kind=kLoop, calls=%fused_computation | loop fusion | flops 1310720 | bytes 2129984 | tf_op jit(solution)/shard_map/div | solution.py:60
  (4 shorter events, 0.1 us)
Async XLA Ops:
  0.6 10.2 %copy-start.4 = (f32[16]{0:T(128)S(1)}, f32[16]{0:T(128)}, u32[]{:S(2)}) copy-start(f32[16]{0:T(128)} %ratio_ref.1) | copy-start | bytes 196
  3.5 7.6 %collective-permute-start = (f32[16,2,128]{2,1,0:T(2,128)}, f32[16,2,128]{2,1,0:T(2,128)S(1)}, u32[]{:S(2)}, u32[]{:S(2)}) collective-permute-start(f32[16,2,128]{2,1,0:T(2,128)} %get-tuple-element.9), channel_id=1, source_target_pairs={{0,16},{16,32},{32,48},{48,64},{64,80},{80,96},{96,112},{112,128},... | collective-permute-start | bytes 49160 | tf_op jit(solution)/shard_map/ppermute | solution.py:21
  5.4 5.7 %collective-permute-start.1 = (f32[16,2,128]{2,1,0:T(2,128)}, f32[16,2,128]{2,1,0:T(2,128)S(1)}, u32[]{:S(2)}, u32[]{:S(2)}) collective-permute-start(f32[16,2,128]{2,1,0:T(2,128)} %get-tuple-element.10), channel_id=1, source_target_pairs={{0,240},{16,0},{32,16},{48,32},{64,48},{80,64},{96,80},{112,96},{1... | collective-permute-start | bytes 49160 | tf_op jit(solution)/shard_map/ppermute | solution.py:22
  5.5 7.0 %collective-permute-start.2 = (f32[16,2,128]{2,1,0:T(2,128)}, f32[16,2,128]{2,1,0:T(2,128)S(1)}, u32[]{:S(2)}, u32[]{:S(2)}) collective-permute-start(f32[16,2,128]{2,1,0:T(2,128)} %get-tuple-element.11), channel_id=1, source_target_pairs={{0,1},{1,2},{2,3},{3,4},{4,5},{5,6},{6,7},{7,8},{8,9},{9,10},{10,1... | collective-permute-start | bytes 49160 | tf_op jit(solution)/shard_map/ppermute | solution.py:21
  5.5 7.0 %collective-permute-start.3 = (f32[16,2,128]{2,1,0:T(2,128)}, f32[16,2,128]{2,1,0:T(2,128)S(1)}, u32[]{:S(2)}, u32[]{:S(2)}) collective-permute-start(f32[16,2,128]{2,1,0:T(2,128)} %get-tuple-element.12), channel_id=1, source_target_pairs={{0,15},{1,0},{2,1},{3,2},{4,3},{5,4},{6,5},{7,6},{8,7},{9,8},{10,9... | collective-permute-start | bytes 49160 | tf_op jit(solution)/shard_map/ppermute | solution.py:22
  11.0 1.5 %copy-start = (f32[16,2,128]{2,1,0:T(2,128)}, f32[16,2,128]{2,1,0:T(2,128)S(1)}, u32[]{:S(2)}) copy-start(f32[16,2,128]{2,1,0:T(2,128)S(1)} %collective-permute-done.x_prev_ref) | copy-start | bytes 49156
  11.1 1.4 %copy-start.1 = (f32[16,2,128]{2,1,0:T(2,128)}, f32[16,2,128]{2,1,0:T(2,128)S(1)}, u32[]{:S(2)}) copy-start(f32[16,2,128]{2,1,0:T(2,128)S(1)} %collective-permute-done.1.x_next_ref) | copy-start | bytes 49156
  12.5 0.6 %copy-start.2 = (f32[16,2,128]{2,1,0:T(2,128)}, f32[16,2,128]{2,1,0:T(2,128)S(1)}, u32[]{:S(2)}) copy-start(f32[16,2,128]{2,1,0:T(2,128)S(1)} %collective-permute-done.2.y_prev_ref) | copy-start | bytes 49156
  13.1 0.6 %copy-start.3 = (f32[16,2,128]{2,1,0:T(2,128)}, f32[16,2,128]{2,1,0:T(2,128)S(1)}, u32[]{:S(2)}) copy-start(f32[16,2,128]{2,1,0:T(2,128)S(1)} %collective-permute-done.3.y_next_ref) | copy-start | bytes 49156
  21.3 19.9 %all-to-all-start = ((f32[16,16,2,128]{3,2,1,0:T(2,128)}), f32[16,16,2,128]{3,2,1,0:T(2,128)S(1)}, u32[]{:S(2)}, u32[]{:S(2)}) async-start(f32[16,16,2,128]{3,2,1,0:T(2,128)} %get-tuple-element.14), calls=%async_computation | async-start | bytes 524288 | tf_op jit(solution)/shard_map/all_to_all | solution.py:37

commit v7 on v6

--- a/solution.py
+++ b/solution.py
@@ -78,81 +78,103 @@
 
 
 def stencil_kernel(
-    spacing_ref, ratio_ref, t_ref, u_ref, v_ref, w_ref, early_ref, wall_ref,
-    x_prev_ref, x_next_ref, y_prev_ref, y_next_ref, rate_ref, source_ref, ends_ref,
+    spacing_ref, ratio_ref, t_ref, t_dn_ref, t_up_ref, u_ref, v_ref, w_ref, w_dn_ref, w_up_ref,
+    early_ref, wall_ref, x_prev_ref, x_next_ref, y_prev_ref, y_next_ref,
+    rate_ref, source_ref, ends_ref,
 ):
-    per_step = rate_ref.shape[0]
-    levels, rows, cols = t_ref.shape
-    top = levels - 1
-    row = lax.broadcasted_iota(jnp.int32, (rows, cols), 0)
-    col = lax.broadcasted_iota(jnp.int32, (rows, cols), 1)
+    per_step, rows, cols = t_ref.shape
+    top = x_prev_ref.shape[0] - 1
+    chunk = 16
+    row = lax.broadcasted_iota(jnp.int32, (chunk, cols), 0)
+    col = lax.broadcasted_iota(jnp.int32, (chunk, cols), 1)
     row_f = row.astype(jnp.float32)
     slot = lax.broadcasted_iota(jnp.int32, (8, rows), 0)
+    copies = ends_ref.shape[0]
     for j in range(per_step):
         k = pl.program_id(0) * per_step + j
-        below = jnp.maximum(k - 1, 0)
-        above = jnp.minimum(k + 1, top)
-        t = t_ref[k]
-        u = u_ref[0, j]
-        v = v_ref[0, j]
-        w = w_ref[k]
-        xp = x_prev_ref[j]
-        xn = x_next_ref[j]
-        yp = y_prev_ref[j]
-        yn = y_next_ref[j]
+        xp = x_prev_ref[k]
+        xn = x_next_ref[k]
+        yp = y_prev_ref[k]
+        yn = y_next_ref[k]
         y_rows = jnp.where(
             slot == 0, yp[0:1],
             jnp.where(slot == 1, yp[1:2], jnp.where(slot == 2, yn[0:1], jnp.where(slot == 3, yn[1:2], 0.0))),
         )
         yh = y_rows.T
-
-        def along_x(a, prev, nxt):
-            a_next = jnp.where(row == rows - 1, nxt, pltpu.roll(a, rows - 1, 0))
-            a_prev = jnp.where(row == 0, prev, pltpu.roll(a, 1, 0))
-            return a_prev, a_next
-
-        def along_y(a, prev, nxt):
-            a_next = jnp.where(col == cols - 1, nxt, pltpu.roll(a, cols - 1, 1))
-            a_prev = jnp.where(col == 0, prev, pltpu.roll(a, 1, 1))
-            return a_prev, a_next
-
-        t_xp, t_xn = along_x(t, xp[0:1], xn[0:1])
-        u_xp, u_xn = along_x(u, xp[1:2], xn[1:2])
-        t_yp, t_yn = along_y(t, yh[:, 0:1], yh[:, 2:3])
-        v_yp, v_yn = along_y(v, yh[:, 1:2], yh[:, 3:4])
-        flux_x_hi = (u + u_xn) * (t + t_xn) * 0.25
-        flux_x_lo = (u_xp + u) * (t_xp + t) * 0.25
-        flux_y_hi = (v + v_yn) * (t + t_yn) * 0.25
-        flux_y_lo = (v_yp + v) * (t_yp + t) * 0.25
-        advect_xy = (flux_x_hi - flux_x_lo) + (flux_y_hi - flux_y_lo)
-
-        t_up = t_ref[above]
-        t_dn = t_ref[below]
-        flux_up = jnp.where(k == top, 0.0, (w + w_ref[above]) * (t + t_up) * 0.25)
-        flux_dn = jnp.where(k == 0, 0.0, (w_ref[below] + w) * (t_dn + t) * 0.25)
         dz = spacing_ref[k]
-        between_up = jnp.where(k == top, dz, 0.5 * (dz + spacing_ref[above]))
-        between_dn = jnp.where(k == 0, dz, 0.5 * (spacing_ref[below] + dz))
+        dz_up = spacing_ref[jnp.minimum(k + 1, top)]
+        dz_dn = spacing_ref[jnp.maximum(k - 1, 0)]
+        between_up = jnp.where(k == top, dz, 0.5 * (dz + dz_up))
+        between_dn = jnp.where(k == 0, dz, 0.5 * (dz_dn + dz))
         inv_dz = 1.0 / jnp.full((1, cols), dz, jnp.float32)
-        carry_through_depth = (flux_up - flux_dn) * inv_dz
-        ghost_up = jnp.where(k == top, wall_ref[1], t_up)
-        ghost_dn = jnp.where(k == 0, wall_ref[0], t_dn)
-        slope_up = (ghost_up - t) * (1.0 / jnp.full((1, cols), between_up, jnp.float32))
-        slope_dn = (t - ghost_dn) * (1.0 / jnp.full((1, cols), between_dn, jnp.float32))
-        thermal_spreading_step = (slope_up - slope_dn) * inv_dz
-        stacked_layer_count = t_yn - 2.0 * t + t_yp
-        rate = (
-            -COURANT * (advect_xy + carry_through_depth)
-            + DIFF_Y * stacked_layer_count
-            + DIFF_Z * thermal_spreading_step
-        )
-        source = t + NEW_TERM_COEF * rate + OLD_TERM_COEF * early_ref[j]
-        rate_ref[j] = rate
-        source_ref[j] = source
+        inv_up = 1.0 / jnp.full((1, cols), between_up, jnp.float32)
+        inv_dn = 1.0 / jnp.full((1, cols), between_dn, jnp.float32)
         log_lam = spread_root(jnp.full((1, cols), ratio_ref[k], jnp.float32))[0]
-        to_end = jnp.sum(jnp.exp(log_lam * ((rows - 1.0) - row_f)) * source, axis=0, keepdims=True)
-        from_start = jnp.sum(jnp.exp(log_lam * row_f) * source, axis=0, keepdims=True)
-        copies = ends_ref.shape[0]
+        t_lvl = t_ref.at[j]
+        u_lvl = u_ref.at[0, j]
+        w_lvl = w_ref.at[j]
+        t_above = t_ref.at[j + 1] if j + 1 < per_step else t_up_ref.at[0]
+        w_above = w_ref.at[j + 1] if j + 1 < per_step else w_up_ref.at[0]
+        t_below = t_ref.at[j - 1] if j > 0 else t_dn_ref.at[0]
+        w_below = w_ref.at[j - 1] if j > 0 else w_dn_ref.at[0]
+        to_end = jnp.zeros((1, cols), jnp.float32)
+        from_start = jnp.zeros((1, cols), jnp.float32)
+        for c in range(rows // chunk):
+            lo, hi = c * chunk, (c + 1) * chunk
+            t = t_lvl[lo:hi]
+            u = u_lvl[lo:hi]
+            v = v_ref[0, j, lo:hi]
+            w = w_lvl[lo:hi]
+            t_prev_row = xp[0:1] if c == 0 else t_lvl[lo - 1 : lo]
+            u_prev_row = xp[1:2] if c == 0 else u_lvl[lo - 1 : lo]
+            t_next_row = xn[0:1] if hi == rows else t_lvl[hi : hi + 1]
+            u_next_row = xn[1:2] if hi == rows else u_lvl[hi : hi + 1]
+            t_xn = jnp.where(row == chunk - 1, t_next_row, pltpu.roll(t, chunk - 1, 0))
+            t_xp = jnp.where(row == 0, t_prev_row, pltpu.roll(t, 1, 0))
+            u_xn = jnp.where(row == chunk - 1, u_next_row, pltpu.roll(u, chunk - 1, 0))
+            u_xp = jnp.where(row == 0, u_prev_row, pltpu.roll(u, 1, 0))
+            t_yn = jnp.where(col == cols - 1, yh[lo:hi, 2:3], pltpu.roll(t, cols - 1, 1))
+            t_yp = jnp.where(col == 0, yh[lo:hi, 0:1], pltpu.roll(t, 1, 1))
+            v_yn = jnp.where(col == cols - 1, yh[lo:hi, 3:4], pltpu.roll(v, cols - 1, 1))
+            v_yp = jnp.where(col == 0, yh[lo:hi, 1:2], pltpu.roll(v, 1, 1))
+            flux_x_hi = (u + u_xn) * (t + t_xn) * 0.25
+            flux_x_lo = (u_xp + u) * (t_xp + t) * 0.25
+            flux_y_hi = (v + v_yn) * (t + t_yn) * 0.25
+            flux_y_lo = (v_yp + v) * (t_yp + t) * 0.25
+            advect_xy = (flux_x_hi - flux_x_lo) + (flux_y_hi - flux_y_lo)
+
+            t_up = t_above[lo:hi]
+            t_dn = t_below[lo:hi]
+            flux_up = (w + w_above[lo:hi]) * (t + t_up) * 0.25
+            flux_dn = (w_below[lo:hi] + w) * (t_dn + t) * 0.25
+            ghost_up = t_up
+            ghost_dn = t_dn
+            if j + 1 == per_step:
+                flux_up = jnp.where(k == top, 0.0, flux_up)
+                ghost_up = jnp.where(k == top, wall_ref[1, lo:hi], t_up)
+            if j == 0:
+                flux_dn = jnp.where(k == 0, 0.0, flux_dn)
+                ghost_dn = jnp.where(k == 0, wall_ref[0, lo:hi], t_dn)
+            carry_through_depth = (flux_up - flux_dn) * inv_dz
+            slope_up = (ghost_up - t) * inv_up
+            slope_dn = (t - ghost_dn) * inv_dn
+            thermal_spreading_step = (slope_up - slope_dn) * inv_dz
+            stacked_layer_count = t_yn - 2.0 * t + t_yp
+            rate = (
+                -COURANT * (advect_xy + carry_through_depth)
+                + DIFF_Y * stacked_layer_count
+                + DIFF_Z * thermal_spreading_step
+            )
+            source = t + NEW_TERM_COEF * rate + OLD_TERM_COEF * early_ref[j, lo:hi]
+            rate_ref[j, lo:hi] = rate
+            source_ref[j, lo:hi] = source
+            place = row_f + float(lo)
+            to_end = to_end + jnp.sum(
+                jnp.exp(log_lam * ((rows - 1.0) - place)) * source, axis=0, keepdims=True
+            )
+            from_start = from_start + jnp.sum(
+                jnp.exp(log_lam * place) * source, axis=0, keepdims=True
+            )
         ends_ref[:, j, 0:1, :] = jnp.broadcast_to(to_end[None], (copies, 1, cols))
         ends_ref[:, j, 1:2, :] = jnp.broadcast_to(from_start[None], (copies, 1, cols))
 
@@ -195,6 +217,13 @@
     per_step = 4 if levels % 4 == 0 else 1
     level = lambda shape: pl.BlockSpec(shape, lambda g: (g,) + (0,) * (len(shape) - 1))
     parts = lax.axis_size("gx")
+    vmem = pl.BlockSpec(memory_space=pltpu.VMEM)
+    below = pl.BlockSpec(
+        (1, rows, cols), lambda g: (jnp.maximum(g * per_step - 1, 0), 0, 0)
+    )
+    above = pl.BlockSpec(
+        (1, rows, cols), lambda g: (jnp.minimum(g * per_step + per_step, levels - 1), 0, 0)
+    )
     smem = pl.BlockSpec(memory_space=pltpu.SMEM)
     current_rate_change, linear_system_source, ends = pl.pallas_call(
         stencil_kernel,
@@ -202,16 +231,20 @@
         in_specs=[
             smem,
             smem,
-            whole((levels, rows, cols)),
+            level((per_step, rows, cols)),
+            below,
+            above,
             pl.BlockSpec((1, per_step, rows, cols), lambda g: (0, g, 0, 0)),
             pl.BlockSpec((1, per_step, rows, cols), lambda g: (1, g, 0, 0)),
-            whole((levels, rows, cols)),
+            level((per_step, rows, cols)),
+            below,
+            above,
             level((per_step, rows, cols)),
             whole((2, rows, cols)),
-            level((per_step, 2, cols)),
-            level((per_step, 2, cols)),
-            level((per_step, 2, rows)),
-            level((per_step, 2, rows)),
+            vmem,
+            vmem,
+            vmem,
+            vmem,
         ],
         out_specs=[
             level((per_step, rows, cols)),
@@ -227,8 +260,9 @@
             flops=100 * t.size, bytes_accessed=4 * 8 * t.size, transcendentals=2 * t.size
         ),
     )(
-        layer_depth_spacing, backward_spread_ratio, t, horizontal_motion_pair,
-        horizontal_motion_pair, z_directed_motion, earlier_rate_change, wall_warmth_bounds,
+        layer_depth_spacing, backward_spread_ratio, t, t, t, horizontal_motion_pair,
+        horizontal_motion_pair, z_directed_motion, z_directed_motion, z_directed_motion,
+        earlier_rate_change, wall_warmth_bounds,
         x_prev, x_next, y_prev, y_next,
     )
     resulting_warmth_field = periodic_solve(linear_system_source, ends, log_lam, root)

time: 43.9 us -> 44.4 us (1.011)
  no operation moved by 1% of the time
where the time goes in v7:
time: 44.4 us; the launch traced here: 43.6 us
  starting transfers between devices  18.2 us (41%)
  Pallas kernels  10.9 us (25%)
  waiting for transfers between devices  7.9 us (18%)
  matrix products  2.5 us (6%)
  other arithmetic  1.94 us (4%)
  local copies, waits for them, and re-layouts  1.39 us (3%)
  between operations  0.74 us (2%)
    all_to_all x1, starting transfers between devices, periodic_solve(): gathered = lax.all_to_all(ends, 'gx', 0, 0, tiled=True)  10.8 us
    pallas_call x1, Pallas kernels, on_device(): pl.pallas_call(stencil_kernel, grid=(levels // per_step,), in_specs=[smem...  8.08 us
    all_to_all x1, waiting for transfers between devices, periodic_solve(): gathered = lax.all_to_all(ends, 'gx', 0, 0, tiled=True)  6.47 us
    ppermute x2, starting transfers between devices, exchange_edges(): from_next = lax.ppermute(first, axis, ring_pairs(count, -1))  5.47 us
    pallas_call x1, Pallas kernels, on_device(): pl.pallas_call(edge_kernel, grid=(1,), in_specs=[whole((levels, rows, col...  2.81 us
    dot_general x1, matrix products, periodic_solve(): jnp.einsum('kij,kjc->kic', kernel, source, precision=lax.Precision.HIGHEST)  2.5 us
    ppermute x2, starting transfers between devices, exchange_edges(): from_prev = lax.ppermute(last, axis, ring_pairs(count, 1))  1.92 us
    div x1, other arithmetic, periodic_solve(): return total / root[:, None, None]  1.52 us
  transfers between devices with their start and end apart: 5, of which 2 were waited for; matrix products, arithmetic and copies ran while one was open for 6% of the time, Pallas kernels for 0%

profile of v7, /device:TPU:32, one launch (start us, length us, event | category | flops | bytes accessed | tf_op | source)
XLA Modules:
  0.0 43.6 jit_solution(16896317253707871757)
XLA Ops:
  0.6 0.0 copy-start.4
  0.6 2.8 %shard_map.86 = (f32[16,2,128]{2,1,0:T(2,128)}, f32[16,2,128]{2,1,0:T(2,128)}, f32[16,2,128]{2,1,0:T(2,128)}, f32[16,2,128]{2,1,0:T(2,128)}) custom-call(f32[16,128,128]{2,1,0:T(8,128)} %t_up_ref.1, f32[2,16,128,128]{3,2,1,0:T(8,128)} %v_ref.3, f32[2,16,128,128]{3,2,1,0:T(8,128)} %v_ref.3, f32[2,16,128,128]{3,2,1,0:T(8,128)} %v_ref.3), custom_call_target="tpu_custom_call" | custom-call | tf_op jit(solution)/shard_map/pallas_call | solution.py:196
  3.5 1.9 %collective-permute-start = (f32[16,2,128]{2,1,0:T(2,128)}, f32[16,2,128]{2,1,0:T(2,128)S(1)}, u32[]{:S(2)}, u32[]{:S(2)}) collective-permute-start(f32[16,2,128]{2,1,0:T(2,128)} %get-tuple-element.9), channel_id=1, source_target_pairs={{0,16},{16,32},{32,48},{48,64},{64,80},{80,96},{96,112},{112,128},... | collective-permute-start | bytes 49160 | tf_op jit(solution)/shard_map/ppermute | solution.py:21
  5.4 0.1 collective-permute-start.1
  5.5 0.0 collective-permute-start.2
  5.5 5.4 %collective-permute-start.3 = (f32[16,2,128]{2,1,0:T(2,128)}, f32[16,2,128]{2,1,0:T(2,128)S(1)}, u32[]{:S(2)}, u32[]{:S(2)}) collective-permute-start(f32[16,2,128]{2,1,0:T(2,128)} %get-tuple-element.12), channel_id=1, source_target_pairs={{0,15},{1,0},{2,1},{3,2},{4,3},{5,4},{6,5},{7,6},{8,7},{9,8},{10,9... | collective-permute-start | bytes 49160 | tf_op jit(solution)/shard_map/ppermute | solution.py:22
  10.9 0.0 copy-done.4
  10.9 0.1 exponential_divide_fusion.1
  11.0 0.0 collective-permute-done.x_prev_ref
  11.0 0.0 copy-start
  11.1 0.0 collective-permute-done.1.x_next_ref
  11.1 0.0 copy-start.1
  11.1 1.4 %collective-permute-done.2.y_prev_ref = f32[16,2,128]{2,1,0:T(2,128)S(1)} collective-permute-done((f32[16,2,128]{2,1,0:T(2,128)}, f32[16,2,128]{2,1,0:T(2,128)S(1)}, u32[]{:S(2)}, u32[]{:S(2)}) %collective-permute-start.2) | collective-permute-done | bytes 16416 | tf_op jit(solution)/shard_map/ppermute | solution.py:21
  12.5 0.0 copy-start.2
  12.5 0.0 collective-permute-done.3.y_next_ref
  12.5 0.0 copy-done
  12.5 0.0 copy-done.1
  12.5 0.6 %copy-done.2 = f32[16,2,128]{2,1,0:T(2,128)} copy-done((f32[16,2,128]{2,1,0:T(2,128)}, f32[16,2,128]{2,1,0:T(2,128)S(1)}, u32[]{:S(2)}) %copy-start.2) | copy-done | bytes 16408
  13.1 0.0 copy-start.3
  13.1 0.6 %copy-done.3 = f32[16,2,128]{2,1,0:T(2,128)} copy-done((f32[16,2,128]{2,1,0:T(2,128)}, f32[16,2,128]{2,1,0:T(2,128)S(1)}, u32[]{:S(2)}) %copy-start.3) | copy-done | bytes 16408
  13.7 8.1 %shard_map.87 = (f32[16,128,128]{2,1,0:T(8,128)}, f32[16,128,128]{2,1,0:T(8,128)}, f32[16,16,2,128]{3,2,1,0:T(2,128)}) custom-call(f32[16]{0:T(128)} %spacing_ref.1, f32[16]{0:T(128)} %ratio_ref.1, f32[16,128,128]{2,1,0:T(8,128)} %t_up_ref.1, f32[16,128,128]{2,1,0:T(8,128)} %t_up_ref.1, f32[16,128,128]{2,1,0:T(8,128)} %t_up_ref.1, ...), custom_call_target="tpu_custom_call" | custom-call | flops 26214400 | bytes 8388608 | tf_op jit(solution)/shard_map/pallas_call | solution.py:228
  21.8 10.8 %all-to-all-start = ((f32[16,16,2,128]{3,2,1,0:T(2,128)}), f32[16,16,2,128]{3,2,1,0:T(2,128)S(1)}, u32[]{:S(2)}, u32[]{:S(2)}) async-start(f32[16,16,2,128]{3,2,1,0:T(2,128)} %get-tuple-element.14), calls=%async_computation | async-start | bytes 524288 | tf_op jit(solution)/shard_map/all_to_all | solution.py:37
  32.6 0.1 multiply_exponential_fusion.1
  32.6 2.5 %fusion = f32[16,128,128]{2,1,0:T(8,128)S(1)} fusion(f32[16,128,128]{2,1,0:T(8,128)} %get-tuple-element.13, f32[128,128]{1,0:T(8,128)S(1)} %subtract_abs_fusion, f32[16]{0:T(128)S(1)} %get-tuple-element.17), kind=kOutput, calls=%fused_computation.1 | convolution fusion | flops 402915328 | bytes 2162752 | tf_op jit(solution)/shard_map/kij,kjc->kic/dot_general | solution.py:42
  35.2 6.5 %all-to-all-done = f32[16,16,2,128]{3,2,1,0:T(2,128)S(1)} async-done(((f32[16,16,2,128]{3,2,1,0:T(2,128)}), f32[16,16,2,128]{3,2,1,0:T(2,128)S(1)}, u32[]{:S(2)}, u32[]{:S(2)}) %all-to-all-start) | async-done | bytes 262176 | tf_op jit(solution)/shard_map/all_to_all | solution.py:37
  41.6 0.2 fusion.11
  41.8 0.1 multiply_reduce_fusion
  41.9 0.1 multiply_reduce_fusion.1
  42.0 1.5 %add_divide_fusion = f32[16,128,128]{2,1,0:T(8,128)} fusion(f32[16,128,128]{2,1,0:T(8,128)S(1)} %fusion, f32[16]{0:T(128)S(1)} %get-tuple-element.24, f32[16,128]{1,0:T(8,128)S(1)} %multiply_reduce_fusion, f32[16,128]{1,0:T(8,128)S(1)} %get-tuple-element.23, f32[16,128]{1,0:T(8,128)S(1)} %multiply_reduce_fusion.1, f32[16,128]{1,0:T(8,128)S(1)} %get-tuple-element.22), kind=kLoop, calls=%fused_computation | loop fusion | flops 1310720 | bytes 2129984 | tf_op jit(solution)/shard_map/div | solution.py:60
  (4 shorter events, 0.1 us)
Async XLA Ops:
  0.6 10.2 %copy-start.4 = (f32[16]{0:T(128)S(1)}, f32[16]{0:T(128)}, u32[]{:S(2)}) copy-start(f32[16]{0:T(128)} %ratio_ref.1) | copy-start | bytes 196
  3.5 7.6 %collective-permute-start = (f32[16,2,128]{2,1,0:T(2,128)}, f32[16,2,128]{2,1,0:T(2,128)S(1)}, u32[]{:S(2)}, u32[]{:S(2)}) collective-permute-start(f32[16,2,128]{2,1,0:T(2,128)} %get-tuple-element.9), channel_id=1, source_target_pairs={{0,16},{16,32},{32,48},{48,64},{64,80},{80,96},{96,112},{112,128},... | collective-permute-start | bytes 49160 | tf_op jit(solution)/shard_map/ppermute | solution.py:21
  5.4 5.7 %collective-permute-start.1 = (f32[16,2,128]{2,1,0:T(2,128)}, f32[16,2,128]{2,1,0:T(2,128)S(1)}, u32[]{:S(2)}, u32[]{:S(2)}) collective-permute-start(f32[16,2,128]{2,1,0:T(2,128)} %get-tuple-element.10), channel_id=1, source_target_pairs={{0,240},{16,0},{32,16},{48,32},{64,48},{80,64},{96,80},{112,96},{1... | collective-permute-start | bytes 49160 | tf_op jit(solution)/shard_map/ppermute | solution.py:22
  5.5 7.0 %collective-permute-start.2 = (f32[16,2,128]{2,1,0:T(2,128)}, f32[16,2,128]{2,1,0:T(2,128)S(1)}, u32[]{:S(2)}, u32[]{:S(2)}) collective-permute-start(f32[16,2,128]{2,1,0:T(2,128)} %get-tuple-element.11), channel_id=1, source_target_pairs={{0,1},{1,2},{2,3},{3,4},{4,5},{5,6},{6,7},{7,8},{8,9},{9,10},{10,1... | collective-permute-start | bytes 49160 | tf_op jit(solution)/shard_map/ppermute | solution.py:21
  5.5 7.0 %collective-permute-start.3 = (f32[16,2,128]{2,1,0:T(2,128)}, f32[16,2,128]{2,1,0:T(2,128)S(1)}, u32[]{:S(2)}, u32[]{:S(2)}) collective-permute-start(f32[16,2,128]{2,1,0:T(2,128)} %get-tuple-element.12), channel_id=1, source_target_pairs={{0,15},{1,0},{2,1},{3,2},{4,3},{5,4},{6,5},{7,6},{8,7},{9,8},{10,9... | collective-permute-start | bytes 49160 | tf_op jit(solution)/shard_map/ppermute | solution.py:22
  11.0 1.5 %copy-start = (f32[16,2,128]{2,1,0:T(2,128)}, f32[16,2,128]{2,1,0:T(2,128)S(1)}, u32[]{:S(2)}) copy-start(f32[16,2,128]{2,1,0:T(2,128)S(1)} %collective-permute-done.x_prev_ref) | copy-start | bytes 49156
  11.1 1.4 %copy-start.1 = (f32[16,2,128]{2,1,0:T(2,128)}, f32[16,2,128]{2,1,0:T(2,128)S(1)}, u32[]{:S(2)}) copy-start(f32[16,2,128]{2,1,0:T(2,128)S(1)} %collective-permute-done.1.x_next_ref) | copy-start | bytes 49156
  12.5 0.6 %copy-start.2 = (f32[16,2,128]{2,1,0:T(2,128)}, f32[16,2,128]{2,1,0:T(2,128)S(1)}, u32[]{:S(2)}) copy-start(f32[16,2,128]{2,1,0:T(2,128)S(1)} %collective-permute-done.2.y_prev_ref) | copy-start | bytes 49156
  13.1 0.6 %copy-start.3 = (f32[16,2,128]{2,1,0:T(2,128)}, f32[16,2,128]{2,1,0:T(2,128)S(1)}, u32[]{:S(2)}) copy-start(f32[16,2,128]{2,1,0:T(2,128)S(1)} %collective-permute-done.3.y_next_ref) | copy-start | bytes 49156
  21.8 19.9 %all-to-all-start = ((f32[16,16,2,128]{3,2,1,0:T(2,128)}), f32[16,16,2,128]{3,2,1,0:T(2,128)S(1)}, u32[]{:S(2)}, u32[]{:S(2)}) async-start(f32[16,16,2,128]{3,2,1,0:T(2,128)} %get-tuple-element.14), calls=%async_computation | async-start | bytes 524288 | tf_op jit(solution)/shard_map/all_to_all | solution.py:37

commit v8 on v7

--- a/solution.py
+++ b/solution.py
@@ -80,7 +80,7 @@
 def stencil_kernel(
     spacing_ref, ratio_ref, t_ref, t_dn_ref, t_up_ref, u_ref, v_ref, w_ref, w_dn_ref, w_up_ref,
     early_ref, wall_ref, x_prev_ref, x_next_ref, y_prev_ref, y_next_ref,
-    rate_ref, source_ref, ends_ref,
+    rate_ref, ends_ref,
 ):
     per_step, rows, cols = t_ref.shape
     top = x_prev_ref.shape[0] - 1
@@ -167,7 +167,6 @@
             )
             source = t + NEW_TERM_COEF * rate + OLD_TERM_COEF * early_ref[j, lo:hi]
             rate_ref[j, lo:hi] = rate
-            source_ref[j, lo:hi] = source
             place = row_f + float(lo)
             to_end = to_end + jnp.sum(
                 jnp.exp(log_lam * ((rows - 1.0) - place)) * source, axis=0, keepdims=True
@@ -225,7 +224,7 @@
         (1, rows, cols), lambda g: (jnp.minimum(g * per_step + per_step, levels - 1), 0, 0)
     )
     smem = pl.BlockSpec(memory_space=pltpu.SMEM)
-    current_rate_change, linear_system_source, ends = pl.pallas_call(
+    current_rate_change, ends = pl.pallas_call(
         stencil_kernel,
         grid=(levels // per_step,),
         in_specs=[
@@ -248,16 +247,14 @@
         ],
         out_specs=[
             level((per_step, rows, cols)),
-            level((per_step, rows, cols)),
             pl.BlockSpec((parts, per_step, 2, cols), lambda g: (0, g, 0, 0)),
         ],
         out_shape=[
             jax.ShapeDtypeStruct(t.shape, f32),
-            jax.ShapeDtypeStruct(t.shape, f32),
             jax.ShapeDtypeStruct((parts, levels, 2, cols), f32),
         ],
         cost_estimate=pl.CostEstimate(
-            flops=100 * t.size, bytes_accessed=4 * 8 * t.size, transcendentals=2 * t.size
+            flops=100 * t.size, bytes_accessed=4 * 7 * t.size, transcendentals=2 * t.size
         ),
     )(
         layer_depth_spacing, backward_spread_ratio, t, t, t, horizontal_motion_pair,
@@ -265,6 +262,9 @@
         earlier_rate_change, wall_warmth_bounds,
         x_prev, x_next, y_prev, y_next,
     )
+    linear_system_source = (
+        t + NEW_TERM_COEF * current_rate_change + OLD_TERM_COEF * earlier_rate_change
+    )
     resulting_warmth_field = periodic_solve(linear_system_source, ends, log_lam, root)
     return (resulting_warmth_field, current_rate_change)
 

time: 44.4 us -> 44.2 us (level)
    unnamed x10 -> x14, local copies, waits for them, and re-layouts: 1.18 us -> 1.2 us
  transfers between devices with their start and end apart: 5 -> 5, of which waited for: 2 -> 2; matrix products, arithmetic and copies ran while one was open for 6% -> 7% of each run, Pallas kernels for 0% -> 0%
where the time goes in v8:
time: 44.2 us; the launch traced here: 43.4 us
  starting transfers between devices  18.2 us (41%)
  Pallas kernels  10.8 us (24%)
  waiting for transfers between devices  7.74 us (18%)
  matrix products  2.61 us (6%)
  other arithmetic  1.94 us (4%)
  local copies, waits for them, and re-layouts  1.4 us (3%)
  between operations  0.77 us (2%)
    all_to_all x1, starting transfers between devices, periodic_solve(): gathered = lax.all_to_all(ends, 'gx', 0, 0, tiled=True)  10.8 us
    pallas_call x1, Pallas kernels, on_device(): pl.pallas_call(stencil_kernel, grid=(levels // per_step,), in_specs=[smem...  7.95 us
    all_to_all x1, waiting for transfers between devices, periodic_solve(): gathered = lax.all_to_all(ends, 'gx', 0, 0, tiled=True)  6.3 us
    ppermute x2, starting transfers between devices, exchange_edges(): from_next = lax.ppermute(first, axis, ring_pairs(count, -1))  5.47 us
    pallas_call x1, Pallas kernels, on_device(): pl.pallas_call(edge_kernel, grid=(1,), in_specs=[whole((levels, rows, col...  2.82 us
    dot_general x1, matrix products, periodic_solve(): jnp.einsum('kij,kjc->kic', kernel, source, precision=lax.Precision.HIGHEST)  2.61 us
    ppermute x2, starting transfers between devices, exchange_edges(): from_prev = lax.ppermute(last, axis, ring_pairs(count, 1))  1.92 us
    div x1, other arithmetic, periodic_solve(): return total / root[:, None, None]  1.52 us
  transfers between devices with their start and end apart: 5, of which 2 were waited for; matrix products, arithmetic and copies ran while one was open for 7% of the time, Pallas kernels for 0%

profile of v8, /device:TPU:32, one launch (start us, length us, event | category | flops | bytes accessed | tf_op | source)
XLA Modules:
  0.0 43.4 jit_solution(17423290922766716892)
XLA Ops:
  0.6 0.0 copy-start.6
  0.6 2.8 %shard_map.86 = (f32[16,2,128]{2,1,0:T(2,128)}, f32[16,2,128]{2,1,0:T(2,128)}, f32[16,2,128]{2,1,0:T(2,128)}, f32[16,2,128]{2,1,0:T(2,128)}) custom-call(f32[16,128,128]{2,1,0:T(8,128)} %t_up_ref.1, f32[2,16,128,128]{3,2,1,0:T(8,128)} %v_ref.3, f32[2,16,128,128]{3,2,1,0:T(8,128)} %v_ref.3, f32[2,16,128,128]{3,2,1,0:T(8,128)} %v_ref.3), custom_call_target="tpu_custom_call" | custom-call | tf_op jit(solution)/shard_map/pallas_call | solution.py:195
  3.5 1.9 %collective-permute-start = (f32[16,2,128]{2,1,0:T(2,128)}, f32[16,2,128]{2,1,0:T(2,128)S(1)}, u32[]{:S(2)}, u32[]{:S(2)}) collective-permute-start(f32[16,2,128]{2,1,0:T(2,128)} %get-tuple-element.8), channel_id=1, source_target_pairs={{0,16},{16,32},{32,48},{48,64},{64,80},{80,96},{96,112},{112,128},... | collective-permute-start | bytes 49160 | tf_op jit(solution)/shard_map/ppermute | solution.py:21
  5.4 0.1 collective-permute-start.1
  5.5 0.0 collective-permute-start.2
  5.5 5.4 %collective-permute-start.3 = (f32[16,2,128]{2,1,0:T(2,128)}, f32[16,2,128]{2,1,0:T(2,128)S(1)}, u32[]{:S(2)}, u32[]{:S(2)}) collective-permute-start(f32[16,2,128]{2,1,0:T(2,128)} %get-tuple-element.11), channel_id=1, source_target_pairs={{0,15},{1,0},{2,1},{3,2},{4,3},{5,4},{6,5},{7,6},{8,7},{9,8},{10,9... | collective-permute-start | bytes 49160 | tf_op jit(solution)/shard_map/ppermute | solution.py:22
  10.9 0.0 copy-done.6
  10.9 0.1 exponential_divide_fusion.1
  11.0 0.0 copy-start
  11.0 0.0 copy-start.1
  11.0 0.0 collective-permute-done.x_prev_ref
  11.0 0.0 copy-start.2
  11.0 0.0 collective-permute-done.1.x_next_ref
  11.1 0.0 copy-start.3
  11.1 1.4 %collective-permute-done.2.y_prev_ref = f32[16,2,128]{2,1,0:T(2,128)S(1)} collective-permute-done((f32[16,2,128]{2,1,0:T(2,128)}, f32[16,2,128]{2,1,0:T(2,128)S(1)}, u32[]{:S(2)}, u32[]{:S(2)}) %collective-permute-start.2) | collective-permute-done | bytes 16416 | tf_op jit(solution)/shard_map/ppermute | solution.py:21
  12.5 0.0 copy-start.4
  12.5 0.0 collective-permute-done.3.y_next_ref
  12.5 0.0 copy-done.2
  12.5 0.0 copy-done.3
  12.5 0.6 %copy-done.4 = f32[16,2,128]{2,1,0:T(2,128)} copy-done((f32[16,2,128]{2,1,0:T(2,128)}, f32[16,2,128]{2,1,0:T(2,128)S(1)}, u32[]{:S(2)}) %copy-start.4) | copy-done | bytes 16408
  13.1 0.0 copy-start.5
  13.1 0.6 %copy-done.5 = f32[16,2,128]{2,1,0:T(2,128)} copy-done((f32[16,2,128]{2,1,0:T(2,128)}, f32[16,2,128]{2,1,0:T(2,128)S(1)}, u32[]{:S(2)}) %copy-start.5) | copy-done | bytes 16408
  13.7 7.9 %shard_map.87 = (f32[16,128,128]{2,1,0:T(8,128)}, f32[16,16,2,128]{3,2,1,0:T(2,128)}) custom-call(f32[16]{0:T(128)} %spacing_ref.1, f32[16]{0:T(128)} %ratio_ref.1, f32[16,128,128]{2,1,0:T(8,128)} %t_up_ref.1, f32[16,128,128]{2,1,0:T(8,128)} %t_up_ref.1, f32[16,128,128]{2,1,0:T(8,128)} %t_up_ref.1, f32[2,16,128,128]{3,2,1,0:T(8,128)} %v_ref.3, ...), custom_call_target="tpu_custom_call" | custom-call | flops 26214400 | bytes 7340032 | tf_op jit(solution)/shard_map/pallas_call | solution.py:227
  21.6 10.8 %all-to-all-start = ((f32[16,16,2,128]{3,2,1,0:T(2,128)}), f32[16,16,2,128]{3,2,1,0:T(2,128)S(1)}, u32[]{:S(2)}, u32[]{:S(2)}) async-start(f32[16,16,2,128]{3,2,1,0:T(2,128)} %get-tuple-element.13), calls=%async_computation | async-start | bytes 524288 | tf_op jit(solution)/shard_map/all_to_all | solution.py:37
  32.5 0.1 multiply_exponential_fusion.1
  32.6 0.0 copy-done
  32.6 0.0 copy-done.1
  32.6 2.6 %fusion = f32[16,128,128]{2,1,0:T(8,128)S(1)} fusion(f32[16,128,128]{2,1,0:T(8,128)S(1)} %copy-done.1, f32[16,128,128]{2,1,0:T(8,128)S(1)} %copy-done, f32[16,128,128]{2,1,0:T(8,128)} %get-tuple-element.7, f32[128,128]{1,0:T(8,128)S(1)} %subtract_abs_fusion, f32[16]{0:T(128)S(1)} %get-tuple-element.15), kind=kOutput, calls=%fused_computation.1 | convolution fusion | flops 403963904 | bytes 4259904 | tf_op jit(solution)/shard_map/kij,kjc->kic/dot_general | solution.py:42
  35.2 6.3 %all-to-all-done = f32[16,16,2,128]{3,2,1,0:T(2,128)S(1)} async-done(((f32[16,16,2,128]{3,2,1,0:T(2,128)}), f32[16,16,2,128]{3,2,1,0:T(2,128)S(1)}, u32[]{:S(2)}, u32[]{:S(2)}) %all-to-all-start) | async-done | bytes 262176 | tf_op jit(solution)/shard_map/all_to_all | solution.py:37
  41.5 0.2 fusion.19
  41.7 0.1 multiply_reduce_fusion.1
  41.8 0.1 multiply_reduce_fusion
  41.9 1.5 %add_divide_fusion = f32[16,128,128]{2,1,0:T(8,128)} fusion(f32[16,128,128]{2,1,0:T(8,128)S(1)} %fusion, f32[16]{0:T(128)S(1)} %get-tuple-element.22, f32[16,128]{1,0:T(8,128)S(1)} %multiply_reduce_fusion, f32[16,128]{1,0:T(8,128)S(1)} %get-tuple-element.21, f32[16,128]{1,0:T(8,128)S(1)} %multiply_reduce_fusion.1, f32[16,128]{1,0:T(8,128)S(1)} %get-tuple-element.20), kind=kLoop, calls=%fused_computation | loop fusion | flops 1310720 | bytes 2129984 | tf_op jit(solution)/shard_map/div | solution.py:60
  (4 shorter events, 0.1 us)
Async XLA Ops:
  0.6 10.2 %copy-start.6 = (f32[16]{0:T(128)S(1)}, f32[16]{0:T(128)}, u32[]{:S(2)}) copy-start(f32[16]{0:T(128)} %ratio_ref.1) | copy-start | bytes 196
  3.5 7.6 %collective-permute-start = (f32[16,2,128]{2,1,0:T(2,128)}, f32[16,2,128]{2,1,0:T(2,128)S(1)}, u32[]{:S(2)}, u32[]{:S(2)}) collective-permute-start(f32[16,2,128]{2,1,0:T(2,128)} %get-tuple-element.8), channel_id=1, source_target_pairs={{0,16},{16,32},{32,48},{48,64},{64,80},{80,96},{96,112},{112,128},... | collective-permute-start | bytes 49160 | tf_op jit(solution)/shard_map/ppermute | solution.py:21
  5.4 5.7 %collective-permute-start.1 = (f32[16,2,128]{2,1,0:T(2,128)}, f32[16,2,128]{2,1,0:T(2,128)S(1)}, u32[]{:S(2)}, u32[]{:S(2)}) collective-permute-start(f32[16,2,128]{2,1,0:T(2,128)} %get-tuple-element.9), channel_id=1, source_target_pairs={{0,240},{16,0},{32,16},{48,32},{64,48},{80,64},{96,80},{112,96},{1... | collective-permute-start | bytes 49160 | tf_op jit(solution)/shard_map/ppermute | solution.py:22
  5.5 7.0 %collective-permute-start.2 = (f32[16,2,128]{2,1,0:T(2,128)}, f32[16,2,128]{2,1,0:T(2,128)S(1)}, u32[]{:S(2)}, u32[]{:S(2)}) collective-permute-start(f32[16,2,128]{2,1,0:T(2,128)} %get-tuple-element.10), channel_id=1, source_target_pairs={{0,1},{1,2},{2,3},{3,4},{4,5},{5,6},{6,7},{7,8},{8,9},{9,10},{10,1... | collective-permute-start | bytes 49160 | tf_op jit(solution)/shard_map/ppermute | solution.py:21
  5.5 7.0 %collective-permute-start.3 = (f32[16,2,128]{2,1,0:T(2,128)}, f32[16,2,128]{2,1,0:T(2,128)S(1)}, u32[]{:S(2)}, u32[]{:S(2)}) collective-permute-start(f32[16,2,128]{2,1,0:T(2,128)} %get-tuple-element.11), channel_id=1, source_target_pairs={{0,15},{1,0},{2,1},{3,2},{4,3},{5,4},{6,5},{7,6},{8,7},{9,8},{10,9... | collective-permute-start | bytes 49160 | tf_op jit(solution)/shard_map/ppermute | solution.py:22
  11.0 21.6 %copy-start = (f32[16,128,128]{2,1,0:T(8,128)S(1)}, f32[16,128,128]{2,1,0:T(8,128)}, u32[]{:S(2)}) copy-start(f32[16,128,128]{2,1,0:T(8,128)} %t_up_ref.1) | copy-start | bytes 3145732
  11.0 21.6 %copy-start.1 = (f32[16,128,128]{2,1,0:T(8,128)S(1)}, f32[16,128,128]{2,1,0:T(8,128)}, u32[]{:S(2)}) copy-start(f32[16,128,128]{2,1,0:T(8,128)} %early_ref.1) | copy-start | bytes 3145732
  11.0 1.5 %copy-start.2 = (f32[16,2,128]{2,1,0:T(2,128)}, f32[16,2,128]{2,1,0:T(2,128)S(1)}, u32[]{:S(2)}) copy-start(f32[16,2,128]{2,1,0:T(2,128)S(1)} %collective-permute-done.x_prev_ref) | copy-start | bytes 49156
  11.1 1.4 %copy-start.3 = (f32[16,2,128]{2,1,0:T(2,128)}, f32[16,2,128]{2,1,0:T(2,128)S(1)}, u32[]{:S(2)}) copy-start(f32[16,2,128]{2,1,0:T(2,128)S(1)} %collective-permute-done.1.x_next_ref) | copy-start | bytes 49156
  12.5 0.6 %copy-start.4 = (f32[16,2,128]{2,1,0:T(2,128)}, f32[16,2,128]{2,1,0:T(2,128)S(1)}, u32[]{:S(2)}) copy-start(f32[16,2,128]{2,1,0:T(2,128)S(1)} %collective-permute-done.2.y_prev_ref) | copy-start | bytes 49156
  13.1 0.6 %copy-start.5 = (f32[16,2,128]{2,1,0:T(2,128)}, f32[16,2,128]{2,1,0:T(2,128)S(1)}, u32[]{:S(2)}) copy-start(f32[16,2,128]{2,1,0:T(2,128)S(1)} %collective-permute-done.3.y_next_ref) | copy-start | bytes 49156
  21.6 19.9 %all-to-all-start = ((f32[16,16,2,128]{3,2,1,0:T(2,128)}), f32[16,16,2,128]{3,2,1,0:T(2,128)S(1)}, u32[]{:S(2)}, u32[]{:S(2)}) async-start(f32[16,16,2,128]{3,2,1,0:T(2,128)} %get-tuple-element.13), calls=%async_computation | async-start | bytes 524288 | tf_op jit(solution)/shard_map/all_to_all | solution.py:37

commit v9 on v7

--- a/solution.py
+++ b/solution.py
@@ -130,17 +130,16 @@
             t_next_row = xn[0:1] if hi == rows else t_lvl[hi : hi + 1]
             u_next_row = xn[1:2] if hi == rows else u_lvl[hi : hi + 1]
             t_xn = jnp.where(row == chunk - 1, t_next_row, pltpu.roll(t, chunk - 1, 0))
-            t_xp = jnp.where(row == 0, t_prev_row, pltpu.roll(t, 1, 0))
             u_xn = jnp.where(row == chunk - 1, u_next_row, pltpu.roll(u, chunk - 1, 0))
-            u_xp = jnp.where(row == 0, u_prev_row, pltpu.roll(u, 1, 0))
             t_yn = jnp.where(col == cols - 1, yh[lo:hi, 2:3], pltpu.roll(t, cols - 1, 1))
             t_yp = jnp.where(col == 0, yh[lo:hi, 0:1], pltpu.roll(t, 1, 1))
             v_yn = jnp.where(col == cols - 1, yh[lo:hi, 3:4], pltpu.roll(v, cols - 1, 1))
-            v_yp = jnp.where(col == 0, yh[lo:hi, 1:2], pltpu.roll(v, 1, 1))
             flux_x_hi = (u + u_xn) * (t + t_xn) * 0.25
-            flux_x_lo = (u_xp + u) * (t_xp + t) * 0.25
+            face_x = (u_prev_row + u[0:1]) * (t_prev_row + t[0:1]) * 0.25
+            flux_x_lo = jnp.where(row == 0, face_x, pltpu.roll(flux_x_hi, 1, 0))
             flux_y_hi = (v + v_yn) * (t + t_yn) * 0.25
-            flux_y_lo = (v_yp + v) * (t_yp + t) * 0.25
+            face_y = (yh[lo:hi, 1:2] + v[:, 0:1]) * (yh[lo:hi, 0:1] + t[:, 0:1]) * 0.25
+            flux_y_lo = jnp.where(col == 0, face_y, pltpu.roll(flux_y_hi, 1, 1))
             advect_xy = (flux_x_hi - flux_x_lo) + (flux_y_hi - flux_y_lo)
 
             t_up = t_above[lo:hi]

time: 44.4 us -> 50.2 us (1.13)
  Pallas kernels: 10.9 us -> 16.8 us
    pallas_call x1, Pallas kernels: 8.08 us -> 14 us  [on_device(): pl.pallas_call(stencil_kernel, grid=(levels // per_step,), in_specs=[smem...]
  transfers between devices with their start and end apart: 5 -> 5, of which waited for: 2 -> 2; matrix products, arithmetic and copies ran while one was open for 6% -> 5% of each run, Pallas kernels for 0% -> 0%
where the time goes in v9:
time: 50.2 us; the launch traced here: 49.5 us
  starting transfers between devices  18.2 us (36%)
  Pallas kernels  16.8 us (33%)
  waiting for transfers between devices  7.9 us (16%)
  matrix products  2.5 us (5%)
  other arithmetic  1.94 us (4%)
  local copies, waits for them, and re-layouts  1.39 us (3%)
  between operations  0.74 us (1%)
    pallas_call x1, Pallas kernels, on_device(): pl.pallas_call(stencil_kernel, grid=(levels // per_step,), in_specs=[smem...  14 us
    all_to_all x1, starting transfers between devices, periodic_solve(): gathered = lax.all_to_all(ends, 'gx', 0, 0, tiled=True)  10.8 us
    all_to_all x1, waiting for transfers between devices, periodic_solve(): gathered = lax.all_to_all(ends, 'gx', 0, 0, tiled=True)  6.47 us
    ppermute x2, starting transfers between devices, exchange_edges(): from_next = lax.ppermute(first, axis, ring_pairs(count, -1))  5.47 us
    pallas_call x1, Pallas kernels, on_device(): pl.pallas_call(edge_kernel, grid=(1,), in_specs=[whole((levels, rows, col...  2.81 us
    dot_general x1, matrix products, periodic_solve(): jnp.einsum('kij,kjc->kic', kernel, source, precision=lax.Precision.HIGHEST)  2.5 us
    ppermute x2, starting transfers between devices, exchange_edges(): from_prev = lax.ppermute(last, axis, ring_pairs(count, 1))  1.92 us
    div x1, other arithmetic, periodic_solve(): return total / root[:, None, None]  1.52 us
  transfers between devices with their start and end apart: 5, of which 2 were waited for; matrix products, arithmetic and copies ran while one was open for 5% of the time, Pallas kernels for 0%

profile of v9, /device:TPU:32, one launch (start us, length us, event | category | flops | bytes accessed | tf_op | source)
XLA Modules:
  0.0 49.5 jit_solution(18033966334817103061)
XLA Ops:
  0.6 0.0 copy-start.4
  0.6 2.8 %shard_map.86 = (f32[16,2,128]{2,1,0:T(2,128)}, f32[16,2,128]{2,1,0:T(2,128)}, f32[16,2,128]{2,1,0:T(2,128)}, f32[16,2,128]{2,1,0:T(2,128)}) custom-call(f32[16,128,128]{2,1,0:T(8,128)} %t_up_ref.1, f32[2,16,128,128]{3,2,1,0:T(8,128)} %v_ref.3, f32[2,16,128,128]{3,2,1,0:T(8,128)} %v_ref.3, f32[2,16,128,128]{3,2,1,0:T(8,128)} %v_ref.3), custom_call_target="tpu_custom_call" | custom-call | tf_op jit(solution)/shard_map/pallas_call | solution.py:195
  3.5 1.9 %collective-permute-start = (f32[16,2,128]{2,1,0:T(2,128)}, f32[16,2,128]{2,1,0:T(2,128)S(1)}, u32[]{:S(2)}, u32[]{:S(2)}) collective-permute-start(f32[16,2,128]{2,1,0:T(2,128)} %get-tuple-element.9), channel_id=1, source_target_pairs={{0,16},{16,32},{32,48},{48,64},{64,80},{80,96},{96,112},{112,128},... | collective-permute-start | bytes 49160 | tf_op jit(solution)/shard_map/ppermute | solution.py:21
  5.4 0.1 collective-permute-start.1
  5.5 0.0 collective-permute-start.2
  5.5 5.4 %collective-permute-start.3 = (f32[16,2,128]{2,1,0:T(2,128)}, f32[16,2,128]{2,1,0:T(2,128)S(1)}, u32[]{:S(2)}, u32[]{:S(2)}) collective-permute-start(f32[16,2,128]{2,1,0:T(2,128)} %get-tuple-element.12), channel_id=1, source_target_pairs={{0,15},{1,0},{2,1},{3,2},{4,3},{5,4},{6,5},{7,6},{8,7},{9,8},{10,9... | collective-permute-start | bytes 49160 | tf_op jit(solution)/shard_map/ppermute | solution.py:22
  10.9 0.0 copy-done.4
  10.9 0.1 exponential_divide_fusion.1
  11.0 0.0 collective-permute-done.x_prev_ref
  11.0 0.0 copy-start
  11.1 0.0 collective-permute-done.1.x_next_ref
  11.1 0.0 copy-start.1
  11.1 1.4 %collective-permute-done.2.y_prev_ref = f32[16,2,128]{2,1,0:T(2,128)S(1)} collective-permute-done((f32[16,2,128]{2,1,0:T(2,128)}, f32[16,2,128]{2,1,0:T(2,128)S(1)}, u32[]{:S(2)}, u32[]{:S(2)}) %collective-permute-start.2) | collective-permute-done | bytes 16416 | tf_op jit(solution)/shard_map/ppermute | solution.py:21
  12.5 0.0 copy-start.2
  12.5 0.0 collective-permute-done.3.y_next_ref
  12.5 0.0 copy-done
  12.5 0.0 copy-done.1
  12.5 0.6 %copy-done.2 = f32[16,2,128]{2,1,0:T(2,128)} copy-done((f32[16,2,128]{2,1,0:T(2,128)}, f32[16,2,128]{2,1,0:T(2,128)S(1)}, u32[]{:S(2)}) %copy-start.2) | copy-done | bytes 16408
  13.1 0.0 copy-start.3
  13.1 0.6 %copy-done.3 = f32[16,2,128]{2,1,0:T(2,128)} copy-done((f32[16,2,128]{2,1,0:T(2,128)}, f32[16,2,128]{2,1,0:T(2,128)S(1)}, u32[]{:S(2)}) %copy-start.3) | copy-done | bytes 16408
  13.7 14.0 %shard_map.87 = (f32[16,128,128]{2,1,0:T(8,128)}, f32[16,128,128]{2,1,0:T(8,128)}, f32[16,16,2,128]{3,2,1,0:T(2,128)}) custom-call(f32[16]{0:T(128)} %spacing_ref.1, f32[16]{0:T(128)} %ratio_ref.1, f32[16,128,128]{2,1,0:T(8,128)} %t_up_ref.1, f32[16,128,128]{2,1,0:T(8,128)} %t_up_ref.1, f32[16,128,128]{2,1,0:T(8,128)} %t_up_ref.1, ...), custom_call_target="tpu_custom_call" | custom-call | flops 26214400 | bytes 8388608 | tf_op jit(solution)/shard_map/pallas_call | solution.py:227
  27.7 10.8 %all-to-all-start = ((f32[16,16,2,128]{3,2,1,0:T(2,128)}), f32[16,16,2,128]{3,2,1,0:T(2,128)S(1)}, u32[]{:S(2)}, u32[]{:S(2)}) async-start(f32[16,16,2,128]{3,2,1,0:T(2,128)} %get-tuple-element.14), calls=%async_computation | async-start | bytes 524288 | tf_op jit(solution)/shard_map/all_to_all | solution.py:37
  38.5 0.1 multiply_exponential_fusion.1
  38.6 2.5 %fusion = f32[16,128,128]{2,1,0:T(8,128)S(1)} fusion(f32[16,128,128]{2,1,0:T(8,128)} %get-tuple-element.13, f32[128,128]{1,0:T(8,128)S(1)} %subtract_abs_fusion, f32[16]{0:T(128)S(1)} %get-tuple-element.17), kind=kOutput, calls=%fused_computation.1 | convolution fusion | flops 402915328 | bytes 2162752 | tf_op jit(solution)/shard_map/kij,kjc->kic/dot_general | solution.py:42
  41.1 6.5 %all-to-all-done = f32[16,16,2,128]{3,2,1,0:T(2,128)S(1)} async-done(((f32[16,16,2,128]{3,2,1,0:T(2,128)}), f32[16,16,2,128]{3,2,1,0:T(2,128)S(1)}, u32[]{:S(2)}, u32[]{:S(2)}) %all-to-all-start) | async-done | bytes 262176 | tf_op jit(solution)/shard_map/all_to_all | solution.py:37
  47.6 0.2 fusion.11
  47.8 0.1 multiply_reduce_fusion
  47.9 0.1 multiply_reduce_fusion.1
  48.0 1.5 %add_divide_fusion = f32[16,128,128]{2,1,0:T(8,128)} fusion(f32[16,128,128]{2,1,0:T(8,128)S(1)} %fusion, f32[16]{0:T(128)S(1)} %get-tuple-element.24, f32[16,128]{1,0:T(8,128)S(1)} %multiply_reduce_fusion, f32[16,128]{1,0:T(8,128)S(1)} %get-tuple-element.23, f32[16,128]{1,0:T(8,128)S(1)} %multiply_reduce_fusion.1, f32[16,128]{1,0:T(8,128)S(1)} %get-tuple-element.22), kind=kLoop, calls=%fused_computation | loop fusion | flops 1310720 | bytes 2129984 | tf_op jit(solution)/shard_map/div | solution.py:60
  (4 shorter events, 0.1 us)
Async XLA Ops:
  0.6 10.2 %copy-start.4 = (f32[16]{0:T(128)S(1)}, f32[16]{0:T(128)}, u32[]{:S(2)}) copy-start(f32[16]{0:T(128)} %ratio_ref.1) | copy-start | bytes 196
  3.5 7.6 %collective-permute-start = (f32[16,2,128]{2,1,0:T(2,128)}, f32[16,2,128]{2,1,0:T(2,128)S(1)}, u32[]{:S(2)}, u32[]{:S(2)}) collective-permute-start(f32[16,2,128]{2,1,0:T(2,128)} %get-tuple-element.9), channel_id=1, source_target_pairs={{0,16},{16,32},{32,48},{48,64},{64,80},{80,96},{96,112},{112,128},... | collective-permute-start | bytes 49160 | tf_op jit(solution)/shard_map/ppermute | solution.py:21
  5.4 5.7 %collective-permute-start.1 = (f32[16,2,128]{2,1,0:T(2,128)}, f32[16,2,128]{2,1,0:T(2,128)S(1)}, u32[]{:S(2)}, u32[]{:S(2)}) collective-permute-start(f32[16,2,128]{2,1,0:T(2,128)} %get-tuple-element.10), channel_id=1, source_target_pairs={{0,240},{16,0},{32,16},{48,32},{64,48},{80,64},{96,80},{112,96},{1... | collective-permute-start | bytes 49160 | tf_op jit(solution)/shard_map/ppermute | solution.py:22
  5.5 7.0 %collective-permute-start.2 = (f32[16,2,128]{2,1,0:T(2,128)}, f32[16,2,128]{2,1,0:T(2,128)S(1)}, u32[]{:S(2)}, u32[]{:S(2)}) collective-permute-start(f32[16,2,128]{2,1,0:T(2,128)} %get-tuple-element.11), channel_id=1, source_target_pairs={{0,1},{1,2},{2,3},{3,4},{4,5},{5,6},{6,7},{7,8},{8,9},{9,10},{10,1... | collective-permute-start | bytes 49160 | tf_op jit(solution)/shard_map/ppermute | solution.py:21
  5.5 7.0 %collective-permute-start.3 = (f32[16,2,128]{2,1,0:T(2,128)}, f32[16,2,128]{2,1,0:T(2,128)S(1)}, u32[]{:S(2)}, u32[]{:S(2)}) collective-permute-start(f32[16,2,128]{2,1,0:T(2,128)} %get-tuple-element.12), channel_id=1, source_target_pairs={{0,15},{1,0},{2,1},{3,2},{4,3},{5,4},{6,5},{7,6},{8,7},{9,8},{10,9... | collective-permute-start | bytes 49160 | tf_op jit(solution)/shard_map/ppermute | solution.py:22
  11.0 1.5 %copy-start = (f32[16,2,128]{2,1,0:T(2,128)}, f32[16,2,128]{2,1,0:T(2,128)S(1)}, u32[]{:S(2)}) copy-start(f32[16,2,128]{2,1,0:T(2,128)S(1)} %collective-permute-done.x_prev_ref) | copy-start | bytes 49156
  11.1 1.4 %copy-start.1 = (f32[16,2,128]{2,1,0:T(2,128)}, f32[16,2,128]{2,1,0:T(2,128)S(1)}, u32[]{:S(2)}) copy-start(f32[16,2,128]{2,1,0:T(2,128)S(1)} %collective-permute-done.1.x_next_ref) | copy-start | bytes 49156
  12.5 0.6 %copy-start.2 = (f32[16,2,128]{2,1,0:T(2,128)}, f32[16,2,128]{2,1,0:T(2,128)S(1)}, u32[]{:S(2)}) copy-start(f32[16,2,128]{2,1,0:T(2,128)S(1)} %collective-permute-done.2.y_prev_ref) | copy-start | bytes 49156
  13.1 0.6 %copy-start.3 = (f32[16,2,128]{2,1,0:T(2,128)}, f32[16,2,128]{2,1,0:T(2,128)S(1)}, u32[]{:S(2)}) copy-start(f32[16,2,128]{2,1,0:T(2,128)S(1)} %collective-permute-done.3.y_next_ref) | copy-start | bytes 49156
  27.7 19.9 %all-to-all-start = ((f32[16,16,2,128]{3,2,1,0:T(2,128)}), f32[16,16,2,128]{3,2,1,0:T(2,128)S(1)}, u32[]{:S(2)}, u32[]{:S(2)}) async-start(f32[16,16,2,128]{3,2,1,0:T(2,128)} %get-tuple-element.14), calls=%async_computation | async-start | bytes 524288 | tf_op jit(solution)/shard_map/all_to_all | solution.py:37

commit v10 on v9

--- a/solution.py
+++ b/solution.py
@@ -134,12 +134,12 @@
             t_yn = jnp.where(col == cols - 1, yh[lo:hi, 2:3], pltpu.roll(t, cols - 1, 1))
             t_yp = jnp.where(col == 0, yh[lo:hi, 0:1], pltpu.roll(t, 1, 1))
             v_yn = jnp.where(col == cols - 1, yh[lo:hi, 3:4], pltpu.roll(v, cols - 1, 1))
+            v_yp = jnp.where(col == 0, yh[lo:hi, 1:2], pltpu.roll(v, 1, 1))
             flux_x_hi = (u + u_xn) * (t + t_xn) * 0.25
             face_x = (u_prev_row + u[0:1]) * (t_prev_row + t[0:1]) * 0.25
             flux_x_lo = jnp.where(row == 0, face_x, pltpu.roll(flux_x_hi, 1, 0))
             flux_y_hi = (v + v_yn) * (t + t_yn) * 0.25
-            face_y = (yh[lo:hi, 1:2] + v[:, 0:1]) * (yh[lo:hi, 0:1] + t[:, 0:1]) * 0.25
-            flux_y_lo = jnp.where(col == 0, face_y, pltpu.roll(flux_y_hi, 1, 1))
+            flux_y_lo = (v_yp + v) * (t_yp + t) * 0.25
             advect_xy = (flux_x_hi - flux_x_lo) + (flux_y_hi - flux_y_lo)
 
             t_up = t_above[lo:hi]

time: 50.2 us -> 44.2 us (0.88)
  Pallas kernels: 16.8 us -> 10.7 us
    pallas_call x1, Pallas kernels: 14 us -> 7.89 us  [on_device(): pl.pallas_call(stencil_kernel, grid=(levels // per_step,), in_specs=[smem...]
  transfers between devices with their start and end apart: 5 -> 5, of which waited for: 2 -> 2; matrix products, arithmetic and copies ran while one was open for 5% -> 6% of each run, Pallas kernels for 0% -> 0%
where the time goes in v10:
time: 44.2 us; the launch traced here: 43.4 us
  starting transfers between devices  18.2 us (41%)
  Pallas kernels  10.7 us (24%)
  waiting for transfers between devices  7.9 us (18%)
  matrix products  2.5 us (6%)
  other arithmetic  1.94 us (4%)
  local copies, waits for them, and re-layouts  1.39 us (3%)
  between operations  0.74 us (2%)
    all_to_all x1, starting transfers between devices, periodic_solve(): gathered = lax.all_to_all(ends, 'gx', 0, 0, tiled=True)  10.8 us
    pallas_call x1, Pallas kernels, on_device(): pl.pallas_call(stencil_kernel, grid=(levels // per_step,), in_specs=[smem...  7.89 us
    all_to_all x1, waiting for transfers between devices, periodic_solve(): gathered = lax.all_to_all(ends, 'gx', 0, 0, tiled=True)  6.47 us
    ppermute x2, starting transfers between devices, exchange_edges(): from_next = lax.ppermute(first, axis, ring_pairs(count, -1))  5.47 us
    pallas_call x1, Pallas kernels, on_device(): pl.pallas_call(edge_kernel, grid=(1,), in_specs=[whole((levels, rows, col...  2.81 us
    dot_general x1, matrix products, periodic_solve(): jnp.einsum('kij,kjc->kic', kernel, source, precision=lax.Precision.HIGHEST)  2.5 us
    ppermute x2, starting transfers between devices, exchange_edges(): from_prev = lax.ppermute(last, axis, ring_pairs(count, 1))  1.92 us
    div x1, other arithmetic, periodic_solve(): return total / root[:, None, None]  1.52 us
  transfers between devices with their start and end apart: 5, of which 2 were waited for; matrix products, arithmetic and copies ran while one was open for 6% of the time, Pallas kernels for 0%

profile of v10, /device:TPU:32, one launch (start us, length us, event | category | flops | bytes accessed | tf_op | source)
XLA Modules:
  0.0 43.4 jit_solution(116718101471971759)
XLA Ops:
  0.6 0.0 copy-start.4
  0.6 2.8 %shard_map.86 = (f32[16,2,128]{2,1,0:T(2,128)}, f32[16,2,128]{2,1,0:T(2,128)}, f32[16,2,128]{2,1,0:T(2,128)}, f32[16,2,128]{2,1,0:T(2,128)}) custom-call(f32[16,128,128]{2,1,0:T(8,128)} %t_up_ref.1, f32[2,16,128,128]{3,2,1,0:T(8,128)} %v_ref.3, f32[2,16,128,128]{3,2,1,0:T(8,128)} %v_ref.3, f32[2,16,128,128]{3,2,1,0:T(8,128)} %v_ref.3), custom_call_target="tpu_custom_call" | custom-call | tf_op jit(solution)/shard_map/pallas_call | solution.py:195
  3.5 1.9 %collective-permute-start = (f32[16,2,128]{2,1,0:T(2,128)}, f32[16,2,128]{2,1,0:T(2,128)S(1)}, u32[]{:S(2)}, u32[]{:S(2)}) collective-permute-start(f32[16,2,128]{2,1,0:T(2,128)} %get-tuple-element.9), channel_id=1, source_target_pairs={{0,16},{16,32},{32,48},{48,64},{64,80},{80,96},{96,112},{112,128},... | collective-permute-start | bytes 49160 | tf_op jit(solution)/shard_map/ppermute | solution.py:21
  5.4 0.1 collective-permute-start.1
  5.5 0.0 collective-permute-start.2
  5.5 5.4 %collective-permute-start.3 = (f32[16,2,128]{2,1,0:T(2,128)}, f32[16,2,128]{2,1,0:T(2,128)S(1)}, u32[]{:S(2)}, u32[]{:S(2)}) collective-permute-start(f32[16,2,128]{2,1,0:T(2,128)} %get-tuple-element.12), channel_id=1, source_target_pairs={{0,15},{1,0},{2,1},{3,2},{4,3},{5,4},{6,5},{7,6},{8,7},{9,8},{10,9... | collective-permute-start | bytes 49160 | tf_op jit(solution)/shard_map/ppermute | solution.py:22
  10.9 0.0 copy-done.4
  10.9 0.1 exponential_divide_fusion.1
  11.0 0.0 collective-permute-done.x_prev_ref
  11.0 0.0 copy-start
  11.1 0.0 collective-permute-done.1.x_next_ref
  11.1 0.0 copy-start.1
  11.1 1.4 %collective-permute-done.2.y_prev_ref = f32[16,2,128]{2,1,0:T(2,128)S(1)} collective-permute-done((f32[16,2,128]{2,1,0:T(2,128)}, f32[16,2,128]{2,1,0:T(2,128)S(1)}, u32[]{:S(2)}, u32[]{:S(2)}) %collective-permute-start.2) | collective-permute-done | bytes 16416 | tf_op jit(solution)/shard_map/ppermute | solution.py:21
  12.5 0.0 copy-start.2
  12.5 0.0 collective-permute-done.3.y_next_ref
  12.5 0.0 copy-done
  12.5 0.0 copy-done.1
  12.5 0.6 %copy-done.2 = f32[16,2,128]{2,1,0:T(2,128)} copy-done((f32[16,2,128]{2,1,0:T(2,128)}, f32[16,2,128]{2,1,0:T(2,128)S(1)}, u32[]{:S(2)}) %copy-start.2) | copy-done | bytes 16408
  13.1 0.0 copy-start.3
  13.1 0.6 %copy-done.3 = f32[16,2,128]{2,1,0:T(2,128)} copy-done((f32[16,2,128]{2,1,0:T(2,128)}, f32[16,2,128]{2,1,0:T(2,128)S(1)}, u32[]{:S(2)}) %copy-start.3) | copy-done | bytes 16408
  13.7 7.9 %shard_map.87 = (f32[16,128,128]{2,1,0:T(8,128)}, f32[16,128,128]{2,1,0:T(8,128)}, f32[16,16,2,128]{3,2,1,0:T(2,128)}) custom-call(f32[16]{0:T(128)} %spacing_ref.1, f32[16]{0:T(128)} %ratio_ref.1, f32[16,128,128]{2,1,0:T(8,128)} %t_up_ref.1, f32[16,128,128]{2,1,0:T(8,128)} %t_up_ref.1, f32[16,128,128]{2,1,0:T(8,128)} %t_up_ref.1, ...), custom_call_target="tpu_custom_call" | custom-call | flops 26214400 | bytes 8388608 | tf_op jit(solution)/shard_map/pallas_call | solution.py:227
  21.6 10.8 %all-to-all-start = ((f32[16,16,2,128]{3,2,1,0:T(2,128)}), f32[16,16,2,128]{3,2,1,0:T(2,128)S(1)}, u32[]{:S(2)}, u32[]{:S(2)}) async-start(f32[16,16,2,128]{3,2,1,0:T(2,128)} %get-tuple-element.14), calls=%async_computation | async-start | bytes 524288 | tf_op jit(solution)/shard_map/all_to_all | solution.py:37
  32.4 0.1 multiply_exponential_fusion.1
  32.5 2.5 %fusion = f32[16,128,128]{2,1,0:T(8,128)S(1)} fusion(f32[16,128,128]{2,1,0:T(8,128)} %get-tuple-element.13, f32[128,128]{1,0:T(8,128)S(1)} %subtract_abs_fusion, f32[16]{0:T(128)S(1)} %get-tuple-element.17), kind=kOutput, calls=%fused_computation.1 | convolution fusion | flops 402915328 | bytes 2162752 | tf_op jit(solution)/shard_map/kij,kjc->kic/dot_general | solution.py:42
  35.0 6.5 %all-to-all-done = f32[16,16,2,128]{3,2,1,0:T(2,128)S(1)} async-done(((f32[16,16,2,128]{3,2,1,0:T(2,128)}), f32[16,16,2,128]{3,2,1,0:T(2,128)S(1)}, u32[]{:S(2)}, u32[]{:S(2)}) %all-to-all-start) | async-done | bytes 262176 | tf_op jit(solution)/shard_map/all_to_all | solution.py:37
  41.4 0.2 fusion.11
  41.6 0.1 multiply_reduce_fusion
  41.7 0.1 multiply_reduce_fusion.1
  41.8 1.5 %add_divide_fusion = f32[16,128,128]{2,1,0:T(8,128)} fusion(f32[16,128,128]{2,1,0:T(8,128)S(1)} %fusion, f32[16]{0:T(128)S(1)} %get-tuple-element.24, f32[16,128]{1,0:T(8,128)S(1)} %multiply_reduce_fusion, f32[16,128]{1,0:T(8,128)S(1)} %get-tuple-element.23, f32[16,128]{1,0:T(8,128)S(1)} %multiply_reduce_fusion.1, f32[16,128]{1,0:T(8,128)S(1)} %get-tuple-element.22), kind=kLoop, calls=%fused_computation | loop fusion | flops 1310720 | bytes 2129984 | tf_op jit(solution)/shard_map/div | solution.py:60
  (4 shorter events, 0.1 us)
Async XLA Ops:
  0.6 10.2 %copy-start.4 = (f32[16]{0:T(128)S(1)}, f32[16]{0:T(128)}, u32[]{:S(2)}) copy-start(f32[16]{0:T(128)} %ratio_ref.1) | copy-start | bytes 196
  3.5 7.6 %collective-permute-start = (f32[16,2,128]{2,1,0:T(2,128)}, f32[16,2,128]{2,1,0:T(2,128)S(1)}, u32[]{:S(2)}, u32[]{:S(2)}) collective-permute-start(f32[16,2,128]{2,1,0:T(2,128)} %get-tuple-element.9), channel_id=1, source_target_pairs={{0,16},{16,32},{32,48},{48,64},{64,80},{80,96},{96,112},{112,128},... | collective-permute-start | bytes 49160 | tf_op jit(solution)/shard_map/ppermute | solution.py:21
  5.4 5.7 %collective-permute-start.1 = (f32[16,2,128]{2,1,0:T(2,128)}, f32[16,2,128]{2,1,0:T(2,128)S(1)}, u32[]{:S(2)}, u32[]{:S(2)}) collective-permute-start(f32[16,2,128]{2,1,0:T(2,128)} %get-tuple-element.10), channel_id=1, source_target_pairs={{0,240},{16,0},{32,16},{48,32},{64,48},{80,64},{96,80},{112,96},{1... | collective-permute-start | bytes 49160 | tf_op jit(solution)/shard_map/ppermute | solution.py:22
  5.5 7.0 %collective-permute-start.2 = (f32[16,2,128]{2,1,0:T(2,128)}, f32[16,2,128]{2,1,0:T(2,128)S(1)}, u32[]{:S(2)}, u32[]{:S(2)}) collective-permute-start(f32[16,2,128]{2,1,0:T(2,128)} %get-tuple-element.11), channel_id=1, source_target_pairs={{0,1},{1,2},{2,3},{3,4},{4,5},{5,6},{6,7},{7,8},{8,9},{9,10},{10,1... | collective-permute-start | bytes 49160 | tf_op jit(solution)/shard_map/ppermute | solution.py:21
  5.5 7.0 %collective-permute-start.3 = (f32[16,2,128]{2,1,0:T(2,128)}, f32[16,2,128]{2,1,0:T(2,128)S(1)}, u32[]{:S(2)}, u32[]{:S(2)}) collective-permute-start(f32[16,2,128]{2,1,0:T(2,128)} %get-tuple-element.12), channel_id=1, source_target_pairs={{0,15},{1,0},{2,1},{3,2},{4,3},{5,4},{6,5},{7,6},{8,7},{9,8},{10,9... | collective-permute-start | bytes 49160 | tf_op jit(solution)/shard_map/ppermute | solution.py:22
  11.0 1.5 %copy-start = (f32[16,2,128]{2,1,0:T(2,128)}, f32[16,2,128]{2,1,0:T(2,128)S(1)}, u32[]{:S(2)}) copy-start(f32[16,2,128]{2,1,0:T(2,128)S(1)} %collective-permute-done.x_prev_ref) | copy-start | bytes 49156
  11.1 1.4 %copy-start.1 = (f32[16,2,128]{2,1,0:T(2,128)}, f32[16,2,128]{2,1,0:T(2,128)S(1)}, u32[]{:S(2)}) copy-start(f32[16,2,128]{2,1,0:T(2,128)S(1)} %collective-permute-done.1.x_next_ref) | copy-start | bytes 49156
  12.5 0.6 %copy-start.2 = (f32[16,2,128]{2,1,0:T(2,128)}, f32[16,2,128]{2,1,0:T(2,128)S(1)}, u32[]{:S(2)}) copy-start(f32[16,2,128]{2,1,0:T(2,128)S(1)} %collective-permute-done.2.y_prev_ref) | copy-start | bytes 49156
  13.1 0.6 %copy-start.3 = (f32[16,2,128]{2,1,0:T(2,128)}, f32[16,2,128]{2,1,0:T(2,128)S(1)}, u32[]{:S(2)}) copy-start(f32[16,2,128]{2,1,0:T(2,128)S(1)} %collective-permute-done.3.y_next_ref) | copy-start | bytes 49156
  21.6 19.9 %all-to-all-start = ((f32[16,16,2,128]{3,2,1,0:T(2,128)}), f32[16,16,2,128]{3,2,1,0:T(2,128)S(1)}, u32[]{:S(2)}, u32[]{:S(2)}) async-start(f32[16,16,2,128]{3,2,1,0:T(2,128)} %get-tuple-element.14), calls=%async_computation | async-start | bytes 524288 | tf_op jit(solution)/shard_map/all_to_all | solution.py:37

commit v11 on v7

--- a/solution.py
+++ b/solution.py
@@ -214,7 +214,7 @@
     y_prev, y_next = exchange_edges(y_first, y_last, "gy")
 
     log_lam, root = spread_root(backward_spread_ratio)
-    per_step = 4 if levels % 4 == 0 else 1
+    per_step = 8 if levels % 8 == 0 else 1
     level = lambda shape: pl.BlockSpec(shape, lambda g: (g,) + (0,) * (len(shape) - 1))
     parts = lax.axis_size("gx")
     vmem = pl.BlockSpec(memory_space=pltpu.VMEM)

time: 44.4 us -> 44.6 us (level)
  no operation moved by 1% of the time
where the time goes in v11:
time: 44.6 us; the launch traced here: 43.8 us
  starting transfers between devices  18.2 us (41%)
  Pallas kernels  11.2 us (25%)
  waiting for transfers between devices  7.9 us (18%)
  matrix products  2.5 us (6%)
  other arithmetic  1.94 us (4%)
  local copies, waits for them, and re-layouts  1.39 us (3%)
  between operations  0.74 us (2%)
    all_to_all x1, starting transfers between devices, periodic_solve(): gathered = lax.all_to_all(ends, 'gx', 0, 0, tiled=True)  10.8 us
    pallas_call x1, Pallas kernels, on_device(): pl.pallas_call(stencil_kernel, grid=(levels // per_step,), in_specs=[smem...  8.36 us
    all_to_all x1, waiting for transfers between devices, periodic_solve(): gathered = lax.all_to_all(ends, 'gx', 0, 0, tiled=True)  6.47 us
    ppermute x2, starting transfers between devices, exchange_edges(): from_next = lax.ppermute(first, axis, ring_pairs(count, -1))  5.47 us
    pallas_call x1, Pallas kernels, on_device(): pl.pallas_call(edge_kernel, grid=(1,), in_specs=[whole((levels, rows, col...  2.81 us
    dot_general x1, matrix products, periodic_solve(): jnp.einsum('kij,kjc->kic', kernel, source, precision=lax.Precision.HIGHEST)  2.5 us
    ppermute x2, starting transfers between devices, exchange_edges(): from_prev = lax.ppermute(last, axis, ring_pairs(count, 1))  1.92 us
    div x1, other arithmetic, periodic_solve(): return total / root[:, None, None]  1.52 us
  transfers between devices with their start and end apart: 5, of which 2 were waited for; matrix products, arithmetic and copies ran while one was open for 6% of the time, Pallas kernels for 0%

profile of v11, /device:TPU:32, one launch (start us, length us, event | category | flops | bytes accessed | tf_op | source)
XLA Modules:
  0.0 43.8 jit_solution(8985410342499029045)
XLA Ops:
  0.6 0.0 copy-start.4
  0.6 2.8 %shard_map.86 = (f32[16,2,128]{2,1,0:T(2,128)}, f32[16,2,128]{2,1,0:T(2,128)}, f32[16,2,128]{2,1,0:T(2,128)}, f32[16,2,128]{2,1,0:T(2,128)}) custom-call(f32[16,128,128]{2,1,0:T(8,128)} %t_up_ref.1, f32[2,16,128,128]{3,2,1,0:T(8,128)} %v_ref.3, f32[2,16,128,128]{3,2,1,0:T(8,128)} %v_ref.3, f32[2,16,128,128]{3,2,1,0:T(8,128)} %v_ref.3), custom_call_target="tpu_custom_call" | custom-call | tf_op jit(solution)/shard_map/pallas_call | solution.py:196
  3.5 1.9 %collective-permute-start = (f32[16,2,128]{2,1,0:T(2,128)}, f32[16,2,128]{2,1,0:T(2,128)S(1)}, u32[]{:S(2)}, u32[]{:S(2)}) collective-permute-start(f32[16,2,128]{2,1,0:T(2,128)} %get-tuple-element.9), channel_id=1, source_target_pairs={{0,16},{16,32},{32,48},{48,64},{64,80},{80,96},{96,112},{112,128},... | collective-permute-start | bytes 49160 | tf_op jit(solution)/shard_map/ppermute | solution.py:21
  5.4 0.1 collective-permute-start.1
  5.5 0.0 collective-permute-start.2
  5.5 5.4 %collective-permute-start.3 = (f32[16,2,128]{2,1,0:T(2,128)}, f32[16,2,128]{2,1,0:T(2,128)S(1)}, u32[]{:S(2)}, u32[]{:S(2)}) collective-permute-start(f32[16,2,128]{2,1,0:T(2,128)} %get-tuple-element.12), channel_id=1, source_target_pairs={{0,15},{1,0},{2,1},{3,2},{4,3},{5,4},{6,5},{7,6},{8,7},{9,8},{10,9... | collective-permute-start | bytes 49160 | tf_op jit(solution)/shard_map/ppermute | solution.py:22
  10.9 0.0 copy-done.4
  10.9 0.1 exponential_divide_fusion.1
  11.0 0.0 collective-permute-done.x_prev_ref
  11.0 0.0 copy-start
  11.1 0.0 collective-permute-done.1.x_next_ref
  11.1 0.0 copy-start.1
  11.1 1.4 %collective-permute-done.2.y_prev_ref = f32[16,2,128]{2,1,0:T(2,128)S(1)} collective-permute-done((f32[16,2,128]{2,1,0:T(2,128)}, f32[16,2,128]{2,1,0:T(2,128)S(1)}, u32[]{:S(2)}, u32[]{:S(2)}) %collective-permute-start.2) | collective-permute-done | bytes 16416 | tf_op jit(solution)/shard_map/ppermute | solution.py:21
  12.5 0.0 copy-start.2
  12.5 0.0 collective-permute-done.3.y_next_ref
  12.5 0.0 copy-done
  12.5 0.0 copy-done.1
  12.5 0.6 %copy-done.2 = f32[16,2,128]{2,1,0:T(2,128)} copy-done((f32[16,2,128]{2,1,0:T(2,128)}, f32[16,2,128]{2,1,0:T(2,128)S(1)}, u32[]{:S(2)}) %copy-start.2) | copy-done | bytes 16408
  13.1 0.0 copy-start.3
  13.1 0.6 %copy-done.3 = f32[16,2,128]{2,1,0:T(2,128)} copy-done((f32[16,2,128]{2,1,0:T(2,128)}, f32[16,2,128]{2,1,0:T(2,128)S(1)}, u32[]{:S(2)}) %copy-start.3) | copy-done | bytes 16408
  13.7 8.4 %shard_map.87 = (f32[16,128,128]{2,1,0:T(8,128)}, f32[16,128,128]{2,1,0:T(8,128)}, f32[16,16,2,128]{3,2,1,0:T(2,128)}) custom-call(f32[16]{0:T(128)} %spacing_ref.1, f32[16]{0:T(128)} %ratio_ref.1, f32[16,128,128]{2,1,0:T(8,128)} %t_up_ref.1, f32[16,128,128]{2,1,0:T(8,128)} %t_up_ref.1, f32[16,128,128]{2,1,0:T(8,128)} %t_up_ref.1, ...), custom_call_target="tpu_custom_call" | custom-call | flops 26214400 | bytes 8388608 | tf_op jit(solution)/shard_map/pallas_call | solution.py:228
  22.0 10.8 %all-to-all-start = ((f32[16,16,2,128]{3,2,1,0:T(2,128)}), f32[16,16,2,128]{3,2,1,0:T(2,128)S(1)}, u32[]{:S(2)}, u32[]{:S(2)}) async-start(f32[16,16,2,128]{3,2,1,0:T(2,128)} %get-tuple-element.14), calls=%async_computation | async-start | bytes 524288 | tf_op jit(solution)/shard_map/all_to_all | solution.py:37
  32.9 0.1 multiply_exponential_fusion.1
  32.9 2.5 %fusion = f32[16,128,128]{2,1,0:T(8,128)S(1)} fusion(f32[16,128,128]{2,1,0:T(8,128)} %get-tuple-element.13, f32[128,128]{1,0:T(8,128)S(1)} %subtract_abs_fusion, f32[16]{0:T(128)S(1)} %get-tuple-element.17), kind=kOutput, calls=%fused_computation.1 | convolution fusion | flops 402915328 | bytes 2162752 | tf_op jit(solution)/shard_map/kij,kjc->kic/dot_general | solution.py:42
  35.4 6.5 %all-to-all-done = f32[16,16,2,128]{3,2,1,0:T(2,128)S(1)} async-done(((f32[16,16,2,128]{3,2,1,0:T(2,128)}), f32[16,16,2,128]{3,2,1,0:T(2,128)S(1)}, u32[]{:S(2)}, u32[]{:S(2)}) %all-to-all-start) | async-done | bytes 262176 | tf_op jit(solution)/shard_map/all_to_all | solution.py:37
  41.9 0.2 fusion.11
  42.1 0.1 multiply_reduce_fusion
  42.2 0.1 multiply_reduce_fusion.1
  42.3 1.5 %add_divide_fusion = f32[16,128,128]{2,1,0:T(8,128)} fusion(f32[16,128,128]{2,1,0:T(8,128)S(1)} %fusion, f32[16]{0:T(128)S(1)} %get-tuple-element.24, f32[16,128]{1,0:T(8,128)S(1)} %multiply_reduce_fusion, f32[16,128]{1,0:T(8,128)S(1)} %get-tuple-element.23, f32[16,128]{1,0:T(8,128)S(1)} %multiply_reduce_fusion.1, f32[16,128]{1,0:T(8,128)S(1)} %get-tuple-element.22), kind=kLoop, calls=%fused_computation | loop fusion | flops 1310720 | bytes 2129984 | tf_op jit(solution)/shard_map/div | solution.py:60
  (4 shorter events, 0.1 us)
Async XLA Ops:
  0.6 10.2 %copy-start.4 = (f32[16]{0:T(128)S(1)}, f32[16]{0:T(128)}, u32[]{:S(2)}) copy-start(f32[16]{0:T(128)} %ratio_ref.1) | copy-start | bytes 196
  3.5 7.6 %collective-permute-start = (f32[16,2,128]{2,1,0:T(2,128)}, f32[16,2,128]{2,1,0:T(2,128)S(1)}, u32[]{:S(2)}, u32[]{:S(2)}) collective-permute-start(f32[16,2,128]{2,1,0:T(2,128)} %get-tuple-element.9), channel_id=1, source_target_pairs={{0,16},{16,32},{32,48},{48,64},{64,80},{80,96},{96,112},{112,128},... | collective-permute-start | bytes 49160 | tf_op jit(solution)/shard_map/ppermute | solution.py:21
  5.4 5.7 %collective-permute-start.1 = (f32[16,2,128]{2,1,0:T(2,128)}, f32[16,2,128]{2,1,0:T(2,128)S(1)}, u32[]{:S(2)}, u32[]{:S(2)}) collective-permute-start(f32[16,2,128]{2,1,0:T(2,128)} %get-tuple-element.10), channel_id=1, source_target_pairs={{0,240},{16,0},{32,16},{48,32},{64,48},{80,64},{96,80},{112,96},{1... | collective-permute-start | bytes 49160 | tf_op jit(solution)/shard_map/ppermute | solution.py:22
  5.5 7.0 %collective-permute-start.2 = (f32[16,2,128]{2,1,0:T(2,128)}, f32[16,2,128]{2,1,0:T(2,128)S(1)}, u32[]{:S(2)}, u32[]{:S(2)}) collective-permute-start(f32[16,2,128]{2,1,0:T(2,128)} %get-tuple-element.11), channel_id=1, source_target_pairs={{0,1},{1,2},{2,3},{3,4},{4,5},{5,6},{6,7},{7,8},{8,9},{9,10},{10,1... | collective-permute-start | bytes 49160 | tf_op jit(solution)/shard_map/ppermute | solution.py:21
  5.5 7.0 %collective-permute-start.3 = (f32[16,2,128]{2,1,0:T(2,128)}, f32[16,2,128]{2,1,0:T(2,128)S(1)}, u32[]{:S(2)}, u32[]{:S(2)}) collective-permute-start(f32[16,2,128]{2,1,0:T(2,128)} %get-tuple-element.12), channel_id=1, source_target_pairs={{0,15},{1,0},{2,1},{3,2},{4,3},{5,4},{6,5},{7,6},{8,7},{9,8},{10,9... | collective-permute-start | bytes 49160 | tf_op jit(solution)/shard_map/ppermute | solution.py:22
  11.0 1.5 %copy-start = (f32[16,2,128]{2,1,0:T(2,128)}, f32[16,2,128]{2,1,0:T(2,128)S(1)}, u32[]{:S(2)}) copy-start(f32[16,2,128]{2,1,0:T(2,128)S(1)} %collective-permute-done.x_prev_ref) | copy-start | bytes 49156
  11.1 1.4 %copy-start.1 = (f32[16,2,128]{2,1,0:T(2,128)}, f32[16,2,128]{2,1,0:T(2,128)S(1)}, u32[]{:S(2)}) copy-start(f32[16,2,128]{2,1,0:T(2,128)S(1)} %collective-permute-done.1.x_next_ref) | copy-start | bytes 49156
  12.5 0.6 %copy-start.2 = (f32[16,2,128]{2,1,0:T(2,128)}, f32[16,2,128]{2,1,0:T(2,128)S(1)}, u32[]{:S(2)}) copy-start(f32[16,2,128]{2,1,0:T(2,128)S(1)} %collective-permute-done.2.y_prev_ref) | copy-start | bytes 49156
  13.1 0.6 %copy-start.3 = (f32[16,2,128]{2,1,0:T(2,128)}, f32[16,2,128]{2,1,0:T(2,128)S(1)}, u32[]{:S(2)}) copy-start(f32[16,2,128]{2,1,0:T(2,128)S(1)} %collective-permute-done.3.y_next_ref) | copy-start | bytes 49156
  22.0 19.9 %all-to-all-start = ((f32[16,16,2,128]{3,2,1,0:T(2,128)}), f32[16,16,2,128]{3,2,1,0:T(2,128)S(1)}, u32[]{:S(2)}, u32[]{:S(2)}) async-start(f32[16,16,2,128]{3,2,1,0:T(2,128)} %get-tuple-element.14), calls=%async_computation | async-start | bytes 524288 | tf_op jit(solution)/shard_map/all_to_all | solution.py:37

commit v12 on v11

--- a/solution.py
+++ b/solution.py
@@ -214,7 +214,7 @@
     y_prev, y_next = exchange_edges(y_first, y_last, "gy")
 
     log_lam, root = spread_root(backward_spread_ratio)
-    per_step = 8 if levels % 8 == 0 else 1
+    per_step = 2 if levels % 2 == 0 else 1
     level = lambda shape: pl.BlockSpec(shape, lambda g: (g,) + (0,) * (len(shape) - 1))
     parts = lax.axis_size("gx")
     vmem = pl.BlockSpec(memory_space=pltpu.VMEM)

time: 44.6 us -> 46 us (1.031)
  Pallas kernels: 11.2 us -> 12.4 us
    pallas_call x1, Pallas kernels: 8.36 us -> 9.58 us  [on_device(): pl.pallas_call(stencil_kernel, grid=(levels // per_step,), in_specs=[smem...]
where the time goes in v12:
time: 46 us; the launch traced here: 45.1 us
  starting transfers between devices  18.2 us (40%)
  Pallas kernels  12.4 us (27%)
  waiting for transfers between devices  7.9 us (17%)
  matrix products  2.5 us (5%)
  other arithmetic  1.94 us (4%)
  local copies, waits for them, and re-layouts  1.39 us (3%)
  between operations  0.74 us (2%)
    all_to_all x1, starting transfers between devices, periodic_solve(): gathered = lax.all_to_all(ends, 'gx', 0, 0, tiled=True)  10.8 us
    pallas_call x1, Pallas kernels, on_device(): pl.pallas_call(stencil_kernel, grid=(levels // per_step,), in_specs=[smem...  9.58 us
    all_to_all x1, waiting for transfers between devices, periodic_solve(): gathered = lax.all_to_all(ends, 'gx', 0, 0, tiled=True)  6.47 us
    ppermute x2, starting transfers between devices, exchange_edges(): from_next = lax.ppermute(first, axis, ring_pairs(count, -1))  5.47 us
    pallas_call x1, Pallas kernels, on_device(): pl.pallas_call(edge_kernel, grid=(1,), in_specs=[whole((levels, rows, col...  2.81 us
    dot_general x1, matrix products, periodic_solve(): jnp.einsum('kij,kjc->kic', kernel, source, precision=lax.Precision.HIGHEST)  2.5 us
    ppermute x2, starting transfers between devices, exchange_edges(): from_prev = lax.ppermute(last, axis, ring_pairs(count, 1))  1.92 us
    div x1, other arithmetic, periodic_solve(): return total / root[:, None, None]  1.52 us
  transfers between devices with their start and end apart: 5, of which 2 were waited for; matrix products, arithmetic and copies ran while one was open for 6% of the time, Pallas kernels for 0%

profile of v12, /device:TPU:32, one launch (start us, length us, event | category | flops | bytes accessed | tf_op | source)
XLA Modules:
  0.0 45.1 jit_solution(4769774747184249462)
XLA Ops:
  0.6 0.0 copy-start.4
  0.6 2.8 %shard_map.86 = (f32[16,2,128]{2,1,0:T(2,128)}, f32[16,2,128]{2,1,0:T(2,128)}, f32[16,2,128]{2,1,0:T(2,128)}, f32[16,2,128]{2,1,0:T(2,128)}) custom-call(f32[16,128,128]{2,1,0:T(8,128)} %t_up_ref.1, f32[2,16,128,128]{3,2,1,0:T(8,128)} %v_ref.3, f32[2,16,128,128]{3,2,1,0:T(8,128)} %v_ref.3, f32[2,16,128,128]{3,2,1,0:T(8,128)} %v_ref.3), custom_call_target="tpu_custom_call" | custom-call | tf_op jit(solution)/shard_map/pallas_call | solution.py:196
  3.5 1.9 %collective-permute-start = (f32[16,2,128]{2,1,0:T(2,128)}, f32[16,2,128]{2,1,0:T(2,128)S(1)}, u32[]{:S(2)}, u32[]{:S(2)}) collective-permute-start(f32[16,2,128]{2,1,0:T(2,128)} %get-tuple-element.9), channel_id=1, source_target_pairs={{0,16},{16,32},{32,48},{48,64},{64,80},{80,96},{96,112},{112,128},... | collective-permute-start | bytes 49160 | tf_op jit(solution)/shard_map/ppermute | solution.py:21
  5.4 0.1 collective-permute-start.1
  5.5 0.0 collective-permute-start.2
  5.5 5.4 %collective-permute-start.3 = (f32[16,2,128]{2,1,0:T(2,128)}, f32[16,2,128]{2,1,0:T(2,128)S(1)}, u32[]{:S(2)}, u32[]{:S(2)}) collective-permute-start(f32[16,2,128]{2,1,0:T(2,128)} %get-tuple-element.12), channel_id=1, source_target_pairs={{0,15},{1,0},{2,1},{3,2},{4,3},{5,4},{6,5},{7,6},{8,7},{9,8},{10,9... | collective-permute-start | bytes 49160 | tf_op jit(solution)/shard_map/ppermute | solution.py:22
  10.9 0.0 copy-done.4
  10.9 0.1 exponential_divide_fusion.1
  11.0 0.0 collective-permute-done.x_prev_ref
  11.0 0.0 copy-start
  11.1 0.0 collective-permute-done.1.x_next_ref
  11.1 0.0 copy-start.1
  11.1 1.4 %collective-permute-done.2.y_prev_ref = f32[16,2,128]{2,1,0:T(2,128)S(1)} collective-permute-done((f32[16,2,128]{2,1,0:T(2,128)}, f32[16,2,128]{2,1,0:T(2,128)S(1)}, u32[]{:S(2)}, u32[]{:S(2)}) %collective-permute-start.2) | collective-permute-done | bytes 16416 | tf_op jit(solution)/shard_map/ppermute | solution.py:21
  12.5 0.0 copy-start.2
  12.5 0.0 collective-permute-done.3.y_next_ref
  12.5 0.0 copy-done
  12.5 0.0 copy-done.1
  12.5 0.6 %copy-done.2 = f32[16,2,128]{2,1,0:T(2,128)} copy-done((f32[16,2,128]{2,1,0:T(2,128)}, f32[16,2,128]{2,1,0:T(2,128)S(1)}, u32[]{:S(2)}) %copy-start.2) | copy-done | bytes 16408
  13.1 0.0 copy-start.3
  13.1 0.6 %copy-done.3 = f32[16,2,128]{2,1,0:T(2,128)} copy-done((f32[16,2,128]{2,1,0:T(2,128)}, f32[16,2,128]{2,1,0:T(2,128)S(1)}, u32[]{:S(2)}) %copy-start.3) | copy-done | bytes 16408
  13.7 9.6 %shard_map.87 = (f32[16,128,128]{2,1,0:T(8,128)}, f32[16,128,128]{2,1,0:T(8,128)}, f32[16,16,2,128]{3,2,1,0:T(2,128)}) custom-call(f32[16]{0:T(128)} %spacing_ref.1, f32[16]{0:T(128)} %ratio_ref.1, f32[16,128,128]{2,1,0:T(8,128)} %t_up_ref.1, f32[16,128,128]{2,1,0:T(8,128)} %t_up_ref.1, f32[16,128,128]{2,1,0:T(8,128)} %t_up_ref.1, ...), custom_call_target="tpu_custom_call" | custom-call | flops 26214400 | bytes 8388608 | tf_op jit(solution)/shard_map/pallas_call | solution.py:228
  23.3 10.8 %all-to-all-start = ((f32[16,16,2,128]{3,2,1,0:T(2,128)}), f32[16,16,2,128]{3,2,1,0:T(2,128)S(1)}, u32[]{:S(2)}, u32[]{:S(2)}) async-start(f32[16,16,2,128]{3,2,1,0:T(2,128)} %get-tuple-element.14), calls=%async_computation | async-start | bytes 524288 | tf_op jit(solution)/shard_map/all_to_all | solution.py:37
  34.1 0.1 multiply_exponential_fusion.1
  34.2 2.5 %fusion = f32[16,128,128]{2,1,0:T(8,128)S(1)} fusion(f32[16,128,128]{2,1,0:T(8,128)} %get-tuple-element.13, f32[128,128]{1,0:T(8,128)S(1)} %subtract_abs_fusion, f32[16]{0:T(128)S(1)} %get-tuple-element.17), kind=kOutput, calls=%fused_computation.1 | convolution fusion | flops 402915328 | bytes 2162752 | tf_op jit(solution)/shard_map/kij,kjc->kic/dot_general | solution.py:42
  36.7 6.5 %all-to-all-done = f32[16,16,2,128]{3,2,1,0:T(2,128)S(1)} async-done(((f32[16,16,2,128]{3,2,1,0:T(2,128)}), f32[16,16,2,128]{3,2,1,0:T(2,128)S(1)}, u32[]{:S(2)}, u32[]{:S(2)}) %all-to-all-start) | async-done | bytes 262176 | tf_op jit(solution)/shard_map/all_to_all | solution.py:37
  43.1 0.2 fusion.11
  43.3 0.1 multiply_reduce_fusion
  43.4 0.1 multiply_reduce_fusion.1
  43.5 1.5 %add_divide_fusion = f32[16,128,128]{2,1,0:T(8,128)} fusion(f32[16,128,128]{2,1,0:T(8,128)S(1)} %fusion, f32[16]{0:T(128)S(1)} %get-tuple-element.24, f32[16,128]{1,0:T(8,128)S(1)} %multiply_reduce_fusion, f32[16,128]{1,0:T(8,128)S(1)} %get-tuple-element.23, f32[16,128]{1,0:T(8,128)S(1)} %multiply_reduce_fusion.1, f32[16,128]{1,0:T(8,128)S(1)} %get-tuple-element.22), kind=kLoop, calls=%fused_computation | loop fusion | flops 1310720 | bytes 2129984 | tf_op jit(solution)/shard_map/div | solution.py:60
  (4 shorter events, 0.1 us)
Async XLA Ops:
  0.6 10.2 %copy-start.4 = (f32[16]{0:T(128)S(1)}, f32[16]{0:T(128)}, u32[]{:S(2)}) copy-start(f32[16]{0:T(128)} %ratio_ref.1) | copy-start | bytes 196
  3.5 7.6 %collective-permute-start = (f32[16,2,128]{2,1,0:T(2,128)}, f32[16,2,128]{2,1,0:T(2,128)S(1)}, u32[]{:S(2)}, u32[]{:S(2)}) collective-permute-start(f32[16,2,128]{2,1,0:T(2,128)} %get-tuple-element.9), channel_id=1, source_target_pairs={{0,16},{16,32},{32,48},{48,64},{64,80},{80,96},{96,112},{112,128},... | collective-permute-start | bytes 49160 | tf_op jit(solution)/shard_map/ppermute | solution.py:21
  5.4 5.7 %collective-permute-start.1 = (f32[16,2,128]{2,1,0:T(2,128)}, f32[16,2,128]{2,1,0:T(2,128)S(1)}, u32[]{:S(2)}, u32[]{:S(2)}) collective-permute-start(f32[16,2,128]{2,1,0:T(2,128)} %get-tuple-element.10), channel_id=1, source_target_pairs={{0,240},{16,0},{32,16},{48,32},{64,48},{80,64},{96,80},{112,96},{1... | collective-permute-start | bytes 49160 | tf_op jit(solution)/shard_map/ppermute | solution.py:22
  5.5 7.0 %collective-permute-start.2 = (f32[16,2,128]{2,1,0:T(2,128)}, f32[16,2,128]{2,1,0:T(2,128)S(1)}, u32[]{:S(2)}, u32[]{:S(2)}) collective-permute-start(f32[16,2,128]{2,1,0:T(2,128)} %get-tuple-element.11), channel_id=1, source_target_pairs={{0,1},{1,2},{2,3},{3,4},{4,5},{5,6},{6,7},{7,8},{8,9},{9,10},{10,1... | collective-permute-start | bytes 49160 | tf_op jit(solution)/shard_map/ppermute | solution.py:21
  5.5 7.0 %collective-permute-start.3 = (f32[16,2,128]{2,1,0:T(2,128)}, f32[16,2,128]{2,1,0:T(2,128)S(1)}, u32[]{:S(2)}, u32[]{:S(2)}) collective-permute-start(f32[16,2,128]{2,1,0:T(2,128)} %get-tuple-element.12), channel_id=1, source_target_pairs={{0,15},{1,0},{2,1},{3,2},{4,3},{5,4},{6,5},{7,6},{8,7},{9,8},{10,9... | collective-permute-start | bytes 49160 | tf_op jit(solution)/shard_map/ppermute | solution.py:22
  11.0 1.5 %copy-start = (f32[16,2,128]{2,1,0:T(2,128)}, f32[16,2,128]{2,1,0:T(2,128)S(1)}, u32[]{:S(2)}) copy-start(f32[16,2,128]{2,1,0:T(2,128)S(1)} %collective-permute-done.x_prev_ref) | copy-start | bytes 49156
  11.1 1.4 %copy-start.1 = (f32[16,2,128]{2,1,0:T(2,128)}, f32[16,2,128]{2,1,0:T(2,128)S(1)}, u32[]{:S(2)}) copy-start(f32[16,2,128]{2,1,0:T(2,128)S(1)} %collective-permute-done.1.x_next_ref) | copy-start | bytes 49156
  12.5 0.6 %copy-start.2 = (f32[16,2,128]{2,1,0:T(2,128)}, f32[16,2,128]{2,1,0:T(2,128)S(1)}, u32[]{:S(2)}) copy-start(f32[16,2,128]{2,1,0:T(2,128)S(1)} %collective-permute-done.2.y_prev_ref) | copy-start | bytes 49156
  13.1 0.6 %copy-start.3 = (f32[16,2,128]{2,1,0:T(2,128)}, f32[16,2,128]{2,1,0:T(2,128)S(1)}, u32[]{:S(2)}) copy-start(f32[16,2,128]{2,1,0:T(2,128)S(1)} %collective-permute-done.3.y_next_ref) | copy-start | bytes 49156
  23.3 19.9 %all-to-all-start = ((f32[16,16,2,128]{3,2,1,0:T(2,128)}), f32[16,16,2,128]{3,2,1,0:T(2,128)S(1)}, u32[]{:S(2)}, u32[]{:S(2)}) async-start(f32[16,16,2,128]{3,2,1,0:T(2,128)} %get-tuple-element.14), calls=%async_computation | async-start | bytes 524288 | tf_op jit(solution)/shard_map/all_to_all | solution.py:37
